TPU v7x, 32 devices: a whole 2x2x4 slice. The times are simulated.
32 devices in a mesh: groups: 2 (over x), tiles: 16 (over z, y, core).
Axes of the slice: x: 2, y: 2, z: 4, core: 2. Of those that a mesh axis runs over, the one named last changes fastest.
Arguments:
- coeffs: float32 [8192, 16384], P(('groups', 'tiles')), parts along dimension 0, may hold values from -0.09375 to 0.09375
- occupation: float32 [8192], P(('groups', 'tiles')), parts along dimension 0, may hold values from -1 to 1
- kept_tiles: int32 [64, 2], P('groups'), parts along dimension 0, may hold values from 0 to 255, as said below
- tile_slot: int32 [64], P('groups'), parts along dimension 0, may hold values from 0 to 31, as said below
- blocks: int32 [256, 8], P('groups'), parts along dimension 0, may hold values from 0 to 255, as said below
- batch_slot: int32 [256], P('groups'), parts along dimension 0, may hold values from 0 to 127, as said below
- tables: float32 [256, 512, 256], P(('groups', 'tiles')), parts along dimension 0, may hold values from -3.6 to 3.6
- weights: float32 [256, 256], P(('groups', 'tiles')), parts along dimension 0, may hold values from 0.005 to 0.05
- local_pot: float32 [256, 256], P(('groups', 'tiles')), parts along dimension 0, may hold values from -6 to 6
Outputs:
- density: float32 [256, 256], P(('groups', 'tiles')), parts along dimension 0
- matrix: float32 [64, 4096], P(('groups', 'tiles')), parts along dimension 0
There are 2 independent parts, one for each index of `groups`. A program takes and returns all parts, laid end to end along the dimension named above; each array names one. Nothing has to cross between parts.
Inputs may be any that keep to these rules, and one draw needn't show every extreme that they name: `kept_tiles`: distinct pairs (row block, column block). A permutation; slot tile_slot[k] is held by the device of index tile_slot[k] // 2 along tiles. Of the kept tiles that lie within the blocks of the batches held by one device, at most 2 are held by any one device. Each row names 8 different blocks. The devices come in aligned block clusters of 4 (indices 0 to 3, and so on); all batches held by the devices of one cluster name the same blocks, each batch in an order of its own, and different clusters name disjoint blocks. At most 16 kept tiles lie within the blocks of one batch. A permutation; the tables, weights, potential and density of batch b sit at slot batch_slot[b], held by the device of index batch_slot[b] // 8.
All inputs are finite; a program needn't handle non-finite values.
Results may differ from a plain program's by a relative error of at most 0.0003.
Values sent between devices are 32-bit elements; how exact they have to be, the bound alone decides.
No kernel may reach another device: no remote copies, remote signals or barrier semaphores. Data moves between devices by JAX's collectives and lax.ppermute only.
A program may use at most 128 MiB of HBM per device.

v0:
```python
import jax
import jax.numpy as jnp
from jax import lax
from jax.sharding import PartitionSpec as P

BS = 64
OV = 8


def tile_places(kept_tiles, block_lists):
    ladder = jnp.arange(block_lists.shape[-1], dtype=jnp.int32)
    row_match = kept_tiles[None, :, 0:1] == block_lists[:, None, :]
    col_match = kept_tiles[None, :, 1:2] == block_lists[:, None, :]
    present = jnp.any(row_match, axis=2) & jnp.any(col_match, axis=2)
    row_place = jnp.sum(jnp.where(row_match, ladder, 0), axis=2)
    col_place = jnp.sum(jnp.where(col_match, ladder, 0), axis=2)
    return (present, row_place, col_place)


def batch_step(compact, capacity):

    def per_batch(summed, inputs):
        table_rows, weight_row, base_row, present_row, row_index, col_index = inputs
        kept_values = jnp.where(present_row[:, None], compact, 0.0).reshape(capacity, BS, BS)
        dense_tiles = (
            jnp.zeros((OV, BS, OV, BS), jnp.float32).at[row_index, :, col_index, :].add(kept_values)
        )
        basis_grid = table_rows.reshape(OV, BS, table_rows.shape[-1])
        mixed_rows = jnp.einsum(
            "ixjy,jyp->ixp", dense_tiles, basis_grid, precision=lax.Precision.HIGHEST
        )
        density = jnp.sum(basis_grid * mixed_rows, axis=(0, 1))
        potential = base_row + density - density * density * density / 6.0
        weighted = basis_grid * (weight_row * potential)[None, None, :]
        full_matrix = jnp.einsum(
            "ixp,jyp->ixjy", weighted, basis_grid, precision=lax.Precision.HIGHEST
        )
        picked = full_matrix[row_index, :, col_index, :].reshape(capacity, BS * BS)
        return (summed + jnp.where(present_row[:, None], picked, 0.0), density)

    return per_batch


def body(coeffs, occupation, kept_tiles, tile_slot, blocks, batch_slot, tables, weights, local_pot):
    devices = lax.axis_size("tiles")
    my_index = lax.axis_index("tiles")
    kept_count = kept_tiles.shape[0]
    owned_count = kept_count // devices
    batch_count = tables.shape[0]
    batch_total = batch_slot.shape[0]
    state_count = coeffs.shape[0]
    block_total = coeffs.shape[1] // BS
    blocked = coeffs.reshape(state_count, block_total, BS)
    ladder_kept = jnp.arange(kept_count, dtype=jnp.int32)
    slot_kept = jnp.zeros((kept_count,), jnp.int32).at[tile_slot].set(ladder_kept)
    ladder_batch = jnp.arange(batch_total, dtype=jnp.int32)
    slot_batch = jnp.zeros((batch_total,), jnp.int32).at[batch_slot].set(ladder_batch)
    my_batches = lax.dynamic_slice_in_dim(slot_batch, my_index * batch_count, batch_count)
    my_blocks = blocks[my_batches]
    present, row_place, col_place = tile_places(kept_tiles, my_blocks)
    needed = jnp.any(present, axis=0)
    needed_rank = jnp.cumsum(needed.astype(jnp.int32)) - 1
    capacity = min(OV * OV, devices)
    ladder_cap = jnp.arange(capacity, dtype=jnp.int32)
    choose = needed[None, :] & (needed_rank[None, :] == ladder_cap[:, None])
    compact_kept = jnp.sum(jnp.where(choose, ladder_kept[None, :], 0), axis=1)
    compact_valid = jnp.any(choose, axis=1)
    compact_slot = tile_slot[compact_kept]
    compact_present = present[:, compact_kept] & compact_valid[None, :]
    compact_row = row_place[:, compact_kept]
    compact_col = col_place[:, compact_kept]
    scaled = blocked * occupation[:, None, None]
    tile_pairs = kept_tiles[slot_kept]
    left_rows = jnp.take(blocked, tile_pairs[:, 0], axis=1)
    right_rows = jnp.take(scaled, tile_pairs[:, 1], axis=1)
    owned_tiles = lax.psum_scatter(
        jnp.einsum("srx,sry->rxy", left_rows, right_rows, precision=lax.Precision.HIGHEST).reshape(
            lax.axis_size("tiles") * owned_count, BS * BS
        ),
        "tiles",
        scatter_dimension=0,
        tiled=True,
    )
    shard_rows = lax.all_gather(owned_tiles, "tiles", axis=0, tiled=True)
    inside = (compact_slot >= 0) & (compact_slot < shard_rows.shape[0]) & compact_valid
    fetched = shard_rows[jnp.clip(compact_slot, 0, shard_rows.shape[0] - 1)]
    compact = jnp.where(inside[:, None], fetched, 0.0)
    summed, density = lax.scan(
        batch_step(compact, capacity),
        jnp.zeros((capacity, BS * BS), jnp.float32),
        (tables, weights, local_pot, compact_present, compact_row, compact_col),
    )
    targets = jnp.arange(lax.axis_size("tiles") * owned_count, dtype=jnp.int32)
    hit_table = ((compact_slot[None, :] == targets[:, None]) & compact_valid[None, :]).astype(
        jnp.float32
    )
    matrix = lax.psum_scatter(
        jnp.dot(hit_table, summed, precision=lax.Precision.HIGHEST),
        "tiles",
        scatter_dimension=0,
        tiled=True,
    )
    return (density, matrix)


def solution(mesh):
    in_specs = (
        P(("groups", "tiles"), None),
        P(("groups", "tiles")),
        P("groups", None),
        P("groups"),
        P("groups", None),
        P("groups"),
        P(("groups", "tiles"), None, None),
        P(("groups", "tiles"), None),
        P(("groups", "tiles"), None),
    )
    out_specs = (P(("groups", "tiles"), None), P(("groups", "tiles"), None))
    return jax.shard_map(body, mesh=mesh, in_specs=in_specs, out_specs=out_specs, check_vma=False)
```

profile of v0, /device:TPU:0, one launch (start us, length us, event | category | flops | bytes accessed | tf_op | source)
XLA Modules:
  0.0 360.8 jit_solution(2303243374622515084)
XLA Ops:
  10.1 17.5 %copy.48 = f32[256,16384]{0,1:T(8,128)} copy(f32[256,16384]{1,0:T(8,128)} %param.13) | data formatting | bytes 33554432 | tf_op args[0]
  27.6 12.3 %broadcast_multiply_fusion.1 = f32[256,256,64]{0,2,1:T(8,128)} fusion(f32[256,256,64]{0,2,1:T(8,128)} %bitcast.106, f32[256]{0:T(256)S(1)} %copy-done.3), kind=kLoop, calls=%fused_computation.39 | loop fusion | flops 4194304 | bytes 33555456 | tf_op jit(solution)/shard_map/mul | solution.py:72
  39.9 6.4 %gather_fusion.8 = f32[32,256,64]{1,2,0:T(8,128)S(1)} fusion(f32[256,256,64]{0,2,1:T(8,128)} %bitcast.107, s32[1024]{0:T(1024)S(1)} %pad_clamp_fusion.2), kind=kCustom, calls=%fused_computation.clone | custom fusion | bytes 4194432 | tf_op jit(solution)/shard_map/jit(_take)/gather | solution.py:74
  46.4 7.8 %gather_fusion.9 = f32[32,256,64]{1,2,0:T(8,128)} fusion(f32[256,256,64]{0,2,1:T(8,128)} %broadcast_multiply_fusion.1, s32[1024]{0:T(1024)S(1)} %pad_clamp_fusion.1), kind=kCustom, calls=%fused_computation.2.clone | custom fusion | bytes 4194432 | tf_op jit(solution)/shard_map/jit(_take)/gather | solution.py:75
  54.2 3.8 %fusion.10 = f32[32,64,64]{2,1,0:T(8,128)S(1)} fusion(f32[32,256,64]{1,2,0:T(8,128)} %gather_fusion.9, f32[32,256,64]{1,2,0:T(8,128)S(1)} %gather_fusion.8, pred[32]{0:T(512)(128)(4,1)S(1)} %get-tuple-element.177, pred[32]{0:T(512)(128)(4,1)S(1)} %get-tuple-element.178), kind=kOutput, calls=%fused_computation.40 | convolution fusion | flops 403701760 | bytes 4718656 | tf_op jit(solution)/shard_map/srx,sry->rxy/dot_general | solution.py:77
  66.3 86.0 %all-reduce.5.cloned.1.call-done = f32[32,4096]{1,0:T(8,128)} async-done(((f32[32,4096]{1,0:T(8,128)}), f32[32,4096]{1,0:T(8,128)}) %all-reduce.5.cloned.1.call-update) | async-done | bytes 524304
  153.1 22.5 %all-gather = f32[16,2,4096]{2,1,0:T(2,128)S(1)} all-gather(f32[1,2,4096]{2,1,0:T(2,128)S(1)} %dynamic-slice_bitcast_fusion.1), channel_id=1, replica_groups=mesh['groups'=2,'tiles'=16] {'tiles'}, dimensions={0}, use_global_device_ids=true | all-gather | bytes 557056 | tf_op jit(solution)/shard_map/all_gather | solution.py:84
  176.7 87.0 %while.13 = (s32[]{:T(128)}, f32[16,4096]{1,0:T(8,128)S(1)}, f32[8,256]{1,0:T(8,128)}, pred[8,16]{1,0:T(8,128)(4,1)S(1)}, f32[8,512,256]{2,1,0:T(8,128)}, /*inde...) while((s32[]{:T(128)}, f32[16,4096]{1,0:T(8,128)S(1)}, ...), condition=%wide.region_14.16_spmd.clone, body=%wide.region_11.15_spmd.clone.sunk | while | flops 1611335168 | bytes 11023075 | solution.py:88
  179.9 1.8 fusion.54
  183.6 1.8 fusion.56
  190.8 1.8 fusion.54
  194.4 1.8 fusion.56
  201.7 1.8 fusion.54
  205.3 1.8 fusion.56
  212.5 1.8 fusion.54
  216.2 1.8 fusion.56
  223.4 1.8 fusion.54
  227.1 1.8 fusion.56
  234.3 1.8 fusion.54
  237.9 1.8 fusion.56
  245.1 1.8 fusion.54
  256.0 1.8 fusion.54
  259.7 1.8 fusion.56
  264.9 87.5 %all-reduce.7.cloned.1.call-done = f32[32,4096]{1,0:T(8,128)} async-done(((f32[32,4096]{1,0:T(8,128)}), f32[32,4096]{1,0:T(8,128)}) %all-reduce.7.cloned.1.call-update) | async-done | bytes 524304
  (184 shorter events, 74.0 us)
Async XLA Ops:
  7.2 145.1 %all-reduce.5.cloned.1.call-start = ((), (), s32[]{:S(2)}) async-start(), calls=%async_computation | async-start | bytes 1048576
  10.1 17.5 %copy-start.3 = (f32[256]{0:T(256)S(1)}, f32[256]{0:T(256)}, u32[]{:S(2)}) copy-start(f32[256]{0:T(256)} %param.14) | copy-start | bytes 3076
  58.0 1.3 copy-start.2
  58.0 1.3 copy-start.4
  58.1 2.4 copy-start.1
  58.1 3.8 %copy-start = (s32[32]{0:T(128)S(1)}, s32[32]{0:T(128)}, u32[]{:S(2)}) copy-start(s32[32]{0:T(128)} %param.16) | copy-start | bytes 388
  58.1 6.8 %copy-start.5 = (u32[32]{0:T(128)S(1)}, u32[32]{0:T(128)}, u32[]{:S(2)}) copy-start(u32[32]{0:T(128)} %constant.115) | copy-start | bytes 388
  59.3 293.1 %all-reduce.7.cloned.1.call-start = ((), (), s32[]{:S(2)}) async-start(), calls=%async_computation.1 | async-start | bytes 1048576
Sparse Core Ops, SparseCore 0:
  59.4 92.7 all-reduce.4
  265.0 87.3 all-reduce.6
where the time goes:
time: 363 us; the launch traced here: 361 us
  waiting for transfers between devices  174 us (48%)
  local copies, waits for them, and re-layouts  78.8 us (22%)
  other arithmetic  36.1 us (10%)
  matrix products  34.3 us (9%)
  blocking collectives  22.5 us (6%)
  between operations  15 us (4%)
    unnamed x4, waiting for transfers between devices  174 us
    all_gather x1, blocking collectives, body(): shard_rows = lax.all_gather(owned_tiles, 'tiles', axis=0, tiled=True)  22.5 us
    unnamed x22, local copies, waits for them, and re-layouts  22.1 us
    dot_general x8, matrix products, per_batch(): jnp.einsum('ixjy,jyp->ixp', dense_tiles, basis_grid, precision=lax.Precis...  14.7 us
    dot_general x8, matrix products, per_batch(): jnp.einsum('ixp,jyp->ixjy', weighted, basis_grid, precision=lax.Precision...  14.5 us
    dynamic_slice x16, local copies, waits for them, and re-layouts, body(): lax.scan(batch_step(compact, capacity), jnp.zeros((capacity, BS * BS), jn...  14.5 us
    mul x1, other arithmetic, body(): scaled = blocked * occupation[:, None, None]  12.3 us
    scatter-add x8, other arithmetic, per_batch(): jnp.zeros((OV, BS, OV, BS), jnp.float32).at[row_index, :, col_index, :]  11.8 us
  transfers between devices with their start and end apart: 2, of which 2 were waited for; matrix products, arithmetic and copies ran while one was open for 2% of the time, Pallas kernels for 0%

commit v1 on v0

v1 whole, which is shorter than its diff:
```python
import jax
import jax.numpy as jnp
from jax import lax
from jax.sharding import PartitionSpec as P

BS = 64
OV = 8


def body(coeffs, occupation, kept_tiles, tile_slot, blocks, batch_slot, tables, weights, local_pot):
    devices = lax.axis_size("tiles")
    my_index = lax.axis_index("tiles")
    kept_count = kept_tiles.shape[0]
    batch_count = tables.shape[0]
    batch_total = batch_slot.shape[0]
    state_count = coeffs.shape[0]
    block_total = coeffs.shape[1] // BS
    points = tables.shape[-1]
    width = OV * BS

    blocked = coeffs.reshape(state_count, block_total, BS)
    left_rows = jnp.take(blocked, kept_tiles[:, 0], axis=1)
    right_rows = jnp.take(blocked, kept_tiles[:, 1], axis=1) * occupation[:, None, None]
    partial = jnp.einsum(
        "srx,sry->rxy", left_rows, right_rows, precision=lax.Precision.HIGHEST
    ).reshape(kept_count, BS * BS)
    tile_values = lax.psum(partial, "tiles")

    ladder_batch = jnp.arange(batch_total, dtype=jnp.int32)
    slot_batch = jnp.zeros((batch_total,), jnp.int32).at[batch_slot].set(ladder_batch)
    my_batches = lax.dynamic_slice_in_dim(slot_batch, my_index * batch_count, batch_count)
    my_blocks = blocks[my_batches]
    canon = jnp.sort(my_blocks[0])
    ladder_ov = jnp.arange(OV, dtype=jnp.int32)
    match = my_blocks[:, :, None] == canon[None, None, :]
    source = jnp.sum(jnp.where(match, ladder_ov[None, :, None], 0), axis=1)
    grid = tables.reshape(batch_count, OV, BS, points)
    canon_tables = jnp.take_along_axis(grid, source[:, :, None, None], axis=1).reshape(
        batch_count, width, points
    )

    row_hit = kept_tiles[:, 0:1] == canon[None, :]
    col_hit = kept_tiles[:, 1:2] == canon[None, :]
    present = jnp.any(row_hit, axis=1) & jnp.any(col_hit, axis=1)
    row_place = jnp.sum(jnp.where(row_hit, ladder_ov[None, :], 0), axis=1)
    col_place = jnp.sum(jnp.where(col_hit, ladder_ov[None, :], 0), axis=1)
    kept_values = jnp.where(present[:, None], tile_values, 0.0).reshape(kept_count, BS, BS)
    dense = (
        jnp.zeros((OV, BS, OV, BS), jnp.float32)
        .at[row_place, :, col_place, :]
        .add(kept_values)
        .reshape(width, width)
    )
    mixed = jnp.einsum("uv,bvp->bup", dense, canon_tables, precision=lax.Precision.HIGH)
    density = jnp.sum(canon_tables * mixed, axis=1)
    potential = local_pot + density - density * density * density / 6.0
    weighted = canon_tables * (weights * potential)[:, None, :]
    full_matrix = jnp.einsum(
        "bup,bvp->uv", weighted, canon_tables, precision=lax.Precision.HIGH
    ).reshape(OV, BS, OV, BS)
    picked = full_matrix[row_place, :, col_place, :].reshape(kept_count, BS * BS)
    contrib = jnp.where(present[:, None], picked, 0.0)

    ladder_kept = jnp.arange(kept_count, dtype=jnp.int32)
    slot_kept = jnp.zeros((kept_count,), jnp.int32).at[tile_slot].set(ladder_kept)
    by_slot = contrib[slot_kept]
    matrix = lax.psum_scatter(by_slot, "tiles", scatter_dimension=0, tiled=True)
    return (density, matrix)


def solution(mesh):
    in_specs = (
        P(("groups", "tiles"), None),
        P(("groups", "tiles")),
        P("groups", None),
        P("groups"),
        P("groups", None),
        P("groups"),
        P(("groups", "tiles"), None, None),
        P(("groups", "tiles"), None),
        P(("groups", "tiles"), None),
    )
    out_specs = (P(("groups", "tiles"), None), P(("groups", "tiles"), None))
    return jax.shard_map(body, mesh=mesh, in_specs=in_specs, out_specs=out_specs, check_vma=False)
```

time: 363 us -> 285 us (0.79)
  blocking collectives: 22.5 us -> 0 us
  other arithmetic: 36.1 us -> 14.2 us
  local copies, waits for them, and re-layouts: 78.8 us -> 66.8 us
  waiting for transfers between devices: 174 us -> 163 us
  matrix products: 34.3 us -> 25 us
    unnamed x4 -> x3, waiting for transfers between devices: 174 us -> 89.5 us
    psum x0 -> x1, waiting for transfers between devices: none -> 73.8 us  [body(): tile_values = lax.psum(partial, 'tiles')]
    all_gather x1 -> x0, blocking collectives: 22.5 us -> none  [body(): shard_rows = lax.all_gather(owned_tiles, 'tiles', axis=0, tiled=True)]
    mul x17 -> x1, other arithmetic: 21 us -> 0.01 us  [body(): weighted = canon_tables * (weights * potential)[:, None, :]]
    dynamic_slice x16 -> x0, local copies, waits for them, and re-layouts: 14.5 us -> none  [body(): lax.scan(batch_step(compact, capacity), jnp.zeros((capacity, BS * BS), jn...]
    dot_general x0 -> x2, local copies, waits for them, and re-layouts: none -> 10.9 us  [body(): jnp.einsum('bup,bvp->uv', weighted, canon_tables, precision=lax.Precision...]
    dynamic_update_slice x8 -> x0, local copies, waits for them, and re-layouts: 10.5 us -> none  [body(): lax.scan(batch_step(compact, capacity), jnp.zeros((capacity, BS * BS), jn...]
    dot_general x17 -> x2, matrix products: 30.4 us -> 21 us  [the longest x1 10.8 us: body(): jnp.einsum('bup,bvp->uv', weighted, canon_tables, precision=lax.Precision...]
  transfers between devices with their start and end apart: 2 -> 2, of which waited for: 2 -> 2; matrix products, arithmetic and copies ran while one was open for 2% -> 7% of each run, Pallas kernels for 0% -> 0%
where the time goes in v1:
time: 285 us; the launch traced here: 284 us
  waiting for transfers between devices  163 us (57%)
  local copies, waits for them, and re-layouts  66.8 us (23%)
  matrix products  25 us (9%)
  between operations  15 us (5%)
  other arithmetic  14.2 us (5%)
    unnamed x3, waiting for transfers between devices  89.5 us
    psum x1, waiting for transfers between devices, body(): tile_values = lax.psum(partial, 'tiles')  73.8 us
    unnamed x24, local copies, waits for them, and re-layouts  19.7 us
    dot_general x2, local copies, waits for them, and re-layouts, body(): jnp.einsum('bup,bvp->uv', weighted, canon_tables, precision=lax.Precision...  10.9 us
    dot_general x1, matrix products, body(): jnp.einsum('bup,bvp->uv', weighted, canon_tables, precision=lax.Precision...  10.8 us
    gather x3, local copies, waits for them, and re-layouts, body(): jnp.take_along_axis(grid, source[:, :, None, None], axis=1)  10.4 us
    dot_general x1, matrix products, body(): jnp.einsum('uv,bvp->bup', dense, canon_tables, precision=lax.Precision.HIGH)  10.2 us
    gather x1, local copies, waits for them, and re-layouts, body(): jnp.take(blocked, kept_tiles[:, 1], axis=1) * occupation[:, None, None]  7.8 us
  transfers between devices with their start and end apart: 2, of which 2 were waited for; matrix products, arithmetic and copies ran while one was open for 7% of the time, Pallas kernels for 0%

profile of v1, /device:TPU:0, one launch (start us, length us, event | category | flops | bytes accessed | tf_op | source)
XLA Modules:
  0.0 284.4 jit_solution(15538646823625262167)
XLA Ops:
  8.0 17.5 %copy.35 = f32[256,16384]{0,1:T(8,128)} copy(f32[256,16384]{1,0:T(8,128)} %param.11) | data formatting | bytes 33554432 | tf_op args[0]
  25.4 6.4 %gather_fusion.4 = f32[32,256,64]{1,2,0:T(8,128)S(1)} fusion(f32[256,256,64]{0,2,1:T(8,128)} %bitcast.76, s32[1024]{0:T(1024)S(1)} %get-tuple-element.23), kind=kCustom, calls=%fused_computation.clone | custom fusion | bytes 4194432 | tf_op jit(solution)/shard_map/jit(_take)/gather | solution.py:22
  31.9 7.8 %gather_fusion.5 = f32[32,256,64]{1,2,0:T(8,128)} fusion(f32[256,256,64]{0,2,1:T(8,128)} %bitcast.77, s32[1024]{0:T(1024)S(1)} %get-tuple-element.22), kind=kCustom, calls=%fused_computation.1.clone | custom fusion | bytes 4194432 | tf_op jit(solution)/shard_map/jit(_take)/gather | solution.py:23
  39.7 4.0 %fusion.5 = f32[32,64,64]{2,1,0:T(8,128)S(1)} fusion(f32[32,256,64]{1,2,0:T(8,128)} %gather_fusion.5, f32[32,256,64]{1,2,0:T(8,128)S(1)} %gather_fusion.4, f32[256]{0:T(256)S(1)} %copy-done.6, pred[32]{0:T(512)(128)(4,1)S(1)} %get-tuple-element.18, pred[32]{0:T(512)(128)(4,1)S(1)} %get-tuple-element.10), kind=kOutput, calls=%fused_computation.18 | convolution fusion | flops 404226048 | bytes 4719680 | tf_op jit(solution)/shard_map/srx,sry->rxy/dot_general | solution.py:24
  43.7 1.2 reshape.115
  45.1 1.0 scatter_custom_fusion
  46.8 1.0 sort.15
  48.2 0.9 scatter_custom_fusion.2
  49.0 5.0 %gather_fusion.3 = f32[64,64,256]{2,1,0:T(8,128)} fusion(f32[8,8,64,256]{3,2,1,0:T(8,128)} %bitcast.81, s32[64]{0:T(128)S(1)} %reshape.157), kind=kCustom, calls=%fused_computation.5 | custom fusion | bytes 8389120 | tf_op jit(solution)/shard_map/jit(take_along_axis)/gather | solution.py:38
  54.0 4.5 %broadcast_select_fusion = f32[8,8,64,256]{3,2,1,0:T(8,128)} fusion(f32[8,8,64,256]{3,2,1,0:T(8,128)} %bitcast.78, pred[8,8]{1,0:T(8,128)(4,1)S(1)} %compare_and_fusion), kind=kLoop, calls=%fused_computation.22 | loop fusion | flops 1048576 | bytes 8388672 | tf_op jit(solution)/shard_map/jit(take_along_axis)/select_n | solution.py:38
  58.5 5.4 %copy.34 = f32[8,512,256]{1,2,0:T(8,128)} copy(f32[8,512,256]{2,1,0:T(8,128)} %bitcast.79) | data formatting | bytes 8388608 | tf_op jit(solution)/shard_map/jit(take_along_axis)/gather | solution.py:38
  64.1 73.8 %all-reduce.4.cloned.1.call-done = f32[32,4096]{1,0:T(8,128)} async-done(((f32[32,4096]{1,0:T(8,128)}), f32[32,4096]{1,0:T(8,128)}) %all-reduce.4.cloned.1.call-update) | async-done | bytes 524304 | tf_op jit(solution)/shard_map/psum | solution.py:27
  137.9 1.1 broadcast_select_fusion.2
  139.7 2.4 scatter_fusion
  142.1 2.6 copy.36
  144.7 1.9 reshape.196
  146.7 10.2 %fusion.3 = f32[8,256]{1,0:T(8,128)S(1)} fusion(f32[8,512,256]{1,2,0:T(8,128)} %copy.34, f32[8,512,256]{2,1,0:T(8,128)} %bitcast.80, f32[512,512,1]{1,0,2:T(8,128)S(1)} %reshape.196, pred[8,512]{1,0:T(8,128)(4,1)S(1)} %broadcast_in_dim.107), kind=kOutput, calls=%fused_computation.13 | convolution fusion | flops 3224369152 | bytes 9449472 | tf_op jit(solution)/shard_map/uv,bvp->bup/dot_general | solution.py:54
  157.0 3.9 %multiply_bitcast_fusion = (f32[512,8,256]{0,2,1:T(8,128)}, f32[512,8,256]{0,2,1:T(8,128)}) fusion(f32[8,512,256]{1,2,0:T(8,128)S(1)} %copy-done, f32[8,256]{1,0:T(8,128)S(1)} %fusion.20, pred[8,512]{1,0:T(8,128)(4,1)S(1)} %broadcast_in_dim.107), kind=kLoop, calls=%fused_computation.15 | loop fusion | flops 2097152 | bytes 12595200 | tf_op jit(solution)/shard_map/bup,bvp->uv/dot_general | solution.py:58
  160.9 5.4 %copy.38 = f32[512,8,256]{2,1,0:T(8,128)} copy(f32[512,8,256]{0,2,1:T(8,128)} %get-tuple-element.14) | data formatting | bytes 8388608 | tf_op jit(solution)/shard_map/bup,bvp->uv/dot_general | solution.py:58
  166.4 5.4 %copy.39 = f32[512,8,256]{2,1,0:T(8,128)} copy(f32[512,8,256]{0,2,1:T(8,128)} %get-tuple-element.15) | data formatting | bytes 8388608 | tf_op jit(solution)/shard_map/bup,bvp->uv/dot_general | solution.py:58
  171.8 10.8 %fusion.9 = f32[8,64,8,64]{3,1,2,0:T(8,128)S(1)} fusion(f32[8,64,8,256]{3,2,1,0:T(8,128)} %bitcast.83, f32[8,64,8,256,1]{3,2,1,0,4:T(8,128)} %bitcast.82), kind=kOutput, calls=%fused_computation.23 | convolution fusion | flops 3221225472 | bytes 9437184 | tf_op jit(solution)/shard_map/bup,bvp->uv/dot_general | solution.py:58
  183.8 1.5 gather_fusion.2
  186.6 89.4 %all-reduce.6.cloned.1.call-done = f32[32,4096]{1,0:T(8,128)} async-done(((f32[32,4096]{1,0:T(8,128)}), f32[32,4096]{1,0:T(8,128)}) %all-reduce.6.cloned.1.call-update) | async-done | bytes 524304
  276.0 1.5 constant_dynamic-slice_fusion
  (56 shorter events, 4.6 us)
Async XLA Ops:
  7.2 130.8 %all-reduce.4.cloned.1.call-start = ((), (), s32[]{:S(2)}) async-start(), calls=%async_computation | async-start | bytes 1048576 | tf_op jit(solution)/shard_map/psum | solution.py:27
  31.9 7.8 %copy-start.6 = (f32[256]{0:T(256)S(1)}, f32[256]{0:T(256)}, u32[]{:S(2)}) copy-start(f32[256]{0:T(256)} %param.12) | copy-start | bytes 3076
  39.7 5.3 %copy-start.5 = (s32[32,2]{0,1:T(2,128)S(1)}, s32[32,2]{0,1:T(2,128)}, u32[]{:S(2)}) copy-start(s32[32,2]{0,1:T(2,128)} %param.13) | copy-start | bytes 772
  39.7 5.3 %copy-start.7 = (s32[128]{0:T(128)S(1)}, s32[128]{0:T(128)}, u32[]{:S(2)}) copy-start(s32[128]{0:T(128)} %param.16) | copy-start | bytes 1540
  39.7 6.4 %copy-start.4 = (s32[128,8]{0,1:T(8,128)S(1)}, s32[128,8]{0,1:T(8,128)}, u32[]{:S(2)}) copy-start(s32[128,8]{0,1:T(8,128)} %param.15) | copy-start | bytes 12292
  39.7 8.4 %copy-start.8 = (s32[32]{0:T(128)S(1)}, s32[32]{0:T(128)}, u32[]{:S(2)}) copy-start(s32[32]{0:T(128)} %param.14) | copy-start | bytes 388
  44.9 231.1 %all-reduce.6.cloned.1.call-start = ((), (), s32[]{:S(2)}) async-start(), calls=%async_computation.1 | async-start | bytes 1048576
  146.7 10.2 %copy-start.2 = (f32[8,256]{1,0:T(8,128)S(1)}, f32[8,256]{1,0:T(8,128)}, u32[]{:S(2)}) copy-start(f32[8,256]{1,0:T(8,128)} %param.18) | copy-start | bytes 24580
  146.7 10.2 %copy-start.3 = (f32[8,256]{1,0:T(8,128)S(1)}, f32[8,256]{1,0:T(8,128)}, u32[]{:S(2)}) copy-start(f32[8,256]{1,0:T(8,128)} %param.19) | copy-start | bytes 24580
  146.7 10.3 %copy-start = (f32[8,512,256]{1,2,0:T(8,128)S(1)}, f32[8,512,256]{1,2,0:T(8,128)}, u32[]{:S(2)}) copy-start(f32[8,512,256]{1,2,0:T(8,128)} %copy.34) | copy-start | bytes 12582916
  156.9 4.0 %copy-start.1 = (f32[8,256]{1,0:T(8,128)}, f32[8,256]{1,0:T(8,128)S(1)}, u32[]{:S(2)}) copy-start(f32[8,256]{1,0:T(8,128)S(1)} %fusion.3) | copy-start | bytes 24580
  183.3 2.0 copy-start.9
Sparse Core Ops, SparseCore 0:
  45.1 92.8 all-reduce.3
  185.4 90.5 all-reduce.5

commit v2 on v1

--- a/solution.py
+++ b/solution.py
@@ -11,6 +11,7 @@
     devices = lax.axis_size("tiles")
     my_index = lax.axis_index("tiles")
     kept_count = kept_tiles.shape[0]
+    owned_count = kept_count // devices
     batch_count = tables.shape[0]
     batch_total = batch_slot.shape[0]
     state_count = coeffs.shape[0]
@@ -18,13 +19,23 @@
     points = tables.shape[-1]
     width = OV * BS
 
-    blocked = coeffs.reshape(state_count, block_total, BS)
-    left_rows = jnp.take(blocked, kept_tiles[:, 0], axis=1)
-    right_rows = jnp.take(blocked, kept_tiles[:, 1], axis=1) * occupation[:, None, None]
+    ladder_kept = jnp.arange(kept_count, dtype=jnp.int32)
+    slot_kept = jnp.zeros((kept_count,), jnp.int32).at[tile_slot].set(ladder_kept)
+    pairs = kept_tiles[slot_kept]
+    wide = coeffs.reshape(state_count, block_total // 2, 2 * BS)
+
+    def block_rows(block_ids):
+        rows = jnp.take(wide, block_ids // 2, axis=1)
+        return jnp.where((block_ids % 2 == 0)[None, :, None], rows[:, :, :BS], rows[:, :, BS:])
+
+    left_rows = block_rows(pairs[:, 0])
+    right_rows = block_rows(pairs[:, 1]) * occupation[:, None, None]
     partial = jnp.einsum(
         "srx,sry->rxy", left_rows, right_rows, precision=lax.Precision.HIGHEST
-    ).reshape(kept_count, BS * BS)
-    tile_values = lax.psum(partial, "tiles")
+    ).reshape(devices, owned_count, BS * BS)
+    owned = jnp.sum(lax.all_to_all(partial, "tiles", 0, 0, tiled=False), axis=0)
+    spread = jnp.broadcast_to(owned[None], (devices, owned_count, BS * BS))
+    tile_values = lax.all_to_all(spread, "tiles", 0, 0, tiled=False).reshape(kept_count, BS * BS)
 
     ladder_batch = jnp.arange(batch_total, dtype=jnp.int32)
     slot_batch = jnp.zeros((batch_total,), jnp.int32).at[batch_slot].set(ladder_batch)
@@ -39,8 +50,8 @@
         batch_count, width, points
     )
 
-    row_hit = kept_tiles[:, 0:1] == canon[None, :]
-    col_hit = kept_tiles[:, 1:2] == canon[None, :]
+    row_hit = pairs[:, 0:1] == canon[None, :]
+    col_hit = pairs[:, 1:2] == canon[None, :]
     present = jnp.any(row_hit, axis=1) & jnp.any(col_hit, axis=1)
     row_place = jnp.sum(jnp.where(row_hit, ladder_ov[None, :], 0), axis=1)
     col_place = jnp.sum(jnp.where(col_hit, ladder_ov[None, :], 0), axis=1)
@@ -61,10 +72,8 @@
     picked = full_matrix[row_place, :, col_place, :].reshape(kept_count, BS * BS)
     contrib = jnp.where(present[:, None], picked, 0.0)
 
-    ladder_kept = jnp.arange(kept_count, dtype=jnp.int32)
-    slot_kept = jnp.zeros((kept_count,), jnp.int32).at[tile_slot].set(ladder_kept)
-    by_slot = contrib[slot_kept]
-    matrix = lax.psum_scatter(by_slot, "tiles", scatter_dimension=0, tiled=True)
+    terms = contrib.reshape(devices, owned_count, BS * BS)
+    matrix = jnp.sum(lax.all_to_all(terms, "tiles", 0, 0, tiled=False), axis=0)
     return (density, matrix)
 
 

time: 285 us -> 185 us (0.65)
  waiting for transfers between devices: 163 us -> 11.6 us
  local copies, waits for them, and re-layouts: 66.8 us -> 92.6 us
  blocking collectives: 0 us -> 20.3 us
  between operations: 15 us -> 0.94 us
  starting transfers between devices: 0.08 us -> 11.5 us
  matrix products: 25 us -> 29.2 us
  other arithmetic: 14.2 us -> 17.7 us
    unnamed x3 -> x0, waiting for transfers between devices: 89.5 us -> none
    psum x1 -> x0, waiting for transfers between devices: 73.8 us -> none  [body(): tile_values = lax.psum(partial, 'tiles')]
    all_to_all x0 -> x1, blocking collectives: none -> 20.3 us  [body(): matrix = jnp.sum(lax.all_to_all(terms, 'tiles', 0, 0, tiled=False), axis=0)]
    reshape x1 -> x2, local copies, waits for them, and re-layouts: 0.41 us -> 18 us  [the longest x1 17.4 us: body(): wide = coeffs.reshape(state_count, block_total // 2, 2 * BS)]
    all_to_all x0 -> x2, waiting for transfers between devices: none -> 11.6 us  [the longest x1 11.6 us: body(): owned = jnp.sum(lax.all_to_all(partial, 'tiles', 0, 0, tiled=False), axis=0)]
    all_to_all x0 -> x2, starting transfers between devices: none -> 11.5 us  [the longest x1 7.38 us: body(): owned = jnp.sum(lax.all_to_all(partial, 'tiles', 0, 0, tiled=False), axis=0)]
    gather x3 -> x4, local copies, waits for them, and re-layouts: 15.8 us -> 23.3 us  [the longest x3 22.7 us: block_rows(): rows = jnp.take(wide, block_ids // 2, axis=1)]
    dot_general x1, matrix products: 3.96 us -> 8.15 us  [body(): jnp.einsum('srx,sry->rxy', left_rows, right_rows, precision=lax.Precision...]
  transfers between devices with their start and end apart: 2 -> 2, of which waited for: 2 -> 1; matrix products, arithmetic and copies ran while one was open for 7% -> 10% of each run, Pallas kernels for 0% -> 0%
where the time goes in v2:
time: 185 us; the launch traced here: 184 us
  local copies, waits for them, and re-layouts  92.6 us (50%)
  matrix products  29.2 us (16%)
  blocking collectives  20.3 us (11%)
  other arithmetic  17.7 us (10%)
  waiting for transfers between devices  11.6 us (6%)
  starting transfers between devices  11.5 us (6%)
    gather x3, local copies, waits for them, and re-layouts, block_rows(): rows = jnp.take(wide, block_ids // 2, axis=1)  22.7 us
    all_to_all x1, blocking collectives, body(): matrix = jnp.sum(lax.all_to_all(terms, 'tiles', 0, 0, tiled=False), axis=0)  20.3 us
    unnamed x19, local copies, waits for them, and re-layouts  19.1 us
    reshape x1, local copies, waits for them, and re-layouts, body(): wide = coeffs.reshape(state_count, block_total // 2, 2 * BS)  17.4 us
    all_to_all x1, waiting for transfers between devices, body(): owned = jnp.sum(lax.all_to_all(partial, 'tiles', 0, 0, tiled=False), axis=0)  11.6 us
    dot_general x2, local copies, waits for them, and re-layouts, body(): jnp.einsum('bup,bvp->uv', weighted, canon_tables, precision=lax.Precision...  10.9 us
    dot_general x1, matrix products, body(): jnp.einsum('bup,bvp->uv', weighted, canon_tables, precision=lax.Precision...  10.8 us
    gather x3, local copies, waits for them, and re-layouts, body(): jnp.take_along_axis(grid, source[:, :, None, None], axis=1)  10.4 us
  transfers between devices with their start and end apart: 2, of which 1 were waited for; matrix products, arithmetic and copies ran while one was open for 10% of the time, Pallas kernels for 0%

profile of v2, /device:TPU:0, one launch (start us, length us, event | category | flops | bytes accessed | tf_op | source)
XLA Modules:
  0.0 183.8 jit_solution(13241953993820447859)
XLA Ops:
  3.6 17.5 %copy.58 = f32[256,16384]{0,1:T(8,128)} copy(f32[256,16384]{1,0:T(8,128)} %param.11) | data formatting | bytes 33554432 | tf_op args[0]
  21.0 17.4 %copy.59 = f32[256,128,128]{2,0,1:T(8,128)} copy(f32[256,128,128]{0,2,1:T(8,128)} %bitcast.63) | data formatting | bytes 33554432 | tf_op jit(solution)/shard_map/reshape | solution.py:25
  38.4 8.6 %gather_fusion.5 = f32[32,256,128]{2,1,0:T(8,128)} fusion(f32[256,128,128]{2,0,1:T(8,128)} %copy.59, s32[1024]{0:T(1024)S(1)} %pad_clamp_fusion), kind=kCustom, calls=%fused_computation.1.clone | custom fusion | bytes 8388736 | tf_op jit(solution)/shard_map/jit(_take)/gather | solution.py:28
  47.0 5.6 %copy.61 = f32[32,256,128]{1,2,0:T(8,128)} copy(f32[32,256,128]{2,1,0:T(8,128)} %gather_fusion.5) | data formatting | bytes 8388608 | tf_op jit(solution)/shard_map/jit(_take)/gather | solution.py:28
  52.6 8.6 %gather_fusion.4 = f32[32,256,128]{2,1,0:T(8,128)} fusion(f32[256,128,128]{2,0,1:T(8,128)} %copy.59, s32[1024]{0:T(1024)S(1)} %pad_clamp_fusion.1), kind=kCustom, calls=%fused_computation.clone | custom fusion | bytes 8388736 | tf_op jit(solution)/shard_map/jit(_take)/gather | solution.py:28
  61.1 2.9 %select_bitcast_fusion = f32[256,32,128]{0,2,1:T(8,128)S(1)} fusion(f32[32,256,128]{1,2,0:T(8,128)} %copy.61, pred[32]{0:T(512)(128)(4,1)S(1)} %get-tuple-element.12), kind=kLoop, calls=%fused_computation.18 | loop fusion | flops 1048576 | bytes 8388640 | tf_op jit(solution)/shard_map/jit(_take)/select_n | solution.py:28
  65.3 8.2 %fusion = f32[32,64,64]{2,1,0:T(8,128)S(1)} fusion(f32[256,32,128]{2,0,1:T(8,128)S(1)} %select_bitcast_fusion.1, f32[256,32,128]{0,2,1:T(8,128)S(1)} %select_bitcast_fusion, pred[32]{0:T(512)(128)(4,1)S(1)} %get-tuple-element.22, f32[256]{0:T(256)S(1)} %copy-done.6, pred[32]{0:T(512)(128)(4,1)S(1)} %get-tuple-element.20), kind=kOutput, calls=%fused_computation.10 | convolution fusion | flops 404226048 | bytes 13109248 | tf_op jit(solution)/shard_map/srx,sry->rxy/dot_general | solution.py:33
  73.4 1.3 reshape.177
  74.8 7.4 %all-to-all-start = ((f32[16,2,4096]{2,1,0:T(2,128)}), f32[16,2,4096]{2,1,0:T(2,128)S(1)}, u32[]{:S(2)}, u32[]{:S(2)}) async-start(f32[16,2,4096]{2,1,0:T(2,128)} %reshape.177), calls=%async_computation | async-start | bytes 1048576 | tf_op jit(solution)/shard_map/all_to_all | solution.py:36
  85.0 11.6 %all-to-all-done = f32[16,2,4096]{2,1,0:T(2,128)S(1)} async-done(((f32[16,2,4096]{2,1,0:T(2,128)}), f32[16,2,4096]{2,1,0:T(2,128)S(1)}, u32[]{:S(2)}, u32[]{:S(2)}) %all-to-all-start) | async-done | bytes 524320 | tf_op jit(solution)/shard_map/all_to_all | solution.py:36
  96.8 1.0 broadcast_in_dim.146
  97.8 4.1 %all-to-all-start.1 = ((f32[16,2,4096]{2,1,0:T(2,128)}), f32[16,2,4096]{2,1,0:T(2,128)S(1)}, u32[]{:S(2)}, u32[]{:S(2)}) async-start(f32[16,2,4096]{2,1,0:T(2,128)} %broadcast_in_dim.146), calls=%async_computation.1 | async-start | bytes 1048576 | tf_op jit(solution)/shard_map/all_to_all | solution.py:38
  102.0 5.0 %gather_fusion.3 = f32[64,64,256]{2,1,0:T(8,128)} fusion(f32[8,8,64,256]{3,2,1,0:T(8,128)} %bitcast.67, s32[64]{0:T(128)S(1)} %reshape.219), kind=kCustom, calls=%fused_computation.5 | custom fusion | bytes 8389120 | tf_op jit(solution)/shard_map/jit(take_along_axis)/gather | solution.py:49
  107.0 5.3 %copy.56 = f32[8,512,256]{1,2,0:T(8,128)} copy(f32[8,512,256]{2,1,0:T(8,128)} %bitcast.64) | data formatting | bytes 8388608 | tf_op jit(solution)/shard_map/jit(take_along_axis)/gather | solution.py:49
  112.8 4.5 %broadcast_select_fusion = f32[8,8,64,256]{3,2,1,0:T(8,128)} fusion(f32[8,8,64,256]{3,2,1,0:T(8,128)} %bitcast.65, pred[8,8]{1,0:T(8,128)(4,1)S(1)} %compare_and_fusion), kind=kLoop, calls=%fused_computation.25 | loop fusion | flops 1048576 | bytes 8388672 | tf_op jit(solution)/shard_map/jit(take_along_axis)/select_n | solution.py:49
  118.3 2.4 %scatter_fusion = f32[8,64,8,64]{3,1,2,0:T(8,128)S(1)} fusion(f32[8,64,8,64]{3,1,2,0:T(8,128)S(1)} %broadcast_in_dim.137, s32[32]{0:T(128)S(1)} %get-tuple-element.19, f32[32,64,64]{2,1,0:T(8,128)S(1)} %broadcast_select_fusion.1), kind=kCustom, calls=%fused_computation.8 | custom fusion | flops 131072 | bytes 1573120 | tf_op jit(solution)/shard_map/scatter-add | solution.py:62
  120.7 2.6 %copy.63 = f32[8,64,8,64]{3,2,1,0:T(8,128)} copy(f32[8,64,8,64]{3,1,2,0:T(8,128)S(1)} %scatter_fusion) | data formatting | bytes 2097152 | tf_op jit(solution)/shard_map/scatter-add | solution.py:62
  123.3 1.9 %reshape.258 = f32[512,512,1]{1,0,2:T(8,128)S(1)} reshape(f32[8,64,8,64]{3,2,1,0:T(8,128)} %copy.63) | data formatting | bytes 2097152 | tf_op jit(solution)/shard_map/reshape | solution.py:63
  125.3 10.2 %fusion.5 = f32[8,256]{1,0:T(8,128)S(1)} fusion(f32[8,512,256]{1,2,0:T(8,128)} %copy.56, f32[8,512,256]{2,1,0:T(8,128)} %bitcast.66, f32[512,512,1]{1,0,2:T(8,128)S(1)} %reshape.258, pred[8,512]{1,0:T(8,128)(4,1)S(1)} %broadcast_in_dim.132), kind=kOutput, calls=%fused_computation.16 | convolution fusion | flops 3224369152 | bytes 9449472 | tf_op jit(solution)/shard_map/uv,bvp->bup/dot_general | solution.py:65
  135.6 3.9 %multiply_bitcast_fusion = (f32[512,8,256]{0,2,1:T(8,128)}, f32[512,8,256]{0,2,1:T(8,128)}) fusion(f32[8,512,256]{1,2,0:T(8,128)S(1)} %copy-done, f32[8,256]{1,0:T(8,128)S(1)} %fusion.20, pred[8,512]{1,0:T(8,128)(4,1)S(1)} %broadcast_in_dim.132), kind=kLoop, calls=%fused_computation.20 | loop fusion | flops 2097152 | bytes 12595200 | tf_op jit(solution)/shard_map/bup,bvp->uv/dot_general | solution.py:69
  139.5 5.4 %copy.65 = f32[512,8,256]{2,1,0:T(8,128)} copy(f32[512,8,256]{0,2,1:T(8,128)} %get-tuple-element.16) | data formatting | bytes 8388608 | tf_op jit(solution)/shard_map/bup,bvp->uv/dot_general | solution.py:69
  144.9 5.4 %copy.66 = f32[512,8,256]{2,1,0:T(8,128)} copy(f32[512,8,256]{0,2,1:T(8,128)} %get-tuple-element.17) | data formatting | bytes 8388608 | tf_op jit(solution)/shard_map/bup,bvp->uv/dot_general | solution.py:69
  150.4 10.8 %fusion.11 = f32[8,64,8,64]{3,1,2,0:T(8,128)S(1)} fusion(f32[8,64,8,256]{3,2,1,0:T(8,128)} %bitcast.69, f32[8,64,8,256,1]{3,2,1,0,4:T(8,128)} %bitcast.68), kind=kOutput, calls=%fused_computation.27 | convolution fusion | flops 3221225472 | bytes 9437184 | tf_op jit(solution)/shard_map/bup,bvp->uv/dot_general | solution.py:69
  162.7 20.3 %all_to_all.15 = f32[16,2,4096]{2,1,0:T(2,128)S(1)} all-to-all(f32[16,2,4096]{2,1,0:T(2,128)S(1)} %broadcast_select_fusion.2), channel_id=1, replica_groups=mesh['groups'=2,'tiles'=16] {'tiles'}, dimensions={0} | all-to-all | bytes 1048576 | tf_op jit(solution)/shard_map/all_to_all | solution.py:76
  (59 shorter events, 10.9 us)
Async XLA Ops:
  61.1 3.4 %copy-start.1 = (f32[32,256,128]{2,1,0:T(8,128)S(1)}, f32[32,256,128]{2,1,0:T(8,128)}, u32[]{:S(2)}) copy-start(f32[32,256,128]{2,1,0:T(8,128)} %gather_fusion.4) | copy-start | bytes 12582916
  64.6 0.7 copy-start.6
  65.3 16.9 %copy-start.5 = (s32[128,8]{0,1:T(8,128)S(1)}, s32[128,8]{0,1:T(8,128)}, u32[]{:S(2)}) copy-start(s32[128,8]{0,1:T(8,128)} %param.15) | copy-start | bytes 12292
  65.3 17.0 %copy-start.7 = (s32[128]{0:T(128)S(1)}, s32[128]{0:T(128)}, u32[]{:S(2)}) copy-start(s32[128]{0:T(128)} %param.16) | copy-start | bytes 1540
  74.8 21.9 %all-to-all-start = ((f32[16,2,4096]{2,1,0:T(2,128)}), f32[16,2,4096]{2,1,0:T(2,128)S(1)}, u32[]{:S(2)}, u32[]{:S(2)}) async-start(f32[16,2,4096]{2,1,0:T(2,128)} %reshape.177), calls=%async_computation | async-start | bytes 1048576 | tf_op jit(solution)/shard_map/all_to_all | solution.py:36
  97.8 19.5 %all-to-all-start.1 = ((f32[16,2,4096]{2,1,0:T(2,128)}), f32[16,2,4096]{2,1,0:T(2,128)S(1)}, u32[]{:S(2)}, u32[]{:S(2)}) async-start(f32[16,2,4096]{2,1,0:T(2,128)} %broadcast_in_dim.146), calls=%async_computation.1 | async-start | bytes 1048576 | tf_op jit(solution)/shard_map/all_to_all | solution.py:38
  125.3 10.2 %copy-start.3 = (f32[8,256]{1,0:T(8,128)S(1)}, f32[8,256]{1,0:T(8,128)}, u32[]{:S(2)}) copy-start(f32[8,256]{1,0:T(8,128)} %param.18) | copy-start | bytes 24580
  125.3 10.2 %copy-start.4 = (f32[8,256]{1,0:T(8,128)S(1)}, f32[8,256]{1,0:T(8,128)}, u32[]{:S(2)}) copy-start(f32[8,256]{1,0:T(8,128)} %param.19) | copy-start | bytes 24580
  125.3 10.3 %copy-start = (f32[8,512,256]{1,2,0:T(8,128)S(1)}, f32[8,512,256]{1,2,0:T(8,128)}, u32[]{:S(2)}) copy-start(f32[8,512,256]{1,2,0:T(8,128)} %copy.56) | copy-start | bytes 12582916
  135.5 4.0 %copy-start.2 = (f32[8,256]{1,0:T(8,128)}, f32[8,256]{1,0:T(8,128)S(1)}, u32[]{:S(2)}) copy-start(f32[8,256]{1,0:T(8,128)S(1)} %fusion.5) | copy-start | bytes 24580

commit v3 on v2

--- a/solution.py
+++ b/solution.py
@@ -1,10 +1,49 @@
 import jax
 import jax.numpy as jnp
 from jax import lax
+from jax.experimental import pallas as pl
+from jax.experimental.pallas import tpu as pltpu
 from jax.sharding import PartitionSpec as P
 
 BS = 64
 OV = 8
+
+
+def tile_kernel(pairs_ref, left_ref, right_ref, occ_ref, out_ref):
+    k = pl.program_id(0)
+    row_block = pairs_ref[2 * k]
+    col_block = pairs_ref[2 * k + 1]
+    left = left_ref[...]
+    right = right_ref[...] * occ_ref[...]
+    left = jnp.where(row_block % 2 == 0, left[:, :BS], left[:, BS:])
+    right = jnp.where(col_block % 2 == 0, right[:, :BS], right[:, BS:])
+    out_ref[0] = lax.dot_general(
+        left,
+        right,
+        (((0,), (0,)), ((), ())),
+        precision=lax.Precision.HIGHEST,
+        preferred_element_type=jnp.float32,
+    )
+
+
+def tile_products(coeffs, occupation, pairs):
+    state_count = coeffs.shape[0]
+    kept_count = pairs.shape[0]
+    grid_spec = pltpu.PrefetchScalarGridSpec(
+        num_scalar_prefetch=1,
+        grid=(kept_count,),
+        in_specs=[
+            pl.BlockSpec((state_count, 2 * BS), lambda k, p: (0, p[2 * k] // 2)),
+            pl.BlockSpec((state_count, 2 * BS), lambda k, p: (0, p[2 * k + 1] // 2)),
+            pl.BlockSpec((state_count, 1), lambda k, p: (0, 0)),
+        ],
+        out_specs=pl.BlockSpec((1, BS, BS), lambda k, p: (k, 0, 0)),
+    )
+    return pl.pallas_call(
+        tile_kernel,
+        grid_spec=grid_spec,
+        out_shape=jax.ShapeDtypeStruct((kept_count, BS, BS), jnp.float32),
+    )(pairs.reshape(-1), coeffs, coeffs, occupation.reshape(state_count, 1))
 
 
 def body(coeffs, occupation, kept_tiles, tile_slot, blocks, batch_slot, tables, weights, local_pot):
@@ -22,17 +61,7 @@
     ladder_kept = jnp.arange(kept_count, dtype=jnp.int32)
     slot_kept = jnp.zeros((kept_count,), jnp.int32).at[tile_slot].set(ladder_kept)
     pairs = kept_tiles[slot_kept]
-    wide = coeffs.reshape(state_count, block_total // 2, 2 * BS)
-
-    def block_rows(block_ids):
-        rows = jnp.take(wide, block_ids // 2, axis=1)
-        return jnp.where((block_ids % 2 == 0)[None, :, None], rows[:, :, :BS], rows[:, :, BS:])
-
-    left_rows = block_rows(pairs[:, 0])
-    right_rows = block_rows(pairs[:, 1]) * occupation[:, None, None]
-    partial = jnp.einsum(
-        "srx,sry->rxy", left_rows, right_rows, precision=lax.Precision.HIGHEST
-    ).reshape(devices, owned_count, BS * BS)
+    partial = tile_products(coeffs, occupation, pairs).reshape(devices, owned_count, BS * BS)
     owned = jnp.sum(lax.all_to_all(partial, "tiles", 0, 0, tiled=False), axis=0)
     spread = jnp.broadcast_to(owned[None], (devices, owned_count, BS * BS))
     tile_values = lax.all_to_all(spread, "tiles", 0, 0, tiled=False).reshape(kept_count, BS * BS)

time: 185 us -> 141 us (0.76)
  local copies, waits for them, and re-layouts: 92.6 us -> 37.6 us
  Pallas kernels: 0 us -> 24.7 us
  matrix products: 29.2 us -> 21 us
  other arithmetic: 17.7 us -> 14.3 us
  blocking collectives: 20.3 us -> 18.4 us
    pallas_call x0 -> x1, Pallas kernels: none -> 24.7 us  [tile_products(): pl.pallas_call(tile_kernel, grid_spec=grid_spec, out_shape=jax.ShapeDtype...]
    gather x3 -> x0, local copies, waits for them, and re-layouts: 22.7 us -> none  [block_rows(): rows = jnp.take(wide, block_ids // 2, axis=1)]
    unnamed x19 -> x14, local copies, waits for them, and re-layouts: 19.1 us -> 0.89 us
    reshape x2 -> x3, local copies, waits for them, and re-layouts: 18.7 us -> 4.67 us  [the longest x1 2.59 us: body(): tile_products(coeffs, occupation, pairs)]
    all_to_all x1, waiting for transfers between devices: 11.6 us -> 1.02 us  [body(): owned = jnp.sum(lax.all_to_all(partial, 'tiles', 0, 0, tiled=False), axis=0)]
    all_to_all x1, waiting for transfers between devices: 0.01 us -> 9.47 us  [body(): lax.all_to_all(spread, 'tiles', 0, 0, tiled=False)]
    dot_general x1 -> x0, matrix products: 8.15 us -> none  [body(): jnp.einsum('srx,sry->rxy', left_rows, right_rows, precision=lax.Precision...]
    select_n x2 -> x0, other arithmetic: 3.41 us -> none  [block_rows(): rows = jnp.take(wide, block_ids // 2, axis=1)]
  transfers between devices with their start and end apart: 2 -> 2, of which waited for: 1 -> 2; matrix products, arithmetic and copies ran while one was open for 10% -> 13% of each run, Pallas kernels for 0% -> 0%
where the time goes in v3:
time: 141 us; the launch traced here: 140 us
  local copies, waits for them, and re-layouts  37.6 us (27%)
  Pallas kernels  24.7 us (18%)
  matrix products  21 us (15%)
  blocking collectives  18.4 us (13%)
  other arithmetic  14.3 us (10%)
  starting transfers between devices  12.4 us (9%)
  waiting for transfers between devices  10.5 us (7%)
    pallas_call x1, Pallas kernels, tile_products(): pl.pallas_call(tile_kernel, grid_spec=grid_spec, out_shape=jax.ShapeDtype...  24.7 us
    all_to_all x1, blocking collectives, body(): matrix = jnp.sum(lax.all_to_all(terms, 'tiles', 0, 0, tiled=False), axis=0)  18.4 us
    dot_general x2, local copies, waits for them, and re-layouts, body(): jnp.einsum('bup,bvp->uv', weighted, canon_tables, precision=lax.Precision...  10.9 us
    dot_general x1, matrix products, body(): jnp.einsum('bup,bvp->uv', weighted, canon_tables, precision=lax.Precision...  10.8 us
    gather x3, local copies, waits for them, and re-layouts, body(): jnp.take_along_axis(grid, source[:, :, None, None], axis=1)  10.4 us
    dot_general x1, matrix products, body(): jnp.einsum('uv,bvp->bup', dense, canon_tables, precision=lax.Precision.HIGH)  10.2 us
    all_to_all x1, waiting for transfers between devices, body(): lax.all_to_all(spread, 'tiles', 0, 0, tiled=False)  9.47 us
    all_to_all x1, starting transfers between devices, body(): owned = jnp.sum(lax.all_to_all(partial, 'tiles', 0, 0, tiled=False), axis=0)  7.39 us
  transfers between devices with their start and end apart: 2, of which 2 were waited for; matrix products, arithmetic and copies ran while one was open for 13% of the time, Pallas kernels for 0%

profile of v3, /device:TPU:0, one launch (start us, length us, event | category | flops | bytes accessed | tf_op | source)
XLA Modules:
  0.0 139.7 jit_solution(4139450878275315858)
XLA Ops:
  0.6 0.8 copy.28
  4.0 1.5 %copy.29.occ_ref = f32[256,1]{1,0:T(8,128)} copy(f32[256,1]{0,1:T(1,128)} %bitcast.65) | data formatting | bytes 2048 | tf_op jit(solution)/shard_map/reshape | solution.py:46
  5.4 24.7 %shard_map.104 = f32[32,64,64]{2,1,0:T(8,128)} custom-call(s32[64]{0:T(128)} %reshape.129.pairs_ref, f32[256,16384]{1,0:T(8,128)} %right_ref.1, f32[256,16384]{1,0:T(8,128)} %right_ref.1, f32[256,1]{1,0:T(8,128)} %copy.29.occ_ref), custom_call_target="tpu_custom_call" | custom-call | tf_op jit(solution)/shard_map/pallas_call | solution.py:42
  30.1 2.6 %reshape.131 = f32[16,2,4096]{2,1,0:T(2,128)} reshape(f32[32,64,64]{2,1,0:T(8,128)} %shard_map.104) | data formatting | bytes 1048576 | tf_op jit(solution)/shard_map/reshape | solution.py:64
  32.7 7.4 %all-to-all-start = ((f32[16,2,4096]{2,1,0:T(2,128)}), f32[16,2,4096]{2,1,0:T(2,128)S(1)}, u32[]{:S(2)}, u32[]{:S(2)}) async-start(f32[16,2,4096]{2,1,0:T(2,128)} %reshape.131), calls=%async_computation | async-start | bytes 1048576 | tf_op jit(solution)/shard_map/all_to_all | solution.py:65
  40.3 1.0 scatter_custom_fusion
  41.9 1.0 sort.15
  43.1 5.0 %gather_fusion.3 = f32[64,64,256]{2,1,0:T(8,128)} fusion(f32[8,8,64,256]{3,2,1,0:T(8,128)} %bitcast.62, s32[64]{0:T(128)S(1)} %reshape.157), kind=kCustom, calls=%fused_computation.3 | custom fusion | bytes 8389120 | tf_op jit(solution)/shard_map/jit(take_along_axis)/gather | solution.py:78
  48.0 5.3 %copy.27 = f32[8,512,256]{1,2,0:T(8,128)} copy(f32[8,512,256]{2,1,0:T(8,128)} %bitcast.59) | data formatting | bytes 8388608 | tf_op jit(solution)/shard_map/jit(take_along_axis)/gather | solution.py:78
  53.6 1.0 all-to-all-done
  54.7 1.0 broadcast_in_dim.119
  55.8 5.0 %all-to-all-start.1 = ((f32[16,2,4096]{2,1,0:T(2,128)}), f32[16,2,4096]{2,1,0:T(2,128)S(1)}, u32[]{:S(2)}, u32[]{:S(2)}) async-start(f32[16,2,4096]{2,1,0:T(2,128)} %broadcast_in_dim.119), calls=%async_computation.1 | async-start | bytes 1048576 | tf_op jit(solution)/shard_map/all_to_all | solution.py:67
  61.3 4.5 %broadcast_select_fusion = f32[8,8,64,256]{3,2,1,0:T(8,128)} fusion(f32[8,8,64,256]{3,2,1,0:T(8,128)} %bitcast.60, pred[8,8]{1,0:T(8,128)(4,1)S(1)} %compare_and_fusion), kind=kLoop, calls=%fused_computation.15 | loop fusion | flops 1048576 | bytes 8388672 | tf_op jit(solution)/shard_map/jit(take_along_axis)/select_n | solution.py:78
  65.8 9.5 %all-to-all-done.1 = f32[16,2,4096]{2,1,0:T(2,128)S(1)} async-done(((f32[16,2,4096]{2,1,0:T(2,128)}), f32[16,2,4096]{2,1,0:T(2,128)S(1)}, u32[]{:S(2)}, u32[]{:S(2)}) %all-to-all-start.1) | async-done | bytes 524320 | tf_op jit(solution)/shard_map/all_to_all | solution.py:67
  76.3 2.4 %scatter_fusion = f32[8,64,8,64]{3,1,2,0:T(8,128)S(1)} fusion(f32[8,64,8,64]{3,1,2,0:T(8,128)S(1)} %broadcast_in_dim.112, s32[32]{0:T(128)S(1)} %get-tuple-element.14, f32[32,64,64]{2,1,0:T(8,128)S(1)} %broadcast_select_fusion.1), kind=kCustom, calls=%fused_computation.6 | custom fusion | flops 131072 | bytes 1573120 | tf_op jit(solution)/shard_map/scatter-add | solution.py:91
  78.7 2.5 %copy.30 = f32[8,64,8,64]{3,2,1,0:T(8,128)} copy(f32[8,64,8,64]{3,1,2,0:T(8,128)S(1)} %scatter_fusion) | data formatting | bytes 2097152 | tf_op jit(solution)/shard_map/scatter-add | solution.py:91
  81.2 1.9 %reshape.190 = f32[512,512,1]{1,0,2:T(8,128)S(1)} reshape(f32[8,64,8,64]{3,2,1,0:T(8,128)} %copy.30) | data formatting | bytes 2097152 | tf_op jit(solution)/shard_map/reshape | solution.py:92
  83.2 10.2 %fusion.3 = f32[8,256]{1,0:T(8,128)S(1)} fusion(f32[8,512,256]{1,2,0:T(8,128)} %copy.27, f32[8,512,256]{2,1,0:T(8,128)} %bitcast.61, f32[512,512,1]{1,0,2:T(8,128)S(1)} %reshape.190, pred[8,512]{1,0:T(8,128)(4,1)S(1)} %broadcast_in_dim.107), kind=kOutput, calls=%fused_computation.11 | convolution fusion | flops 3224369152 | bytes 9449472 | tf_op jit(solution)/shard_map/uv,bvp->bup/dot_general | solution.py:94
  93.4 3.9 %multiply_bitcast_fusion = (f32[512,8,256]{0,2,1:T(8,128)}, f32[512,8,256]{0,2,1:T(8,128)}) fusion(f32[8,512,256]{1,2,0:T(8,128)S(1)} %copy-done, f32[8,256]{1,0:T(8,128)S(1)} %fusion.12, pred[8,512]{1,0:T(8,128)(4,1)S(1)} %broadcast_in_dim.107), kind=kLoop, calls=%fused_computation.13 | loop fusion | flops 2097152 | bytes 12595200 | tf_op jit(solution)/shard_map/bup,bvp->uv/dot_general | solution.py:98
  97.4 5.4 %copy.32 = f32[512,8,256]{2,1,0:T(8,128)} copy(f32[512,8,256]{0,2,1:T(8,128)} %get-tuple-element.11) | data formatting | bytes 8388608 | tf_op jit(solution)/shard_map/bup,bvp->uv/dot_general | solution.py:98
  102.8 5.4 %copy.33 = f32[512,8,256]{2,1,0:T(8,128)} copy(f32[512,8,256]{0,2,1:T(8,128)} %get-tuple-element.12) | data formatting | bytes 8388608 | tf_op jit(solution)/shard_map/bup,bvp->uv/dot_general | solution.py:98
  108.2 10.8 %fusion.5 = f32[8,64,8,64]{3,1,2,0:T(8,128)S(1)} fusion(f32[8,64,8,256]{3,2,1,0:T(8,128)} %bitcast.64, f32[8,64,8,256,1]{3,2,1,0,4:T(8,128)} %bitcast.63), kind=kOutput, calls=%fused_computation.16 | convolution fusion | flops 3221225472 | bytes 9437184 | tf_op jit(solution)/shard_map/bup,bvp->uv/dot_general | solution.py:98
  120.6 18.4 %all_to_all.15 = f32[16,2,4096]{2,1,0:T(2,128)S(1)} all-to-all(f32[16,2,4096]{2,1,0:T(2,128)S(1)} %broadcast_select_fusion.2), channel_id=1, replica_groups=mesh['groups'=2,'tiles'=16] {'tiles'}, dimensions={0} | all-to-all | bytes 1048576 | tf_op jit(solution)/shard_map/all_to_all | solution.py:105
  139.0 0.8 reduce_sum.68
  (47 shorter events, 6.8 us)
Async XLA Ops:
  5.4 34.7 %copy-start.5 = (s32[128]{0:T(128)S(1)}, s32[128]{0:T(128)}, u32[]{:S(2)}) copy-start(s32[128]{0:T(128)} %param.14) | copy-start | bytes 1540
  5.4 34.7 %copy-start.4 = (s32[128,8]{0,1:T(8,128)S(1)}, s32[128,8]{0,1:T(8,128)}, u32[]{:S(2)}) copy-start(s32[128,8]{0,1:T(8,128)} %param.13) | copy-start | bytes 12292
  32.7 21.9 %all-to-all-start = ((f32[16,2,4096]{2,1,0:T(2,128)}), f32[16,2,4096]{2,1,0:T(2,128)S(1)}, u32[]{:S(2)}, u32[]{:S(2)}) async-start(f32[16,2,4096]{2,1,0:T(2,128)} %reshape.131), calls=%async_computation | async-start | bytes 1048576 | tf_op jit(solution)/shard_map/all_to_all | solution.py:65
  55.8 19.5 %all-to-all-start.1 = ((f32[16,2,4096]{2,1,0:T(2,128)}), f32[16,2,4096]{2,1,0:T(2,128)S(1)}, u32[]{:S(2)}, u32[]{:S(2)}) async-start(f32[16,2,4096]{2,1,0:T(2,128)} %broadcast_in_dim.119), calls=%async_computation.1 | async-start | bytes 1048576 | tf_op jit(solution)/shard_map/all_to_all | solution.py:67
  83.1 10.2 %copy-start.2 = (f32[8,256]{1,0:T(8,128)S(1)}, f32[8,256]{1,0:T(8,128)}, u32[]{:S(2)}) copy-start(f32[8,256]{1,0:T(8,128)} %param.16) | copy-start | bytes 24580
  83.1 10.2 %copy-start.3 = (f32[8,256]{1,0:T(8,128)S(1)}, f32[8,256]{1,0:T(8,128)}, u32[]{:S(2)}) copy-start(f32[8,256]{1,0:T(8,128)} %param.17) | copy-start | bytes 24580
  83.1 10.3 %copy-start = (f32[8,512,256]{1,2,0:T(8,128)S(1)}, f32[8,512,256]{1,2,0:T(8,128)}, u32[]{:S(2)}) copy-start(f32[8,512,256]{1,2,0:T(8,128)} %copy.27) | copy-start | bytes 12582916
  93.4 4.0 %copy-start.1 = (f32[8,256]{1,0:T(8,128)}, f32[8,256]{1,0:T(8,128)S(1)}, u32[]{:S(2)}) copy-start(f32[8,256]{1,0:T(8,128)S(1)} %fusion.3) | copy-start | bytes 24580

commit v4 on v3

--- a/solution.py
+++ b/solution.py
@@ -46,6 +46,74 @@
     )(pairs.reshape(-1), coeffs, coeffs, occupation.reshape(state_count, 1))
 
 
+def split_dot(left, right, dims):
+    left_hi = left.astype(jnp.bfloat16)
+    left_lo = (left - left_hi.astype(jnp.float32)).astype(jnp.bfloat16)
+    right_hi = right.astype(jnp.bfloat16)
+    right_lo = (right - right_hi.astype(jnp.float32)).astype(jnp.bfloat16)
+
+    def one(a, b):
+        return lax.dot_general(a, b, (dims, ((), ())), preferred_element_type=jnp.float32)
+
+    return one(left_hi, right_hi) + (one(left_hi, right_lo) + one(left_lo, right_hi))
+
+
+def batch_kernel(source_ref, table_ref, dense_ref, weight_ref, base_ref, density_ref, matrix_ref, canon_ref):
+    b = pl.program_id(0)
+    for q in range(OV):
+        start = pl.multiple_of(source_ref[b * OV + q] * BS, BS)
+        canon_ref[q * BS:(q + 1) * BS, :] = table_ref[0, pl.ds(start, BS), :]
+    grid = canon_ref[...]
+    mixed = split_dot(dense_ref[...], grid, ((1,), (0,)))
+    density = jnp.sum(grid * mixed, axis=0, keepdims=True)
+    potential = base_ref[0] + density - density * density * density / 6.0
+    density_ref[0] = density
+    weighted = grid * (weight_ref[0] * potential)
+    terms = split_dot(weighted, grid, ((1,), (1,)))
+
+    @pl.when(b == 0)
+    def _():
+        matrix_ref[...] = terms
+
+    @pl.when(b > 0)
+    def _():
+        matrix_ref[...] += terms
+
+
+def batch_terms(source, tables, dense, weights, local_pot):
+    batch_count, rows, points = tables.shape
+    grid_spec = pltpu.PrefetchScalarGridSpec(
+        num_scalar_prefetch=1,
+        grid=(batch_count,),
+        in_specs=[
+            pl.BlockSpec((1, rows, points), lambda b, s: (b, 0, 0)),
+            pl.BlockSpec((rows, rows), lambda b, s: (0, 0)),
+            pl.BlockSpec((1, 1, points), lambda b, s: (b, 0, 0)),
+            pl.BlockSpec((1, 1, points), lambda b, s: (b, 0, 0)),
+        ],
+        out_specs=[
+            pl.BlockSpec((1, 1, points), lambda b, s: (b, 0, 0)),
+            pl.BlockSpec((rows, rows), lambda b, s: (0, 0)),
+        ],
+        scratch_shapes=[pltpu.VMEM((rows, points), jnp.float32)],
+    )
+    density, matrix = pl.pallas_call(
+        batch_kernel,
+        grid_spec=grid_spec,
+        out_shape=[
+            jax.ShapeDtypeStruct((batch_count, 1, points), jnp.float32),
+            jax.ShapeDtypeStruct((rows, rows), jnp.float32),
+        ],
+    )(
+        source.reshape(-1),
+        tables,
+        dense,
+        weights.reshape(batch_count, 1, points),
+        local_pot.reshape(batch_count, 1, points),
+    )
+    return density.reshape(batch_count, points), matrix
+
+
 def body(coeffs, occupation, kept_tiles, tile_slot, blocks, batch_slot, tables, weights, local_pot):
     devices = lax.axis_size("tiles")
     my_index = lax.axis_index("tiles")
@@ -74,11 +142,6 @@
     ladder_ov = jnp.arange(OV, dtype=jnp.int32)
     match = my_blocks[:, :, None] == canon[None, None, :]
     source = jnp.sum(jnp.where(match, ladder_ov[None, :, None], 0), axis=1)
-    grid = tables.reshape(batch_count, OV, BS, points)
-    canon_tables = jnp.take_along_axis(grid, source[:, :, None, None], axis=1).reshape(
-        batch_count, width, points
-    )
-
     row_hit = pairs[:, 0:1] == canon[None, :]
     col_hit = pairs[:, 1:2] == canon[None, :]
     present = jnp.any(row_hit, axis=1) & jnp.any(col_hit, axis=1)
@@ -91,13 +154,8 @@
         .add(kept_values)
         .reshape(width, width)
     )
-    mixed = jnp.einsum("uv,bvp->bup", dense, canon_tables, precision=lax.Precision.HIGH)
-    density = jnp.sum(canon_tables * mixed, axis=1)
-    potential = local_pot + density - density * density * density / 6.0
-    weighted = canon_tables * (weights * potential)[:, None, :]
-    full_matrix = jnp.einsum(
-        "bup,bvp->uv", weighted, canon_tables, precision=lax.Precision.HIGH
-    ).reshape(OV, BS, OV, BS)
+    density, full_matrix = batch_terms(source, tables, dense, weights, local_pot)
+    full_matrix = full_matrix.reshape(OV, BS, OV, BS)
     picked = full_matrix[row_place, :, col_place, :].reshape(kept_count, BS * BS)
     contrib = jnp.where(present[:, None], picked, 0.0)
 

time: 141 us -> 130 us (0.922)
  waiting for transfers between devices: 10.5 us -> 37.6 us
  matrix products: 21 us -> 0 us
  Pallas kernels: 24.7 us -> 44 us
  blocking collectives: 18.4 us -> 0 us
  local copies, waits for them, and re-layouts: 37.6 us -> 24.2 us
  other arithmetic: 14.3 us -> 6.58 us
  starting transfers between devices: 12.4 us -> 15.6 us
    dot_general x2 -> x0, matrix products: 21 us -> none  [the longest x1 10.8 us: body(): jnp.einsum('bup,bvp->uv', weighted, canon_tables, precision=lax.Precision...]
    pallas_call x0 -> x1, Pallas kernels: none -> 19.4 us  [batch_terms(): pl.pallas_call(batch_kernel, grid_spec=grid_spec, out_shape=[jax.ShapeDty...]
    all_to_all x1 -> x0, blocking collectives: 18.4 us -> none  [body(): matrix = jnp.sum(lax.all_to_all(terms, 'tiles', 0, 0, tiled=False), axis=0)]
    all_to_all x0 -> x1, waiting for transfers between devices: none -> 13.9 us  [body(): matrix = jnp.sum(lax.all_to_all(terms, 'tiles', 0, 0, tiled=False), axis=0)]
    all_to_all x1, waiting for transfers between devices: 1.02 us -> 13.3 us  [body(): owned = jnp.sum(lax.all_to_all(partial, 'tiles', 0, 0, tiled=False), axis=0)]
    dot_general x2 -> x0, local copies, waits for them, and re-layouts: 10.9 us -> none  [body(): jnp.einsum('bup,bvp->uv', weighted, canon_tables, precision=lax.Precision...]
    gather x3 -> x0, local copies, waits for them, and re-layouts: 10.4 us -> none  [body(): jnp.take_along_axis(grid, source[:, :, None, None], axis=1)]
    reshape x0 -> x5, local copies, waits for them, and re-layouts: none -> 5.11 us  [the longest x2 3.3 us: body(): full_matrix = full_matrix.reshape(OV, BS, OV, BS)]
  transfers between devices with their start and end apart: 2 -> 3, of which waited for: 2 -> 3; matrix products, arithmetic and copies ran while one was open for 13% -> 4% of each run, Pallas kernels for 0% -> 0%
where the time goes in v4:
time: 130 us; the launch traced here: 129 us
  Pallas kernels  44 us (34%)
  waiting for transfers between devices  37.6 us (29%)
  local copies, waits for them, and re-layouts  24.2 us (19%)
  starting transfers between devices  15.6 us (12%)
  other arithmetic  6.58 us (5%)
    pallas_call x1, Pallas kernels, tile_products(): pl.pallas_call(tile_kernel, grid_spec=grid_spec, out_shape=jax.ShapeDtype...  24.6 us
    pallas_call x1, Pallas kernels, batch_terms(): pl.pallas_call(batch_kernel, grid_spec=grid_spec, out_shape=[jax.ShapeDty...  19.4 us
    all_to_all x1, waiting for transfers between devices, body(): matrix = jnp.sum(lax.all_to_all(terms, 'tiles', 0, 0, tiled=False), axis=0)  13.9 us
    all_to_all x1, waiting for transfers between devices, body(): owned = jnp.sum(lax.all_to_all(partial, 'tiles', 0, 0, tiled=False), axis=0)  13.3 us
    all_to_all x1, waiting for transfers between devices, body(): lax.all_to_all(spread, 'tiles', 0, 0, tiled=False)  10.5 us
    all_to_all x1, starting transfers between devices, body(): owned = jnp.sum(lax.all_to_all(partial, 'tiles', 0, 0, tiled=False), axis=0)  7.38 us
    all_to_all x1, starting transfers between devices, body(): matrix = jnp.sum(lax.all_to_all(terms, 'tiles', 0, 0, tiled=False), axis=0)  4.1 us
    all_to_all x1, starting transfers between devices, body(): lax.all_to_all(spread, 'tiles', 0, 0, tiled=False)  4.1 us
  transfers between devices with their start and end apart: 3, of which 3 were waited for; matrix products, arithmetic and copies ran while one was open for 4% of the time, Pallas kernels for 0%

profile of v4, /device:TPU:0, one launch (start us, length us, event | category | flops | bytes accessed | tf_op | source)
XLA Modules:
  0.0 128.8 jit_solution(1629491773208673773)
XLA Ops:
  0.6 0.8 copy.20
  1.4 0.7 compare_select_fusion.5
  2.1 0.7 scatter_custom_fusion.1
  4.0 1.5 %copy.21.occ_ref = f32[256,1]{1,0:T(8,128)} copy(f32[256,1]{0,1:T(1,128)} %bitcast.33) | data formatting | bytes 2048 | tf_op jit(solution)/shard_map/reshape | solution.py:46
  5.4 24.6 %shard_map.104 = f32[32,64,64]{2,1,0:T(8,128)} custom-call(s32[64]{0:T(128)} %reshape.90.pairs_ref, f32[256,16384]{1,0:T(8,128)} %right_ref.1, f32[256,16384]{1,0:T(8,128)} %right_ref.1, f32[256,1]{1,0:T(8,128)} %copy.21.occ_ref), custom_call_target="tpu_custom_call" | custom-call | tf_op jit(solution)/shard_map/pallas_call | solution.py:42
  30.1 2.6 %reshape.92 = f32[16,2,4096]{2,1,0:T(2,128)} reshape(f32[32,64,64]{2,1,0:T(8,128)} %shard_map.104) | data formatting | bytes 1048576 | tf_op jit(solution)/shard_map/reshape | solution.py:132
  32.7 7.4 %all-to-all-start = ((f32[16,2,4096]{2,1,0:T(2,128)}), f32[16,2,4096]{2,1,0:T(2,128)S(1)}, u32[]{:S(2)}, u32[]{:S(2)}) async-start(f32[16,2,4096]{2,1,0:T(2,128)} %reshape.92), calls=%async_computation | async-start | bytes 1048576 | tf_op jit(solution)/shard_map/all_to_all | solution.py:133
  40.2 1.0 scatter_custom_fusion
  41.3 13.3 %all-to-all-done = f32[16,2,4096]{2,1,0:T(2,128)S(1)} async-done(((f32[16,2,4096]{2,1,0:T(2,128)}), f32[16,2,4096]{2,1,0:T(2,128)S(1)}, u32[]{:S(2)}, u32[]{:S(2)}) %all-to-all-start) | async-done | bytes 524320 | tf_op jit(solution)/shard_map/all_to_all | solution.py:133
  54.7 1.0 broadcast_in_dim.95
  55.7 4.1 %all-to-all-start.1 = ((f32[16,2,4096]{2,1,0:T(2,128)}), f32[16,2,4096]{2,1,0:T(2,128)S(1)}, u32[]{:S(2)}, u32[]{:S(2)}) async-start(f32[16,2,4096]{2,1,0:T(2,128)} %broadcast_in_dim.95), calls=%async_computation.1 | async-start | bytes 1048576 | tf_op jit(solution)/shard_map/all_to_all | solution.py:135
  60.4 1.0 sort.15
  63.7 10.5 %all-to-all-done.1 = f32[16,2,4096]{2,1,0:T(2,128)S(1)} async-done(((f32[16,2,4096]{2,1,0:T(2,128)}), f32[16,2,4096]{2,1,0:T(2,128)S(1)}, u32[]{:S(2)}, u32[]{:S(2)}) %all-to-all-start.1) | async-done | bytes 524320 | tf_op jit(solution)/shard_map/all_to_all | solution.py:135
  75.3 2.4 %scatter_fusion = f32[8,64,8,64]{3,1,2,0:T(8,128)S(1)} fusion(f32[8,64,8,64]{3,1,2,0:T(8,128)S(1)} %broadcast_in_dim.88, s32[32]{0:T(128)S(1)} %get-tuple-element.16, f32[32,64,64]{2,1,0:T(8,128)S(1)} %broadcast_select_fusion), kind=kCustom, calls=%fused_computation.5 | custom fusion | flops 131072 | bytes 1573120 | tf_op jit(solution)/shard_map/scatter-add | solution.py:154
  77.7 2.5 %copy.22 = f32[8,64,8,64]{3,2,1,0:T(8,128)} copy(f32[8,64,8,64]{3,1,2,0:T(8,128)S(1)} %scatter_fusion) | data formatting | bytes 2097152 | tf_op jit(solution)/shard_map/scatter-add | solution.py:154
  80.2 2.7 %reshape.94.dense_ref = f32[512,512]{1,0:T(8,128)} reshape(f32[8,64,8,64]{3,2,1,0:T(8,128)} %copy.22) | data formatting | bytes 2097152 | tf_op jit(solution)/shard_map/reshape | solution.py:155
  82.9 19.4 %shard_map.105 = (f32[8,1,256]{2,1,0:T(1,128)}, f32[512,512]{1,0:T(8,128)}) custom-call(s32[64]{0:T(128)} %reshape.89.source_ref, f32[8,512,256]{2,1,0:T(8,128)} %table_ref.1, f32[512,512]{1,0:T(8,128)} %reshape.94.dense_ref, f32[8,1,256]{2,1,0:T(1,128)} %reshape.95.weight_ref, f32[8,1,256]{2,1,0:T(1,128)} %reshape.96.base_ref), custom_call_target="tpu_custom_call" | custom-call | tf_op jit(solution)/shard_map/pallas_call | solution.py:100
  102.3 1.6 %reshape.98 = f32[8,64,8,64]{3,2,1,0:T(8,128)S(1)} reshape(f32[512,512]{1,0:T(8,128)} %get-tuple-element.8) | data formatting | bytes 2097152 | tf_op jit(solution)/shard_map/reshape | solution.py:158
  103.9 1.7 %copy.23 = f32[8,64,8,64]{3,1,2,0:T(8,128)} copy(f32[8,64,8,64]{3,2,1,0:T(8,128)S(1)} %reshape.98) | data formatting | bytes 2097152 | tf_op jit(solution)/shard_map/reshape | solution.py:158
  105.6 2.2 %gather_fusion.2 = f32[32,64,64]{2,1,0:T(8,128)S(1)} fusion(f32[8,64,8,64]{3,1,2,0:T(8,128)} %copy.23, s32[32]{0:T(128)S(1)} %get-tuple-element.15), kind=kCustom, calls=%fused_computation.2 | custom fusion | bytes 1048832 | tf_op jit(solution)/shard_map/gather | solution.py:159
  108.4 1.1 broadcast_select_fusion.1
  109.5 4.1 %all-to-all-start.2 = ((f32[16,2,4096]{2,1,0:T(2,128)}), f32[16,2,4096]{2,1,0:T(2,128)S(1)}, u32[]{:S(2)}, u32[]{:S(2)}) async-start(f32[16,2,4096]{2,1,0:T(2,128)} %broadcast_select_fusion.1), calls=%async_computation.2 | async-start | bytes 1048576 | tf_op jit(solution)/shard_map/all_to_all | solution.py:163
  114.2 13.9 %all-to-all-done.2 = f32[16,2,4096]{2,1,0:T(2,128)S(1)} async-done(((f32[16,2,4096]{2,1,0:T(2,128)}), f32[16,2,4096]{2,1,0:T(2,128)S(1)}, u32[]{:S(2)}, u32[]{:S(2)}) %all-to-all-start.2) | async-done | bytes 524320 | tf_op jit(solution)/shard_map/all_to_all | solution.py:163
  128.0 0.8 reduce_sum.55
  (39 shorter events, 6.6 us)
Async XLA Ops:
  30.0 10.0 %copy-start.3 = (s32[128,8]{0,1:T(8,128)S(1)}, s32[128,8]{0,1:T(8,128)}, u32[]{:S(2)}) copy-start(s32[128,8]{0,1:T(8,128)} %param.13) | copy-start | bytes 12292
  30.0 10.1 %copy-start.4 = (s32[128]{0:T(128)S(1)}, s32[128]{0:T(128)}, u32[]{:S(2)}) copy-start(s32[128]{0:T(128)} %param.14) | copy-start | bytes 1540
  30.0 32.0 %copy-start = (f32[8,256]{1,0:T(8,128)S(1)}, f32[8,256]{1,0:T(8,128)}, u32[]{:S(2)}) copy-start(f32[8,256]{1,0:T(8,128)} %param.16) | copy-start | bytes 24580
  30.1 32.6 %copy-start.1 = (f32[8,256]{1,0:T(8,128)S(1)}, f32[8,256]{1,0:T(8,128)}, u32[]{:S(2)}) copy-start(f32[8,256]{1,0:T(8,128)} %param.17) | copy-start | bytes 24580
  32.7 21.9 %all-to-all-start = ((f32[16,2,4096]{2,1,0:T(2,128)}), f32[16,2,4096]{2,1,0:T(2,128)S(1)}, u32[]{:S(2)}, u32[]{:S(2)}) async-start(f32[16,2,4096]{2,1,0:T(2,128)} %reshape.92), calls=%async_computation | async-start | bytes 1048576 | tf_op jit(solution)/shard_map/all_to_all | solution.py:133
  55.7 18.6 %all-to-all-start.1 = ((f32[16,2,4096]{2,1,0:T(2,128)}), f32[16,2,4096]{2,1,0:T(2,128)S(1)}, u32[]{:S(2)}, u32[]{:S(2)}) async-start(f32[16,2,4096]{2,1,0:T(2,128)} %broadcast_in_dim.95), calls=%async_computation.1 | async-start | bytes 1048576 | tf_op jit(solution)/shard_map/all_to_all | solution.py:135
  107.8 5.8 %copy-start.2 = (f32[8,1,256]{2,1,0:T(1,128)S(1)}, f32[8,1,256]{2,1,0:T(1,128)}, u32[]{:S(2)}) copy-start(f32[8,1,256]{2,1,0:T(1,128)} %get-tuple-element.7) | copy-start | bytes 24580
  109.5 18.6 %all-to-all-start.2 = ((f32[16,2,4096]{2,1,0:T(2,128)}), f32[16,2,4096]{2,1,0:T(2,128)S(1)}, u32[]{:S(2)}, u32[]{:S(2)}) async-start(f32[16,2,4096]{2,1,0:T(2,128)} %broadcast_select_fusion.1), calls=%async_computation.2 | async-start | bytes 1048576 | tf_op jit(solution)/shard_map/all_to_all | solution.py:163

commit v5 on v4

--- a/solution.py
+++ b/solution.py
@@ -9,41 +9,51 @@
 OV = 8
 
 
-def tile_kernel(pairs_ref, left_ref, right_ref, occ_ref, out_ref):
+def tile_kernel(pairs_ref, *refs):
+    group = (len(refs) - 2) // 2
+    occ_ref = refs[2 * group]
+    out_ref = refs[2 * group + 1]
     k = pl.program_id(0)
-    row_block = pairs_ref[2 * k]
-    col_block = pairs_ref[2 * k + 1]
-    left = left_ref[...]
-    right = right_ref[...] * occ_ref[...]
-    left = jnp.where(row_block % 2 == 0, left[:, :BS], left[:, BS:])
-    right = jnp.where(col_block % 2 == 0, right[:, :BS], right[:, BS:])
-    out_ref[0] = lax.dot_general(
-        left,
-        right,
-        (((0,), (0,)), ((), ())),
-        precision=lax.Precision.HIGHEST,
-        preferred_element_type=jnp.float32,
-    )
+    occ = occ_ref[...]
+    for i in range(group):
+        row_block = pairs_ref[2 * (group * k + i)]
+        col_block = pairs_ref[2 * (group * k + i) + 1]
+        left = refs[i][...]
+        right = refs[group + i][...] * occ
+        left = jnp.where(row_block % 2 == 0, left[:, :BS], left[:, BS:])
+        right = jnp.where(col_block % 2 == 0, right[:, :BS], right[:, BS:])
+        out_ref[i] = lax.dot_general(
+            left,
+            right,
+            (((0,), (0,)), ((), ())),
+            precision=lax.Precision.HIGHEST,
+            preferred_element_type=jnp.float32,
+        )
 
 
 def tile_products(coeffs, occupation, pairs):
     state_count = coeffs.shape[0]
     kept_count = pairs.shape[0]
+    group = next(g for g in (4, 2, 1) if kept_count % g == 0)
+
+    def block_of(i, side):
+        return pl.BlockSpec(
+            (state_count, 2 * BS), lambda k, p: (0, p[2 * (group * k + i) + side] // 2)
+        )
+
     grid_spec = pltpu.PrefetchScalarGridSpec(
         num_scalar_prefetch=1,
-        grid=(kept_count,),
-        in_specs=[
-            pl.BlockSpec((state_count, 2 * BS), lambda k, p: (0, p[2 * k] // 2)),
-            pl.BlockSpec((state_count, 2 * BS), lambda k, p: (0, p[2 * k + 1] // 2)),
-            pl.BlockSpec((state_count, 1), lambda k, p: (0, 0)),
-        ],
-        out_specs=pl.BlockSpec((1, BS, BS), lambda k, p: (k, 0, 0)),
+        grid=(kept_count // group,),
+        in_specs=[block_of(i, 0) for i in range(group)]
+        + [block_of(i, 1) for i in range(group)]
+        + [pl.BlockSpec((state_count, 1), lambda k, p: (0, 0))],
+        out_specs=pl.BlockSpec((group, BS, BS), lambda k, p: (k, 0, 0)),
     )
     return pl.pallas_call(
         tile_kernel,
         grid_spec=grid_spec,
         out_shape=jax.ShapeDtypeStruct((kept_count, BS, BS), jnp.float32),
-    )(pairs.reshape(-1), coeffs, coeffs, occupation.reshape(state_count, 1))
+    )(pairs.reshape(-1), *([coeffs] * (2 * group)), occupation.reshape(state_count, 1))
 
 
 def split_dot(left, right, dims):

time: 130 us -> 116 us (0.89)
  Pallas kernels: 44 us -> 30.8 us
    pallas_call x1, Pallas kernels: 24.6 us -> 11.4 us  [tile_products(): pl.pallas_call(tile_kernel, grid_spec=grid_spec, out_shape=jax.ShapeDtype...]
  transfers between devices with their start and end apart: 3 -> 3, of which waited for: 3 -> 3; matrix products, arithmetic and copies ran while one was open for 4% -> 5% of each run, Pallas kernels for 0% -> 0%
where the time goes in v5:
time: 116 us
  waiting for transfers between devices  37.6 us (32%)
  Pallas kernels  30.8 us (27%)
  local copies, waits for them, and re-layouts  24.2 us (21%)
  starting transfers between devices  15.6 us (13%)
  other arithmetic  6.57 us (6%)
    pallas_call x1, Pallas kernels, batch_terms(): pl.pallas_call(batch_kernel, grid_spec=grid_spec, out_shape=[jax.ShapeDty...  19.4 us
    all_to_all x1, waiting for transfers between devices, body(): matrix = jnp.sum(lax.all_to_all(terms, 'tiles', 0, 0, tiled=False), axis=0)  13.9 us
    all_to_all x1, waiting for transfers between devices, body(): owned = jnp.sum(lax.all_to_all(partial, 'tiles', 0, 0, tiled=False), axis=0)  13.3 us
    pallas_call x1, Pallas kernels, tile_products(): pl.pallas_call(tile_kernel, grid_spec=grid_spec, out_shape=jax.ShapeDtype...  11.4 us
    all_to_all x1, waiting for transfers between devices, body(): lax.all_to_all(spread, 'tiles', 0, 0, tiled=False)  10.5 us
    all_to_all x1, starting transfers between devices, body(): owned = jnp.sum(lax.all_to_all(partial, 'tiles', 0, 0, tiled=False), axis=0)  7.38 us
    all_to_all x1, starting transfers between devices, body(): matrix = jnp.sum(lax.all_to_all(terms, 'tiles', 0, 0, tiled=False), axis=0)  4.11 us
    all_to_all x1, starting transfers between devices, body(): lax.all_to_all(spread, 'tiles', 0, 0, tiled=False)  4.1 us
  transfers between devices with their start and end apart: 3, of which 3 were waited for; matrix products, arithmetic and copies ran while one was open for 5% of the time, Pallas kernels for 0%

profile of v5, /device:TPU:0, one launch (start us, length us, event | category | flops | bytes accessed | tf_op | source)
XLA Modules:
  0.0 115.6 jit_solution(4336705183214879360)
XLA Ops:
  0.6 0.8 copy.20
  1.4 0.7 compare_select_fusion.5
  2.1 0.7 scatter_custom_fusion.1
  3.9 1.5 %copy.21.refs_8_ = f32[256,1]{1,0:T(8,128)} copy(f32[256,1]{0,1:T(1,128)} %bitcast.33) | data formatting | bytes 2048 | tf_op jit(solution)/shard_map/reshape | solution.py:56
  5.4 11.4 %shard_map.104 = f32[32,64,64]{2,1,0:T(8,128)} custom-call(s32[64]{0:T(128)} %reshape.90.pairs_ref, f32[256,16384]{1,0:T(8,128)} %refs_7_.1, f32[256,16384]{1,0:T(8,128)} %refs_7_.1, f32[256,16384]{1,0:T(8,128)} %refs_7_.1, f32[256,16384]{1,0:T(8,128)} %refs_7_.1, f32[256,16384]{1,0:T(8,128)} %refs_7_.1, f32[256,16384]{1,0:T(8,128)} %refs_7_.1, ...), custom_call_target="tpu_custom_call" | custom-call | tf_op jit(solution)/shard_map/pallas_call | solution.py:52
  16.9 2.6 %reshape.92 = f32[16,2,4096]{2,1,0:T(2,128)} reshape(f32[32,64,64]{2,1,0:T(8,128)} %shard_map.104) | data formatting | bytes 1048576 | tf_op jit(solution)/shard_map/reshape | solution.py:142
  19.5 7.4 %all-to-all-start = ((f32[16,2,4096]{2,1,0:T(2,128)}), f32[16,2,4096]{2,1,0:T(2,128)S(1)}, u32[]{:S(2)}, u32[]{:S(2)}) async-start(f32[16,2,4096]{2,1,0:T(2,128)} %reshape.92), calls=%async_computation | async-start | bytes 1048576 | tf_op jit(solution)/shard_map/all_to_all | solution.py:143
  27.0 1.0 scatter_custom_fusion
  28.1 13.3 %all-to-all-done = f32[16,2,4096]{2,1,0:T(2,128)S(1)} async-done(((f32[16,2,4096]{2,1,0:T(2,128)}), f32[16,2,4096]{2,1,0:T(2,128)S(1)}, u32[]{:S(2)}, u32[]{:S(2)}) %all-to-all-start) | async-done | bytes 524320 | tf_op jit(solution)/shard_map/all_to_all | solution.py:143
  41.5 1.0 broadcast_in_dim.95
  42.5 4.1 %all-to-all-start.1 = ((f32[16,2,4096]{2,1,0:T(2,128)}), f32[16,2,4096]{2,1,0:T(2,128)S(1)}, u32[]{:S(2)}, u32[]{:S(2)}) async-start(f32[16,2,4096]{2,1,0:T(2,128)} %broadcast_in_dim.95), calls=%async_computation.1 | async-start | bytes 1048576 | tf_op jit(solution)/shard_map/all_to_all | solution.py:145
  47.2 1.0 sort.15
  50.5 10.5 %all-to-all-done.1 = f32[16,2,4096]{2,1,0:T(2,128)S(1)} async-done(((f32[16,2,4096]{2,1,0:T(2,128)}), f32[16,2,4096]{2,1,0:T(2,128)S(1)}, u32[]{:S(2)}, u32[]{:S(2)}) %all-to-all-start.1) | async-done | bytes 524320 | tf_op jit(solution)/shard_map/all_to_all | solution.py:145
  62.1 2.4 %scatter_fusion = f32[8,64,8,64]{3,1,2,0:T(8,128)S(1)} fusion(f32[8,64,8,64]{3,1,2,0:T(8,128)S(1)} %broadcast_in_dim.88, s32[32]{0:T(128)S(1)} %get-tuple-element.16, f32[32,64,64]{2,1,0:T(8,128)S(1)} %broadcast_select_fusion), kind=kCustom, calls=%fused_computation.5 | custom fusion | flops 131072 | bytes 1573120 | tf_op jit(solution)/shard_map/scatter-add | solution.py:164
  64.5 2.5 %copy.22 = f32[8,64,8,64]{3,2,1,0:T(8,128)} copy(f32[8,64,8,64]{3,1,2,0:T(8,128)S(1)} %scatter_fusion) | data formatting | bytes 2097152 | tf_op jit(solution)/shard_map/scatter-add | solution.py:164
  67.0 2.7 %reshape.94.dense_ref = f32[512,512]{1,0:T(8,128)} reshape(f32[8,64,8,64]{3,2,1,0:T(8,128)} %copy.22) | data formatting | bytes 2097152 | tf_op jit(solution)/shard_map/reshape | solution.py:165
  69.7 19.4 %shard_map.105 = (f32[8,1,256]{2,1,0:T(1,128)}, f32[512,512]{1,0:T(8,128)}) custom-call(s32[64]{0:T(128)} %reshape.89.source_ref, f32[8,512,256]{2,1,0:T(8,128)} %table_ref.1, f32[512,512]{1,0:T(8,128)} %reshape.94.dense_ref, f32[8,1,256]{2,1,0:T(1,128)} %reshape.95.weight_ref, f32[8,1,256]{2,1,0:T(1,128)} %reshape.96.base_ref), custom_call_target="tpu_custom_call" | custom-call | tf_op jit(solution)/shard_map/pallas_call | solution.py:110
  89.1 1.6 %reshape.98 = f32[8,64,8,64]{3,2,1,0:T(8,128)S(1)} reshape(f32[512,512]{1,0:T(8,128)} %get-tuple-element.8) | data formatting | bytes 2097152 | tf_op jit(solution)/shard_map/reshape | solution.py:168
  90.6 1.7 %copy.23 = f32[8,64,8,64]{3,1,2,0:T(8,128)} copy(f32[8,64,8,64]{3,2,1,0:T(8,128)S(1)} %reshape.98) | data formatting | bytes 2097152 | tf_op jit(solution)/shard_map/reshape | solution.py:168
  92.4 2.2 %gather_fusion.2 = f32[32,64,64]{2,1,0:T(8,128)S(1)} fusion(f32[8,64,8,64]{3,1,2,0:T(8,128)} %copy.23, s32[32]{0:T(128)S(1)} %get-tuple-element.15), kind=kCustom, calls=%fused_computation.2 | custom fusion | bytes 1048832 | tf_op jit(solution)/shard_map/gather | solution.py:169
  95.1 1.1 broadcast_select_fusion.1
  96.3 4.1 %all-to-all-start.2 = ((f32[16,2,4096]{2,1,0:T(2,128)}), f32[16,2,4096]{2,1,0:T(2,128)S(1)}, u32[]{:S(2)}, u32[]{:S(2)}) async-start(f32[16,2,4096]{2,1,0:T(2,128)} %broadcast_select_fusion.1), calls=%async_computation.2 | async-start | bytes 1048576 | tf_op jit(solution)/shard_map/all_to_all | solution.py:173
  101.0 13.9 %all-to-all-done.2 = f32[16,2,4096]{2,1,0:T(2,128)S(1)} async-done(((f32[16,2,4096]{2,1,0:T(2,128)}), f32[16,2,4096]{2,1,0:T(2,128)S(1)}, u32[]{:S(2)}, u32[]{:S(2)}) %all-to-all-start.2) | async-done | bytes 524320 | tf_op jit(solution)/shard_map/all_to_all | solution.py:173
  114.8 0.8 reduce_sum.55
  (39 shorter events, 6.6 us)
Async XLA Ops:
  16.8 10.0 %copy-start.3 = (s32[128,8]{0,1:T(8,128)S(1)}, s32[128,8]{0,1:T(8,128)}, u32[]{:S(2)}) copy-start(s32[128,8]{0,1:T(8,128)} %param.13) | copy-start | bytes 12292
  16.8 10.1 %copy-start.4 = (s32[128]{0:T(128)S(1)}, s32[128]{0:T(128)}, u32[]{:S(2)}) copy-start(s32[128]{0:T(128)} %param.14) | copy-start | bytes 1540
  16.8 32.0 %copy-start = (f32[8,256]{1,0:T(8,128)S(1)}, f32[8,256]{1,0:T(8,128)}, u32[]{:S(2)}) copy-start(f32[8,256]{1,0:T(8,128)} %param.16) | copy-start | bytes 24580
  16.9 32.6 %copy-start.1 = (f32[8,256]{1,0:T(8,128)S(1)}, f32[8,256]{1,0:T(8,128)}, u32[]{:S(2)}) copy-start(f32[8,256]{1,0:T(8,128)} %param.17) | copy-start | bytes 24580
  19.5 21.9 %all-to-all-start = ((f32[16,2,4096]{2,1,0:T(2,128)}), f32[16,2,4096]{2,1,0:T(2,128)S(1)}, u32[]{:S(2)}, u32[]{:S(2)}) async-start(f32[16,2,4096]{2,1,0:T(2,128)} %reshape.92), calls=%async_computation | async-start | bytes 1048576 | tf_op jit(solution)/shard_map/all_to_all | solution.py:143
  42.5 18.6 %all-to-all-start.1 = ((f32[16,2,4096]{2,1,0:T(2,128)}), f32[16,2,4096]{2,1,0:T(2,128)S(1)}, u32[]{:S(2)}, u32[]{:S(2)}) async-start(f32[16,2,4096]{2,1,0:T(2,128)} %broadcast_in_dim.95), calls=%async_computation.1 | async-start | bytes 1048576 | tf_op jit(solution)/shard_map/all_to_all | solution.py:145
  94.6 5.8 %copy-start.2 = (f32[8,1,256]{2,1,0:T(1,128)S(1)}, f32[8,1,256]{2,1,0:T(1,128)}, u32[]{:S(2)}) copy-start(f32[8,1,256]{2,1,0:T(1,128)} %get-tuple-element.7) | copy-start | bytes 24580
  96.3 18.6 %all-to-all-start.2 = ((f32[16,2,4096]{2,1,0:T(2,128)}), f32[16,2,4096]{2,1,0:T(2,128)S(1)}, u32[]{:S(2)}, u32[]{:S(2)}) async-start(f32[16,2,4096]{2,1,0:T(2,128)} %broadcast_select_fusion.1), calls=%async_computation.2 | async-start | bytes 1048576 | tf_op jit(solution)/shard_map/all_to_all | solution.py:173

commit v6 on v5

--- a/solution.py
+++ b/solution.py
@@ -34,7 +34,7 @@
 def tile_products(coeffs, occupation, pairs):
     state_count = coeffs.shape[0]
     kept_count = pairs.shape[0]
-    group = next(g for g in (4, 2, 1) if kept_count % g == 0)
+    group = next(g for g in (8, 4, 2, 1) if kept_count % g == 0)
 
     def block_of(i, side):
         return pl.BlockSpec(
@@ -68,13 +68,35 @@
     return one(left_hi, right_hi) + (one(left_hi, right_lo) + one(left_lo, right_hi))
 
 
-def batch_kernel(source_ref, table_ref, dense_ref, weight_ref, base_ref, density_ref, matrix_ref, canon_ref):
+def batch_kernel(
+    source_ref, pick_ref, table_ref, tile_ref, weight_ref, base_ref,
+    density_ref, pair_ref, canon_ref, dense_hi_ref, dense_lo_ref, acc_ref,
+):
     b = pl.program_id(0)
+
+    @pl.when(b == 0)
+    def _():
+        for q1 in range(OV):
+            for q2 in range(OV):
+                which = pick_ref[q1 * OV + q2]
+                tile = jnp.where(which >= 0, tile_ref[jnp.maximum(which, 0)], 0.0)
+                tile_hi = tile.astype(jnp.bfloat16)
+                tile_lo = (tile - tile_hi.astype(jnp.float32)).astype(jnp.bfloat16)
+                dense_hi_ref[q1 * BS:(q1 + 1) * BS, q2 * BS:(q2 + 1) * BS] = tile_hi
+                dense_lo_ref[q1 * BS:(q1 + 1) * BS, q2 * BS:(q2 + 1) * BS] = tile_lo
+
     for q in range(OV):
         start = pl.multiple_of(source_ref[b * OV + q] * BS, BS)
         canon_ref[q * BS:(q + 1) * BS, :] = table_ref[0, pl.ds(start, BS), :]
     grid = canon_ref[...]
-    mixed = split_dot(dense_ref[...], grid, ((1,), (0,)))
+    grid_hi = grid.astype(jnp.bfloat16)
+    grid_lo = (grid - grid_hi.astype(jnp.float32)).astype(jnp.bfloat16)
+
+    def nn(a, c):
+        return lax.dot_general(a, c, (((1,), (0,)), ((), ())), preferred_element_type=jnp.float32)
+
+    dense_hi = dense_hi_ref[...]
+    mixed = nn(dense_hi, grid_hi) + (nn(dense_hi, grid_lo) + nn(dense_lo_ref[...], grid_hi))
     density = jnp.sum(grid * mixed, axis=0, keepdims=True)
     potential = base_ref[0] + density - density * density * density / 6.0
     density_ref[0] = density
@@ -83,45 +105,58 @@
 
     @pl.when(b == 0)
     def _():
-        matrix_ref[...] = terms
+        acc_ref[...] = terms
 
     @pl.when(b > 0)
     def _():
-        matrix_ref[...] += terms
-
-
-def batch_terms(source, tables, dense, weights, local_pot):
+        acc_ref[...] += terms
+
+    @pl.when(b == pl.num_programs(0) - 1)
+    def _():
+        for q1 in range(OV):
+            for q2 in range(OV):
+                pair_ref[q1 * OV + q2] = acc_ref[q1 * BS:(q1 + 1) * BS, q2 * BS:(q2 + 1) * BS]
+
+
+def batch_terms(source, pick, tables, tile_values, weights, local_pot):
     batch_count, rows, points = tables.shape
+    kept_count = tile_values.shape[0]
     grid_spec = pltpu.PrefetchScalarGridSpec(
-        num_scalar_prefetch=1,
+        num_scalar_prefetch=2,
         grid=(batch_count,),
         in_specs=[
-            pl.BlockSpec((1, rows, points), lambda b, s: (b, 0, 0)),
-            pl.BlockSpec((rows, rows), lambda b, s: (0, 0)),
-            pl.BlockSpec((1, 1, points), lambda b, s: (b, 0, 0)),
-            pl.BlockSpec((1, 1, points), lambda b, s: (b, 0, 0)),
+            pl.BlockSpec((1, rows, points), lambda b, s, k: (b, 0, 0)),
+            pl.BlockSpec((kept_count, BS, BS), lambda b, s, k: (0, 0, 0)),
+            pl.BlockSpec((1, 1, points), lambda b, s, k: (b, 0, 0)),
+            pl.BlockSpec((1, 1, points), lambda b, s, k: (b, 0, 0)),
         ],
         out_specs=[
-            pl.BlockSpec((1, 1, points), lambda b, s: (b, 0, 0)),
-            pl.BlockSpec((rows, rows), lambda b, s: (0, 0)),
-        ],
-        scratch_shapes=[pltpu.VMEM((rows, points), jnp.float32)],
-    )
-    density, matrix = pl.pallas_call(
+            pl.BlockSpec((1, 1, points), lambda b, s, k: (b, 0, 0)),
+            pl.BlockSpec((OV * OV, BS, BS), lambda b, s, k: (0, 0, 0)),
+        ],
+        scratch_shapes=[
+            pltpu.VMEM((rows, points), jnp.float32),
+            pltpu.VMEM((rows, rows), jnp.bfloat16),
+            pltpu.VMEM((rows, rows), jnp.bfloat16),
+            pltpu.VMEM((rows, rows), jnp.float32),
+        ],
+    )
+    density, pair_tiles = pl.pallas_call(
         batch_kernel,
         grid_spec=grid_spec,
         out_shape=[
             jax.ShapeDtypeStruct((batch_count, 1, points), jnp.float32),
-            jax.ShapeDtypeStruct((rows, rows), jnp.float32),
+            jax.ShapeDtypeStruct((OV * OV, BS, BS), jnp.float32),
         ],
     )(
         source.reshape(-1),
+        pick,
         tables,
-        dense,
+        tile_values,
         weights.reshape(batch_count, 1, points),
         local_pot.reshape(batch_count, 1, points),
     )
-    return density.reshape(batch_count, points), matrix
+    return density.reshape(batch_count, points), pair_tiles
 
 
 def body(coeffs, occupation, kept_tiles, tile_slot, blocks, batch_slot, tables, weights, local_pot):
@@ -139,10 +174,10 @@
     ladder_kept = jnp.arange(kept_count, dtype=jnp.int32)
     slot_kept = jnp.zeros((kept_count,), jnp.int32).at[tile_slot].set(ladder_kept)
     pairs = kept_tiles[slot_kept]
-    partial = tile_products(coeffs, occupation, pairs).reshape(devices, owned_count, BS * BS)
+    partial = tile_products(coeffs, occupation, pairs).reshape(devices, owned_count, BS, BS)
     owned = jnp.sum(lax.all_to_all(partial, "tiles", 0, 0, tiled=False), axis=0)
-    spread = jnp.broadcast_to(owned[None], (devices, owned_count, BS * BS))
-    tile_values = lax.all_to_all(spread, "tiles", 0, 0, tiled=False).reshape(kept_count, BS * BS)
+    spread = jnp.broadcast_to(owned[None], (devices, owned_count, BS, BS))
+    tile_values = lax.all_to_all(spread, "tiles", 0, 0, tiled=False).reshape(kept_count, BS, BS)
 
     ladder_batch = jnp.arange(batch_total, dtype=jnp.int32)
     slot_batch = jnp.zeros((batch_total,), jnp.int32).at[batch_slot].set(ladder_batch)
@@ -157,20 +192,18 @@
     present = jnp.any(row_hit, axis=1) & jnp.any(col_hit, axis=1)
     row_place = jnp.sum(jnp.where(row_hit, ladder_ov[None, :], 0), axis=1)
     col_place = jnp.sum(jnp.where(col_hit, ladder_ov[None, :], 0), axis=1)
-    kept_values = jnp.where(present[:, None], tile_values, 0.0).reshape(kept_count, BS, BS)
-    dense = (
-        jnp.zeros((OV, BS, OV, BS), jnp.float32)
-        .at[row_place, :, col_place, :]
-        .add(kept_values)
-        .reshape(width, width)
-    )
-    density, full_matrix = batch_terms(source, tables, dense, weights, local_pot)
-    full_matrix = full_matrix.reshape(OV, BS, OV, BS)
-    picked = full_matrix[row_place, :, col_place, :].reshape(kept_count, BS * BS)
-    contrib = jnp.where(present[:, None], picked, 0.0)
-
-    terms = contrib.reshape(devices, owned_count, BS * BS)
+    pair_code = row_place * OV + col_place
+    ladder_pair = jnp.arange(OV * OV, dtype=jnp.int32)
+    at_pair = present[None, :] & (pair_code[None, :] == ladder_pair[:, None])
+    pick = jnp.where(
+        jnp.any(at_pair, axis=1), jnp.sum(jnp.where(at_pair, ladder_kept[None, :], 0), axis=1), -1
+    )
+    density, pair_tiles = batch_terms(source, pick, tables, tile_values, weights, local_pot)
+    contrib = jnp.where(present[:, None, None], pair_tiles[pair_code], 0.0)
+
+    terms = contrib.reshape(devices, owned_count, BS, BS)
     matrix = jnp.sum(lax.all_to_all(terms, "tiles", 0, 0, tiled=False), axis=0)
+    matrix = matrix.reshape(owned_count, BS * BS)
     return (density, matrix)
 
 

time: 116 us -> 113 us (0.974)
  local copies, waits for them, and re-layouts: 24.2 us -> 19.9 us
  other arithmetic: 6.57 us -> 8.61 us
    reshape x6 -> x1, local copies, waits for them, and re-layouts: 9.73 us -> 0.71 us  [body(): matrix = matrix.reshape(owned_count, BS * BS)]
    unnamed x13 -> x19, local copies, waits for them, and re-layouts: 1.49 us -> 9.29 us
    all_to_all x0 -> x3, other arithmetic: none -> 5.58 us  [the longest x1 1.86 us: body(): lax.all_to_all(spread, 'tiles', 0, 0, tiled=False)]
    all_to_all x1, waiting for transfers between devices: 13.3 us -> 9.56 us  [body(): owned = jnp.sum(lax.all_to_all(partial, 'tiles', 0, 0, tiled=False), axis=0)]
    all_to_all x1, waiting for transfers between devices: 10.5 us -> 13.4 us  [body(): lax.all_to_all(spread, 'tiles', 0, 0, tiled=False)]
    scatter-add x1 -> x0, local copies, waits for them, and re-layouts: 2.55 us -> none  [body(): dense = jnp.zeros((OV, BS, OV, BS), jnp.float32).at[row_place, :, col_pla...]
    scatter-add x1 -> x0, other arithmetic: 2.39 us -> none  [body(): dense = jnp.zeros((OV, BS, OV, BS), jnp.float32).at[row_place, :, col_pla...]
    pallas_call x1, Pallas kernels: 19.4 us -> 20.7 us  [batch_terms(): pl.pallas_call(batch_kernel, grid_spec=grid_spec, out_shape=[jax.ShapeDty...]
  transfers between devices with their start and end apart: 3 -> 3, of which waited for: 3 -> 3; matrix products, arithmetic and copies ran while one was open for 5% -> 6% of each run, Pallas kernels for 0% -> 0%
where the time goes in v6:
time: 113 us
  waiting for transfers between devices  36.9 us (33%)
  Pallas kernels  30.8 us (27%)
  local copies, waits for them, and re-layouts  19.9 us (18%)
  starting transfers between devices  15.6 us (14%)
  other arithmetic  8.61 us (8%)
    pallas_call x1, Pallas kernels, batch_terms(): pl.pallas_call(batch_kernel, grid_spec=grid_spec, out_shape=[jax.ShapeDty...  20.7 us
    all_to_all x1, waiting for transfers between devices, body(): matrix = jnp.sum(lax.all_to_all(terms, 'tiles', 0, 0, tiled=False), axis=0)  13.9 us
    all_to_all x1, waiting for transfers between devices, body(): lax.all_to_all(spread, 'tiles', 0, 0, tiled=False)  13.4 us
    pallas_call x1, Pallas kernels, tile_products(): pl.pallas_call(tile_kernel, grid_spec=grid_spec, out_shape=jax.ShapeDtype...  10.1 us
    all_to_all x1, waiting for transfers between devices, body(): owned = jnp.sum(lax.all_to_all(partial, 'tiles', 0, 0, tiled=False), axis=0)  9.56 us
    unnamed x19, local copies, waits for them, and re-layouts  9.29 us
    all_to_all x1, starting transfers between devices, body(): owned = jnp.sum(lax.all_to_all(partial, 'tiles', 0, 0, tiled=False), axis=0)  7.39 us
    all_to_all x1, starting transfers between devices, body(): matrix = jnp.sum(lax.all_to_all(terms, 'tiles', 0, 0, tiled=False), axis=0)  4.1 us
  transfers between devices with their start and end apart: 3, of which 3 were waited for; matrix products, arithmetic and copies ran while one was open for 6% of the time, Pallas kernels for 0%

profile of v6, /device:TPU:0, one launch (start us, length us, event | category | flops | bytes accessed | tf_op | source)
XLA Modules:
  0.0 112.6 jit_solution(1096290053482614847)
XLA Ops:
  0.6 0.8 copy.17
  1.4 0.7 compare_select_fusion.4
  2.1 0.7 scatter_custom_fusion.1
  3.9 1.5 %copy.18.refs_16_ = f32[256,1]{1,0:T(8,128)} copy(f32[256,1]{0,1:T(1,128)} %bitcast.17) | data formatting | bytes 2048 | tf_op jit(solution)/shard_map/reshape | solution.py:56
  5.4 10.1 %shard_map.104 = f32[32,64,64]{2,1,0:T(8,128)} custom-call(s32[64]{0:T(128)} %reshape.85.pairs_ref, f32[256,16384]{1,0:T(8,128)} %refs_15_.1, f32[256,16384]{1,0:T(8,128)} %refs_15_.1, f32[256,16384]{1,0:T(8,128)} %refs_15_.1, f32[256,16384]{1,0:T(8,128)} %refs_15_.1, f32[256,16384]{1,0:T(8,128)} %refs_15_.1, f32[256,16384]{1,0:T(8,128)} %refs_15_.1, ...), custom_call_target="tpu_custom_call" | custom-call | tf_op jit(solution)/shard_map/pallas_call | solution.py:52
  15.5 2.7 %reshape.143 = f32[16,1,8192]{2,1,0:T(1,128)} reshape(f32[16,2,64,64]{3,2,1,0:T(8,128)} %bitcast.13) | data formatting | bytes 1048576
  18.2 7.4 %all-to-all-start = ((f32[16,1,8192]{2,1,0:T(1,128)}), f32[16,1,8192]{2,1,0:T(1,128)S(1)}, u32[]{:S(2)}, u32[]{:S(2)}) async-start(f32[16,1,8192]{2,1,0:T(1,128)} %reshape.143), calls=%async_computation | async-start | bytes 1048576 | tf_op jit(solution)/shard_map/all_to_all | solution.py:178
  25.7 1.0 scatter_custom_fusion
  27.4 1.0 sort.15
  28.4 0.7 reshape.84.source_ref
  30.5 9.6 %all-to-all-done = f32[16,1,8192]{2,1,0:T(1,128)S(1)} async-done(((f32[16,1,8192]{2,1,0:T(1,128)}), f32[16,1,8192]{2,1,0:T(1,128)S(1)}, u32[]{:S(2)}, u32[]{:S(2)}) %all-to-all-start) | async-done | bytes 524320 | tf_op jit(solution)/shard_map/all_to_all | solution.py:178
  40.6 1.9 %reduce.4 = f32[16,8192]{1,0:T(8,128)S(1)} reduce(f32[16,1,8192]{2,1,0:T(1,128)S(1)} %all-to-all-done, f32[]{:T(128)} %broadcast.82), dimensions={1}, to_apply=%all_to_all.9.reduce_sub_computation | reduce | bytes 1048580 | tf_op jit(solution)/shard_map/all_to_all | solution.py:178
  43.1 1.4 %reshape.145 = f32[16,1,8192]{2,1,0:T(1,128)} reshape(f32[16,2,64,64]{3,2,1,0:T(8,128)S(1)} %broadcast_in_dim.101) | data formatting | bytes 1048576
  44.5 4.1 %all-to-all-start.1 = ((f32[16,1,8192]{2,1,0:T(1,128)}), f32[16,1,8192]{2,1,0:T(1,128)S(1)}, u32[]{:S(2)}, u32[]{:S(2)}) async-start(f32[16,1,8192]{2,1,0:T(1,128)} %reshape.145), calls=%async_computation.1 | async-start | bytes 1048576 | tf_op jit(solution)/shard_map/all_to_all | solution.py:180
  49.6 13.4 %all-to-all-done.1 = f32[16,1,8192]{2,1,0:T(1,128)S(1)} async-done(((f32[16,1,8192]{2,1,0:T(1,128)}), f32[16,1,8192]{2,1,0:T(1,128)S(1)}, u32[]{:S(2)}, u32[]{:S(2)}) %all-to-all-start.1) | async-done | bytes 524320 | tf_op jit(solution)/shard_map/all_to_all | solution.py:180
  63.1 1.9 %reduce.5 = f32[16,8192]{1,0:T(8,128)S(1)} reduce(f32[16,1,8192]{2,1,0:T(1,128)S(1)} %all-to-all-done.1, f32[]{:T(128)} %broadcast.82), dimensions={1}, to_apply=%all_to_all.10.reduce_sub_computation | reduce | bytes 1048580 | tf_op jit(solution)/shard_map/all_to_all | solution.py:180
  64.9 1.4 %reshape.146 = f32[16,2,64,64]{3,2,1,0:T(8,128)} reshape(f32[16,8192]{1,0:T(8,128)S(1)} %reduce.5) | data formatting | bytes 1048576
  66.3 20.7 %shard_map.105 = (f32[8,1,256]{2,1,0:T(1,128)}, f32[64,64,64]{2,1,0:T(8,128)}) custom-call(s32[64]{0:T(128)} %reshape.84.source_ref, s32[64]{0:T(128)} %broadcast_select_fusion.1.pick_ref, f32[8,512,256]{2,1,0:T(8,128)} %table_ref.1, f32[32,64,64]{2,1,0:T(8,128)} %bitcast.15, f32[8,1,256]{2,1,0:T(1,128)} %reshape.89.weight_ref, f32[8,1,256]{2,1,0:T(1,128)} %reshape.90.base_ref), custom_call_target="tpu_custom_call" | custom-call | tf_op jit(solution)/shard_map/pallas_call | solution.py:144
  87.1 2.2 %gather_fusion.2 = f32[32,64,64]{2,1,0:T(8,128)S(1)} fusion(f32[64,64,64]{2,1,0:T(8,128)} %get-tuple-element.8, s32[1024]{0:T(1024)S(1)} %pad_clamp_fusion), kind=kCustom, calls=%fused_computation.2 | custom fusion | bytes 1048704 | tf_op jit(solution)/shard_map/gather | solution.py:202
  89.5 1.4 %reshape.147 = f32[16,1,8192]{2,1,0:T(1,128)} reshape(f32[16,2,64,64]{3,2,1,0:T(8,128)S(1)} %broadcast_select_fusion) | data formatting | bytes 1048576
  90.9 4.1 %all-to-all-start.2 = ((f32[16,1,8192]{2,1,0:T(1,128)}), f32[16,1,8192]{2,1,0:T(1,128)S(1)}, u32[]{:S(2)}, u32[]{:S(2)}) async-start(f32[16,1,8192]{2,1,0:T(1,128)} %reshape.147), calls=%async_computation.2 | async-start | bytes 1048576 | tf_op jit(solution)/shard_map/all_to_all | solution.py:205
  95.6 13.9 %all-to-all-done.2 = f32[16,1,8192]{2,1,0:T(1,128)S(1)} async-done(((f32[16,1,8192]{2,1,0:T(1,128)}), f32[16,1,8192]{2,1,0:T(1,128)S(1)}, u32[]{:S(2)}, u32[]{:S(2)}) %all-to-all-start.2) | async-done | bytes 524320 | tf_op jit(solution)/shard_map/all_to_all | solution.py:205
  109.5 1.9 %reduce.6 = f32[16,8192]{1,0:T(8,128)S(1)} reduce(f32[16,1,8192]{2,1,0:T(1,128)S(1)} %all-to-all-done.2, f32[]{:T(128)} %broadcast.82), dimensions={1}, to_apply=%all_to_all.11.reduce_sub_computation | reduce | bytes 1048580 | tf_op jit(solution)/shard_map/all_to_all | solution.py:205
  111.8 0.7 reshape.92
  (44 shorter events, 6.8 us)
Async XLA Ops:
  5.4 20.2 %copy-start.3 = (s32[128,8]{0,1:T(8,128)S(1)}, s32[128,8]{0,1:T(8,128)}, u32[]{:S(2)}) copy-start(s32[128,8]{0,1:T(8,128)} %param.13) | copy-start | bytes 12292
  5.4 20.3 %copy-start.4 = (s32[128]{0:T(128)S(1)}, s32[128]{0:T(128)}, u32[]{:S(2)}) copy-start(s32[128]{0:T(128)} %param.14) | copy-start | bytes 1540
  5.4 23.7 %copy-start = (f32[8,256]{1,0:T(8,128)S(1)}, f32[8,256]{1,0:T(8,128)}, u32[]{:S(2)}) copy-start(f32[8,256]{1,0:T(8,128)} %param.16) | copy-start | bytes 24580
  5.4 24.3 %copy-start.1 = (f32[8,256]{1,0:T(8,128)S(1)}, f32[8,256]{1,0:T(8,128)}, u32[]{:S(2)}) copy-start(f32[8,256]{1,0:T(8,128)} %param.17) | copy-start | bytes 24580
  18.2 21.9 %all-to-all-start = ((f32[16,1,8192]{2,1,0:T(1,128)}), f32[16,1,8192]{2,1,0:T(1,128)S(1)}, u32[]{:S(2)}, u32[]{:S(2)}) async-start(f32[16,1,8192]{2,1,0:T(1,128)} %reshape.143), calls=%async_computation | async-start | bytes 1048576 | tf_op jit(solution)/shard_map/all_to_all | solution.py:178
  44.5 18.6 %all-to-all-start.1 = ((f32[16,1,8192]{2,1,0:T(1,128)}), f32[16,1,8192]{2,1,0:T(1,128)S(1)}, u32[]{:S(2)}, u32[]{:S(2)}) async-start(f32[16,1,8192]{2,1,0:T(1,128)} %reshape.145), calls=%async_computation.1 | async-start | bytes 1048576 | tf_op jit(solution)/shard_map/all_to_all | solution.py:180
  87.1 7.9 %copy-start.2 = (f32[8,1,256]{2,1,0:T(1,128)S(1)}, f32[8,1,256]{2,1,0:T(1,128)}, u32[]{:S(2)}) copy-start(f32[8,1,256]{2,1,0:T(1,128)} %get-tuple-element.7) | copy-start | bytes 24580
  90.9 18.6 %all-to-all-start.2 = ((f32[16,1,8192]{2,1,0:T(1,128)}), f32[16,1,8192]{2,1,0:T(1,128)S(1)}, u32[]{:S(2)}, u32[]{:S(2)}) async-start(f32[16,1,8192]{2,1,0:T(1,128)} %reshape.147), calls=%async_computation.2 | async-start | bytes 1048576 | tf_op jit(solution)/shard_map/all_to_all | solution.py:205

commit v7 on v6

--- a/solution.py
+++ b/solution.py
@@ -69,25 +69,40 @@
 
 
 def batch_kernel(
-    source_ref, pick_ref, table_ref, tile_ref, weight_ref, base_ref,
-    density_ref, pair_ref, canon_ref, dense_hi_ref, dense_lo_ref, acc_ref,
+    source_ref, pick_ref, table_hbm, tile_hbm, weight_ref, base_ref,
+    density_ref, pair_ref, canon_ref, stage_ref, dense_hi_ref, dense_lo_ref, table_sems, tile_sems,
 ):
-    b = pl.program_id(0)
-
-    @pl.when(b == 0)
-    def _():
-        for q1 in range(OV):
-            for q2 in range(OV):
-                which = pick_ref[q1 * OV + q2]
-                tile = jnp.where(which >= 0, tile_ref[jnp.maximum(which, 0)], 0.0)
-                tile_hi = tile.astype(jnp.bfloat16)
-                tile_lo = (tile - tile_hi.astype(jnp.float32)).astype(jnp.bfloat16)
-                dense_hi_ref[q1 * BS:(q1 + 1) * BS, q2 * BS:(q2 + 1) * BS] = tile_hi
-                dense_lo_ref[q1 * BS:(q1 + 1) * BS, q2 * BS:(q2 + 1) * BS] = tile_lo
-
-    for q in range(OV):
-        start = pl.multiple_of(source_ref[b * OV + q] * BS, BS)
-        canon_ref[q * BS:(q + 1) * BS, :] = table_ref[0, pl.ds(start, BS), :]
+    batch_count, _, points = table_hbm.shape
+    copies = []
+    for b in range(batch_count):
+        for q in range(OV):
+            start = pl.multiple_of(source_ref[b * OV + q] * BS, BS)
+            copy = pltpu.make_async_copy(
+                table_hbm.at[b, pl.ds(start, BS), :],
+                canon_ref.at[q * BS:(q + 1) * BS, b * points:(b + 1) * points],
+                table_sems.at[b * OV + q],
+            )
+            copy.start()
+            copies.append(copy)
+    for p in range(OV * OV):
+        copy = pltpu.make_async_copy(
+            tile_hbm.at[jnp.maximum(pick_ref[p], 0)], stage_ref.at[p], tile_sems.at[p]
+        )
+        copy.start()
+        copies.append(copy)
+    for copy in copies[batch_count * OV:]:
+        copy.wait()
+    for q1 in range(OV):
+        for q2 in range(OV):
+            p = q1 * OV + q2
+            tile = jnp.where(pick_ref[p] >= 0, stage_ref[p], 0.0)
+            tile_hi = tile.astype(jnp.bfloat16)
+            tile_lo = (tile - tile_hi.astype(jnp.float32)).astype(jnp.bfloat16)
+            dense_hi_ref[q1 * BS:(q1 + 1) * BS, q2 * BS:(q2 + 1) * BS] = tile_hi
+            dense_lo_ref[q1 * BS:(q1 + 1) * BS, q2 * BS:(q2 + 1) * BS] = tile_lo
+    for copy in copies[:batch_count * OV]:
+        copy.wait()
+
     grid = canon_ref[...]
     grid_hi = grid.astype(jnp.bfloat16)
     grid_lo = (grid - grid_hi.astype(jnp.float32)).astype(jnp.bfloat16)
@@ -98,54 +113,46 @@
     dense_hi = dense_hi_ref[...]
     mixed = nn(dense_hi, grid_hi) + (nn(dense_hi, grid_lo) + nn(dense_lo_ref[...], grid_hi))
     density = jnp.sum(grid * mixed, axis=0, keepdims=True)
-    potential = base_ref[0] + density - density * density * density / 6.0
-    density_ref[0] = density
-    weighted = grid * (weight_ref[0] * potential)
+    potential = base_ref[...] + density - density * density * density / 6.0
+    density_ref[...] = density
+    weighted = grid * (weight_ref[...] * potential)
     terms = split_dot(weighted, grid, ((1,), (1,)))
-
-    @pl.when(b == 0)
-    def _():
-        acc_ref[...] = terms
-
-    @pl.when(b > 0)
-    def _():
-        acc_ref[...] += terms
-
-    @pl.when(b == pl.num_programs(0) - 1)
-    def _():
-        for q1 in range(OV):
-            for q2 in range(OV):
-                pair_ref[q1 * OV + q2] = acc_ref[q1 * BS:(q1 + 1) * BS, q2 * BS:(q2 + 1) * BS]
+    for q1 in range(OV):
+        for q2 in range(OV):
+            pair_ref[q1 * OV + q2] = terms[q1 * BS:(q1 + 1) * BS, q2 * BS:(q2 + 1) * BS]
 
 
 def batch_terms(source, pick, tables, tile_values, weights, local_pot):
     batch_count, rows, points = tables.shape
-    kept_count = tile_values.shape[0]
+    span = batch_count * points
+    whole = lambda i, s, k: (0, 0)
     grid_spec = pltpu.PrefetchScalarGridSpec(
         num_scalar_prefetch=2,
-        grid=(batch_count,),
+        grid=(1,),
         in_specs=[
-            pl.BlockSpec((1, rows, points), lambda b, s, k: (b, 0, 0)),
-            pl.BlockSpec((kept_count, BS, BS), lambda b, s, k: (0, 0, 0)),
-            pl.BlockSpec((1, 1, points), lambda b, s, k: (b, 0, 0)),
-            pl.BlockSpec((1, 1, points), lambda b, s, k: (b, 0, 0)),
+            pl.BlockSpec(memory_space=pl.ANY),
+            pl.BlockSpec(memory_space=pl.ANY),
+            pl.BlockSpec((1, span), whole),
+            pl.BlockSpec((1, span), whole),
         ],
         out_specs=[
-            pl.BlockSpec((1, 1, points), lambda b, s, k: (b, 0, 0)),
-            pl.BlockSpec((OV * OV, BS, BS), lambda b, s, k: (0, 0, 0)),
+            pl.BlockSpec((1, span), whole),
+            pl.BlockSpec((OV * OV, BS, BS), lambda i, s, k: (0, 0, 0)),
         ],
         scratch_shapes=[
-            pltpu.VMEM((rows, points), jnp.float32),
+            pltpu.VMEM((rows, span), jnp.float32),
+            pltpu.VMEM((OV * OV, BS, BS), jnp.float32),
             pltpu.VMEM((rows, rows), jnp.bfloat16),
             pltpu.VMEM((rows, rows), jnp.bfloat16),
-            pltpu.VMEM((rows, rows), jnp.float32),
+            pltpu.SemaphoreType.DMA((batch_count * OV,)),
+            pltpu.SemaphoreType.DMA((OV * OV,)),
         ],
     )
     density, pair_tiles = pl.pallas_call(
         batch_kernel,
         grid_spec=grid_spec,
         out_shape=[
-            jax.ShapeDtypeStruct((batch_count, 1, points), jnp.float32),
+            jax.ShapeDtypeStruct((1, span), jnp.float32),
             jax.ShapeDtypeStruct((OV * OV, BS, BS), jnp.float32),
         ],
     )(
@@ -153,8 +160,8 @@
         pick,
         tables,
         tile_values,
-        weights.reshape(batch_count, 1, points),
-        local_pot.reshape(batch_count, 1, points),
+        weights.reshape(1, span),
+        local_pot.reshape(1, span),
     )
     return density.reshape(batch_count, points), pair_tiles
 

time: 113 us -> 108 us (0.956)
  Pallas kernels: 30.8 us -> 25.5 us
  waiting for transfers between devices: 36.9 us -> 35.7 us
    pallas_call x1, Pallas kernels: 20.7 us -> 15.4 us  [batch_terms(): pl.pallas_call(batch_kernel, grid_spec=grid_spec, out_shape=[jax.ShapeDty...]
    all_to_all x1, waiting for transfers between devices: 13.9 us -> 12.7 us  [body(): matrix = jnp.sum(lax.all_to_all(terms, 'tiles', 0, 0, tiled=False), axis=0)]
    unnamed x19 -> x20, local copies, waits for them, and re-layouts: 9.29 us -> 9.91 us
  transfers between devices with their start and end apart: 3 -> 3, of which waited for: 3 -> 3; matrix products, arithmetic and copies ran while one was open for 6% -> 7% of each run, Pallas kernels for 0% -> 0%
where the time goes in v7:
time: 108 us; the launch traced here: 107 us
  waiting for transfers between devices  35.7 us (33%)
  Pallas kernels  25.5 us (24%)
  local copies, waits for them, and re-layouts  20.4 us (19%)
  starting transfers between devices  15.2 us (14%)
  other arithmetic  9.28 us (9%)
    pallas_call x1, Pallas kernels, batch_terms(): pl.pallas_call(batch_kernel, grid_spec=grid_spec, out_shape=[jax.ShapeDty...  15.4 us
    all_to_all x1, waiting for transfers between devices, body(): lax.all_to_all(spread, 'tiles', 0, 0, tiled=False)  13.4 us
    all_to_all x1, waiting for transfers between devices, body(): matrix = jnp.sum(lax.all_to_all(terms, 'tiles', 0, 0, tiled=False), axis=0)  12.7 us
    pallas_call x1, Pallas kernels, tile_products(): pl.pallas_call(tile_kernel, grid_spec=grid_spec, out_shape=jax.ShapeDtype...  10.1 us
    unnamed x20, local copies, waits for them, and re-layouts  9.91 us
    all_to_all x1, waiting for transfers between devices, body(): owned = jnp.sum(lax.all_to_all(partial, 'tiles', 0, 0, tiled=False), axis=0)  9.55 us
    all_to_all x1, starting transfers between devices, body(): owned = jnp.sum(lax.all_to_all(partial, 'tiles', 0, 0, tiled=False), axis=0)  7.38 us
    all_to_all x1, starting transfers between devices, body(): lax.all_to_all(spread, 'tiles', 0, 0, tiled=False)  4.11 us
  transfers between devices with their start and end apart: 3, of which 3 were waited for; matrix products, arithmetic and copies ran while one was open for 7% of the time, Pallas kernels for 0%

profile of v7, /device:TPU:0, one launch (start us, length us, event | category | flops | bytes accessed | tf_op | source)
XLA Modules:
  0.0 106.9 jit_solution(7336398489087156570)
XLA Ops:
  0.6 0.8 copy.17
  2.1 0.7 scatter_custom_fusion.1
  3.9 1.5 %copy.18.refs_16_ = f32[256,1]{1,0:T(8,128)} copy(f32[256,1]{0,1:T(1,128)} %bitcast.23) | data formatting | bytes 2048 | tf_op jit(solution)/shard_map/reshape | solution.py:56
  5.4 10.1 %shard_map.104 = f32[32,64,64]{2,1,0:T(8,128)} custom-call(s32[64]{0:T(128)} %reshape.85.pairs_ref, f32[256,16384]{1,0:T(8,128)} %refs_15_.1, f32[256,16384]{1,0:T(8,128)} %refs_15_.1, f32[256,16384]{1,0:T(8,128)} %refs_15_.1, f32[256,16384]{1,0:T(8,128)} %refs_15_.1, f32[256,16384]{1,0:T(8,128)} %refs_15_.1, f32[256,16384]{1,0:T(8,128)} %refs_15_.1, ...), custom_call_target="tpu_custom_call" | custom-call | tf_op jit(solution)/shard_map/pallas_call | solution.py:52
  15.5 2.7 %reshape.152 = f32[16,1,8192]{2,1,0:T(1,128)} reshape(f32[16,2,64,64]{3,2,1,0:T(8,128)} %bitcast.16) | data formatting | bytes 1048576
  18.2 7.4 %all-to-all-start = ((f32[16,1,8192]{2,1,0:T(1,128)}), f32[16,1,8192]{2,1,0:T(1,128)S(1)}, u32[]{:S(2)}, u32[]{:S(2)}) async-start(f32[16,1,8192]{2,1,0:T(1,128)} %reshape.152), calls=%async_computation | async-start | bytes 1048576 | tf_op jit(solution)/shard_map/all_to_all | solution.py:185
  25.7 1.0 scatter_custom_fusion
  27.4 1.0 sort.15
  28.4 0.7 reshape.84.source_ref
  30.5 9.6 %all-to-all-done = f32[16,1,8192]{2,1,0:T(1,128)S(1)} async-done(((f32[16,1,8192]{2,1,0:T(1,128)}), f32[16,1,8192]{2,1,0:T(1,128)S(1)}, u32[]{:S(2)}, u32[]{:S(2)}) %all-to-all-start) | async-done | bytes 524320 | tf_op jit(solution)/shard_map/all_to_all | solution.py:185
  40.6 1.9 %reduce.8 = f32[16,8192]{1,0:T(8,128)S(1)} reduce(f32[16,1,8192]{2,1,0:T(1,128)S(1)} %all-to-all-done, f32[]{:T(128)} %broadcast.86), dimensions={1}, to_apply=%all_to_all.9.reduce_sub_computation | reduce | bytes 1048580 | tf_op jit(solution)/shard_map/all_to_all | solution.py:185
  43.0 1.4 %reshape.154 = f32[16,1,8192]{2,1,0:T(1,128)} reshape(f32[16,2,64,64]{3,2,1,0:T(8,128)S(1)} %broadcast_in_dim.101) | data formatting | bytes 1048576
  44.5 4.1 %all-to-all-start.1 = ((f32[16,1,8192]{2,1,0:T(1,128)}), f32[16,1,8192]{2,1,0:T(1,128)S(1)}, u32[]{:S(2)}, u32[]{:S(2)}) async-start(f32[16,1,8192]{2,1,0:T(1,128)} %reshape.154), calls=%async_computation.1 | async-start | bytes 1048576 | tf_op jit(solution)/shard_map/all_to_all | solution.py:187
  49.6 13.4 %all-to-all-done.1 = f32[16,1,8192]{2,1,0:T(1,128)S(1)} async-done(((f32[16,1,8192]{2,1,0:T(1,128)}), f32[16,1,8192]{2,1,0:T(1,128)S(1)}, u32[]{:S(2)}, u32[]{:S(2)}) %all-to-all-start.1) | async-done | bytes 524320 | tf_op jit(solution)/shard_map/all_to_all | solution.py:187
  63.1 1.9 %reduce.9 = f32[16,8192]{1,0:T(8,128)S(1)} reduce(f32[16,1,8192]{2,1,0:T(1,128)S(1)} %all-to-all-done.1, f32[]{:T(128)} %broadcast.86), dimensions={1}, to_apply=%all_to_all.10.reduce_sub_computation | reduce | bytes 1048580 | tf_op jit(solution)/shard_map/all_to_all | solution.py:187
  64.9 1.4 %reshape.155 = f32[16,2,64,64]{3,2,1,0:T(8,128)} reshape(f32[16,8192]{1,0:T(8,128)S(1)} %reduce.9) | data formatting | bytes 1048576
  66.3 15.4 %shard_map.105 = (f32[1,2048]{1,0:T(1,128)}, f32[64,64,64]{2,1,0:T(8,128)}) custom-call(s32[64]{0:T(128)} %reshape.84.source_ref, s32[64]{0:T(128)} %broadcast_select_fusion.1.pick_ref, f32[8,512,256]{2,1,0:T(8,128)} %table_hbm.1, f32[32,64,64]{2,1,0:T(8,128)} %bitcast.18, f32[1,2048]{1,0:T(1,128)} %bitcast.20, f32[1,2048]{1,0:T(1,128)} %bitcast.19), custom_call_target="tpu_custom_call" | custom-call | tf_op jit(solution)/shard_map/pallas_call | solution.py:151
  81.8 2.2 %gather_fusion.2 = f32[32,64,64]{2,1,0:T(8,128)S(1)} fusion(f32[64,64,64]{2,1,0:T(8,128)} %get-tuple-element.8, s32[1024]{0:T(1024)S(1)} %pad_clamp_fusion), kind=kCustom, calls=%fused_computation.2 | custom fusion | bytes 1048704 | tf_op jit(solution)/shard_map/gather | solution.py:209
  84.2 1.4 %reshape.156 = f32[16,1,8192]{2,1,0:T(1,128)} reshape(f32[16,2,64,64]{3,2,1,0:T(8,128)S(1)} %broadcast_select_fusion) | data formatting | bytes 1048576
  85.6 3.7 %all-to-all-start.2 = ((f32[16,1,8192]{2,1,0:T(1,128)}), f32[16,1,8192]{2,1,0:T(1,128)S(1)}, u32[]{:S(2)}, u32[]{:S(2)}) async-start(f32[16,1,8192]{2,1,0:T(1,128)} %reshape.156), calls=%async_computation.2 | async-start | bytes 1048576 | tf_op jit(solution)/shard_map/all_to_all | solution.py:212
  89.9 0.7 reduce.7
  91.1 12.7 %all-to-all-done.2 = f32[16,1,8192]{2,1,0:T(1,128)S(1)} async-done(((f32[16,1,8192]{2,1,0:T(1,128)}), f32[16,1,8192]{2,1,0:T(1,128)S(1)}, u32[]{:S(2)}, u32[]{:S(2)}) %all-to-all-start.2) | async-done | bytes 524320 | tf_op jit(solution)/shard_map/all_to_all | solution.py:212
  103.8 1.9 %reduce.10 = f32[16,8192]{1,0:T(8,128)S(1)} reduce(f32[16,1,8192]{2,1,0:T(1,128)S(1)} %all-to-all-done.2, f32[]{:T(128)} %broadcast.86), dimensions={1}, to_apply=%all_to_all.11.reduce_sub_computation | reduce | bytes 1048580 | tf_op jit(solution)/shard_map/all_to_all | solution.py:212
  106.2 0.7 reshape.92
  (46 shorter events, 8.0 us)
Async XLA Ops:
  5.4 20.2 %copy-start.3 = (s32[128,8]{0,1:T(8,128)S(1)}, s32[128,8]{0,1:T(8,128)}, u32[]{:S(2)}) copy-start(s32[128,8]{0,1:T(8,128)} %param.13) | copy-start | bytes 12292
  5.4 20.3 %copy-start.4 = (s32[128]{0:T(128)S(1)}, s32[128]{0:T(128)}, u32[]{:S(2)}) copy-start(s32[128]{0:T(128)} %param.14) | copy-start | bytes 1540
  5.4 23.7 %copy-start = (f32[8,256]{1,0:T(8,128)S(1)}, f32[8,256]{1,0:T(8,128)}, u32[]{:S(2)}) copy-start(f32[8,256]{1,0:T(8,128)} %param.17) | copy-start | bytes 24580
  5.4 24.3 %copy-start.1 = (f32[8,256]{1,0:T(8,128)S(1)}, f32[8,256]{1,0:T(8,128)}, u32[]{:S(2)}) copy-start(f32[8,256]{1,0:T(8,128)} %param.16) | copy-start | bytes 24580
  18.2 21.9 %all-to-all-start = ((f32[16,1,8192]{2,1,0:T(1,128)}), f32[16,1,8192]{2,1,0:T(1,128)S(1)}, u32[]{:S(2)}, u32[]{:S(2)}) async-start(f32[16,1,8192]{2,1,0:T(1,128)} %reshape.152), calls=%async_computation | async-start | bytes 1048576 | tf_op jit(solution)/shard_map/all_to_all | solution.py:185
  44.5 18.6 %all-to-all-start.1 = ((f32[16,1,8192]{2,1,0:T(1,128)}), f32[16,1,8192]{2,1,0:T(1,128)S(1)}, u32[]{:S(2)}, u32[]{:S(2)}) async-start(f32[16,1,8192]{2,1,0:T(1,128)} %reshape.154), calls=%async_computation.1 | async-start | bytes 1048576 | tf_op jit(solution)/shard_map/all_to_all | solution.py:187
  81.8 8.1 %copy-start.2 = (f32[1,2048]{1,0:T(1,128)S(1)}, f32[1,2048]{1,0:T(1,128)}, u32[]{:S(2)}) copy-start(f32[1,2048]{1,0:T(1,128)} %get-tuple-element.7) | copy-start | bytes 24580
  85.6 18.2 %all-to-all-start.2 = ((f32[16,1,8192]{2,1,0:T(1,128)}), f32[16,1,8192]{2,1,0:T(1,128)S(1)}, u32[]{:S(2)}, u32[]{:S(2)}) async-start(f32[16,1,8192]{2,1,0:T(1,128)} %reshape.156), calls=%async_computation.2 | async-start | bytes 1048576 | tf_op jit(solution)/shard_map/all_to_all | solution.py:212

commit v8 on v7

--- a/solution.py
+++ b/solution.py
@@ -10,9 +10,10 @@
 
 
 def tile_kernel(pairs_ref, *refs):
-    group = (len(refs) - 2) // 2
+    group = (len(refs) - 3) // 2
     occ_ref = refs[2 * group]
     out_ref = refs[2 * group + 1]
+    tile_ref = refs[2 * group + 2]
     k = pl.program_id(0)
     occ = occ_ref[...]
     for i in range(group):
@@ -22,13 +23,15 @@
         right = refs[group + i][...] * occ
         left = jnp.where(row_block % 2 == 0, left[:, :BS], left[:, BS:])
         right = jnp.where(col_block % 2 == 0, right[:, :BS], right[:, BS:])
-        out_ref[i] = lax.dot_general(
+        tile_ref[:, :BS] = lax.dot_general(
             left,
             right,
             (((0,), (0,)), ((), ())),
             precision=lax.Precision.HIGHEST,
             preferred_element_type=jnp.float32,
         )
+        out_ref[i, :, :BS] = tile_ref[pl.ds(0, BS // 2, stride=2), :BS]
+        out_ref[i, :, BS:] = tile_ref[pl.ds(1, BS // 2, stride=2), :BS]
 
 
 def tile_products(coeffs, occupation, pairs):
@@ -47,12 +50,13 @@
         in_specs=[block_of(i, 0) for i in range(group)]
         + [block_of(i, 1) for i in range(group)]
         + [pl.BlockSpec((state_count, 1), lambda k, p: (0, 0))],
-        out_specs=pl.BlockSpec((group, BS, BS), lambda k, p: (k, 0, 0)),
+        out_specs=pl.BlockSpec((group, BS // 2, 2 * BS), lambda k, p: (k, 0, 0)),
+        scratch_shapes=[pltpu.VMEM((BS, 2 * BS), jnp.float32)],
     )
     return pl.pallas_call(
         tile_kernel,
         grid_spec=grid_spec,
-        out_shape=jax.ShapeDtypeStruct((kept_count, BS, BS), jnp.float32),
+        out_shape=jax.ShapeDtypeStruct((kept_count, BS // 2, 2 * BS), jnp.float32),
     )(pairs.reshape(-1), *([coeffs] * (2 * group)), occupation.reshape(state_count, 1))
 
 
@@ -70,8 +74,11 @@
 
 def batch_kernel(
     source_ref, pick_ref, table_hbm, tile_hbm, weight_ref, base_ref,
-    density_ref, pair_ref, canon_ref, stage_ref, dense_hi_ref, dense_lo_ref, table_sems, tile_sems,
+    density_ref, pair_ref, canon_ref, chunk_ref, perm_ref, stage_ref, dense_hi_ref, dense_lo_ref,
+    table_sems, chunk_sems, tile_sems,
 ):
+    half = BS // 2
+    lane = 2 * BS
     batch_count, _, points = table_hbm.shape
     copies = []
     for b in range(batch_count):
@@ -84,6 +91,19 @@
             )
             copy.start()
             copies.append(copy)
+    chunk_copies = []
+    for b in range(batch_count):
+        for q in range(OV):
+            start = pl.multiple_of(source_ref[b * OV + q] * BS, BS)
+            for h in range(points // lane):
+                c = b * (points // lane) + h
+                copy = pltpu.make_async_copy(
+                    table_hbm.at[b, pl.ds(start, BS), h * lane:(h + 1) * lane],
+                    chunk_ref.at[c, q * BS:(q + 1) * BS, :],
+                    chunk_sems.at[c * OV + q],
+                )
+                copy.start()
+                chunk_copies.append(copy)
     for p in range(OV * OV):
         copy = pltpu.make_async_copy(
             tile_hbm.at[jnp.maximum(pick_ref[p], 0)], stage_ref.at[p], tile_sems.at[p]
@@ -98,10 +118,18 @@
             tile = jnp.where(pick_ref[p] >= 0, stage_ref[p], 0.0)
             tile_hi = tile.astype(jnp.bfloat16)
             tile_lo = (tile - tile_hi.astype(jnp.float32)).astype(jnp.bfloat16)
-            dense_hi_ref[q1 * BS:(q1 + 1) * BS, q2 * BS:(q2 + 1) * BS] = tile_hi
-            dense_lo_ref[q1 * BS:(q1 + 1) * BS, q2 * BS:(q2 + 1) * BS] = tile_lo
-    for copy in copies[:batch_count * OV]:
+            dense_hi_ref[q1 * BS:q1 * BS + half, q2 * BS:(q2 + 1) * BS] = tile_hi[:, :BS]
+            dense_hi_ref[q1 * BS + half:(q1 + 1) * BS, q2 * BS:(q2 + 1) * BS] = tile_hi[:, BS:]
+            dense_lo_ref[q1 * BS:q1 * BS + half, q2 * BS:(q2 + 1) * BS] = tile_lo[:, :BS]
+            dense_lo_ref[q1 * BS + half:(q1 + 1) * BS, q2 * BS:(q2 + 1) * BS] = tile_lo[:, BS:]
+    for copy in copies[:batch_count * OV] + chunk_copies:
         copy.wait()
+    for c in range(chunk_ref.shape[0]):
+        for q in range(OV):
+            perm_ref[q * BS:q * BS + half, c * lane:(c + 1) * lane] = chunk_ref[c, pl.ds(q * BS, half, stride=2), :]
+            perm_ref[q * BS + half:(q + 1) * BS, c * lane:(c + 1) * lane] = chunk_ref[
+                c, pl.ds(q * BS + 1, half, stride=2), :
+            ]
 
     grid = canon_ref[...]
     grid_hi = grid.astype(jnp.bfloat16)
@@ -112,14 +140,16 @@
 
     dense_hi = dense_hi_ref[...]
     mixed = nn(dense_hi, grid_hi) + (nn(dense_hi, grid_lo) + nn(dense_lo_ref[...], grid_hi))
-    density = jnp.sum(grid * mixed, axis=0, keepdims=True)
+    permuted = perm_ref[...]
+    density = jnp.sum(permuted * mixed, axis=0, keepdims=True)
     potential = base_ref[...] + density - density * density * density / 6.0
     density_ref[...] = density
-    weighted = grid * (weight_ref[...] * potential)
+    weighted = permuted * (weight_ref[...] * potential)
     terms = split_dot(weighted, grid, ((1,), (1,)))
     for q1 in range(OV):
         for q2 in range(OV):
-            pair_ref[q1 * OV + q2] = terms[q1 * BS:(q1 + 1) * BS, q2 * BS:(q2 + 1) * BS]
+            pair_ref[q1 * OV + q2, :, :BS] = terms[q1 * BS:q1 * BS + half, q2 * BS:(q2 + 1) * BS]
+            pair_ref[q1 * OV + q2, :, BS:] = terms[q1 * BS + half:(q1 + 1) * BS, q2 * BS:(q2 + 1) * BS]
 
 
 def batch_terms(source, pick, tables, tile_values, weights, local_pot):
@@ -137,14 +167,17 @@
         ],
         out_specs=[
             pl.BlockSpec((1, span), whole),
-            pl.BlockSpec((OV * OV, BS, BS), lambda i, s, k: (0, 0, 0)),
+            pl.BlockSpec((OV * OV, BS // 2, 2 * BS), lambda i, s, k: (0, 0, 0)),
         ],
         scratch_shapes=[
             pltpu.VMEM((rows, span), jnp.float32),
-            pltpu.VMEM((OV * OV, BS, BS), jnp.float32),
+            pltpu.VMEM((span // (2 * BS), rows, 2 * BS), jnp.float32),
+            pltpu.VMEM((rows, span), jnp.float32),
+            pltpu.VMEM((OV * OV, BS // 2, 2 * BS), jnp.float32),
             pltpu.VMEM((rows, rows), jnp.bfloat16),
             pltpu.VMEM((rows, rows), jnp.bfloat16),
             pltpu.SemaphoreType.DMA((batch_count * OV,)),
+            pltpu.SemaphoreType.DMA((span // (2 * BS) * OV,)),
             pltpu.SemaphoreType.DMA((OV * OV,)),
         ],
     )
@@ -153,7 +186,7 @@
         grid_spec=grid_spec,
         out_shape=[
             jax.ShapeDtypeStruct((1, span), jnp.float32),
-            jax.ShapeDtypeStruct((OV * OV, BS, BS), jnp.float32),
+            jax.ShapeDtypeStruct((OV * OV, BS // 2, 2 * BS), jnp.float32),
         ],
     )(
         source.reshape(-1),
@@ -181,10 +214,12 @@
     ladder_kept = jnp.arange(kept_count, dtype=jnp.int32)
     slot_kept = jnp.zeros((kept_count,), jnp.int32).at[tile_slot].set(ladder_kept)
     pairs = kept_tiles[slot_kept]
-    partial = tile_products(coeffs, occupation, pairs).reshape(devices, owned_count, BS, BS)
+    partial = tile_products(coeffs, occupation, pairs).reshape(devices, owned_count, BS // 2, 2 * BS)
     owned = jnp.sum(lax.all_to_all(partial, "tiles", 0, 0, tiled=False), axis=0)
-    spread = jnp.broadcast_to(owned[None], (devices, owned_count, BS, BS))
-    tile_values = lax.all_to_all(spread, "tiles", 0, 0, tiled=False).reshape(kept_count, BS, BS)
+    spread = jnp.broadcast_to(owned[None], (devices, owned_count, BS // 2, 2 * BS))
+    tile_values = lax.all_to_all(spread, "tiles", 0, 0, tiled=False).reshape(
+        kept_count, BS // 2, 2 * BS
+    )
 
     ladder_batch = jnp.arange(batch_total, dtype=jnp.int32)
     slot_batch = jnp.zeros((batch_total,), jnp.int32).at[batch_slot].set(ladder_batch)
@@ -208,7 +243,7 @@
     density, pair_tiles = batch_terms(source, pick, tables, tile_values, weights, local_pot)
     contrib = jnp.where(present[:, None, None], pair_tiles[pair_code], 0.0)
 
-    terms = contrib.reshape(devices, owned_count, BS, BS)
+    terms = contrib.reshape(devices, owned_count, BS // 2, 2 * BS)
     matrix = jnp.sum(lax.all_to_all(terms, "tiles", 0, 0, tiled=False), axis=0)
     matrix = matrix.reshape(owned_count, BS * BS)
     return (density, matrix)

time: 108 us -> 105 us (0.972)
  Pallas kernels: 25.5 us -> 35.1 us
  local copies, waits for them, and re-layouts: 20.4 us -> 13.1 us
  other arithmetic: 9.28 us -> 5.08 us
    pallas_call x1, Pallas kernels: 10.1 us -> 16.6 us  [tile_products(): pl.pallas_call(tile_kernel, grid_spec=grid_spec, out_shape=jax.ShapeDtype...]
    unnamed x20 -> x15, local copies, waits for them, and re-layouts: 9.91 us -> 3.55 us
    all_to_all x3 -> x0, other arithmetic: 5.58 us -> none  [the longest x1 1.86 us: body(): lax.all_to_all(spread, 'tiles', 0, 0, tiled=False)]
    pallas_call x1, Pallas kernels: 15.4 us -> 18.5 us  [batch_terms(): pl.pallas_call(batch_kernel, grid_spec=grid_spec, out_shape=[jax.ShapeDty...]
  transfers between devices with their start and end apart: 3 -> 3, of which waited for: 3 -> 3; matrix products, arithmetic and copies ran while one was open for 7% -> 8% of each run, Pallas kernels for 0% -> 0%
where the time goes in v8:
time: 105 us
  Pallas kernels  35.1 us (33%)
  waiting for transfers between devices  35 us (33%)
  starting transfers between devices  15.7 us (15%)
  local copies, waits for them, and re-layouts  13.1 us (12%)
  other arithmetic  5.08 us (5%)
    pallas_call x1, Pallas kernels, batch_terms(): pl.pallas_call(batch_kernel, grid_spec=grid_spec, out_shape=[jax.ShapeDty...  18.5 us
    pallas_call x1, Pallas kernels, tile_products(): pl.pallas_call(tile_kernel, grid_spec=grid_spec, out_shape=jax.ShapeDtype...  16.6 us
    all_to_all x1, waiting for transfers between devices, body(): lax.all_to_all(spread, 'tiles', 0, 0, tiled=False)  13.4 us
    all_to_all x1, waiting for transfers between devices, body(): matrix = jnp.sum(lax.all_to_all(terms, 'tiles', 0, 0, tiled=False), axis=0)  12 us
    all_to_all x1, waiting for transfers between devices, body(): owned = jnp.sum(lax.all_to_all(partial, 'tiles', 0, 0, tiled=False), axis=0)  9.56 us
    all_to_all x1, starting transfers between devices, body(): owned = jnp.sum(lax.all_to_all(partial, 'tiles', 0, 0, tiled=False), axis=0)  7.4 us
    all_to_all x1, starting transfers between devices, body(): matrix = jnp.sum(lax.all_to_all(terms, 'tiles', 0, 0, tiled=False), axis=0)  4.17 us
    all_to_all x1, starting transfers between devices, body(): lax.all_to_all(spread, 'tiles', 0, 0, tiled=False)  4.1 us
  transfers between devices with their start and end apart: 3, of which 3 were waited for; matrix products, arithmetic and copies ran while one was open for 8% of the time, Pallas kernels for 0%

profile of v8, /device:TPU:0, one launch (start us, length us, event | category | flops | bytes accessed | tf_op | source)
XLA Modules:
  0.0 104.7 jit_solution(8215799501786594298)
XLA Ops:
  0.6 0.8 copy.17
  1.4 0.7 compare_select_fusion.4
  2.1 0.7 scatter_custom_fusion.1
  3.3 0.6 reshape.85.pairs_ref
  3.9 1.5 %copy.18.refs_16_ = f32[256,1]{1,0:T(8,128)} copy(f32[256,1]{0,1:T(1,128)} %bitcast.29) | data formatting | bytes 2048 | tf_op jit(solution)/shard_map/reshape | solution.py:60
  5.4 16.6 %shard_map.104 = f32[32,32,128]{2,1,0:T(8,128)} custom-call(s32[64]{0:T(128)} %reshape.85.pairs_ref, f32[256,16384]{1,0:T(8,128)} %refs_15_.1, f32[256,16384]{1,0:T(8,128)} %refs_15_.1, f32[256,16384]{1,0:T(8,128)} %refs_15_.1, f32[256,16384]{1,0:T(8,128)} %refs_15_.1, f32[256,16384]{1,0:T(8,128)} %refs_15_.1, f32[256,16384]{1,0:T(8,128)} %refs_15_.1, ...), custom_call_target="tpu_custom_call" | custom-call | tf_op jit(solution)/shard_map/pallas_call | solution.py:56
  22.0 7.4 %all-to-all-start = ((f32[16,2,32,128]{3,2,1,0:T(8,128)}), f32[16,2,32,128]{3,2,1,0:T(8,128)S(1)}, u32[]{:S(2)}, u32[]{:S(2)}) async-start(f32[16,2,32,128]{3,2,1,0:T(8,128)} %bitcast.20), calls=%async_computation | async-start | bytes 1048576 | tf_op jit(solution)/shard_map/all_to_all | solution.py:218
  29.6 1.0 scatter_custom_fusion
  31.2 1.0 sort.15
  32.3 0.7 reshape.84.source_ref
  32.9 0.6 copy.20
  33.5 0.6 copy.19
  34.3 9.6 %all-to-all-done = f32[16,2,32,128]{3,2,1,0:T(8,128)S(1)} async-done(((f32[16,2,32,128]{3,2,1,0:T(8,128)}), f32[16,2,32,128]{3,2,1,0:T(8,128)S(1)}, u32[]{:S(2)}, u32[]{:S(2)}) %all-to-all-start) | async-done | bytes 524320 | tf_op jit(solution)/shard_map/all_to_all | solution.py:218
  43.9 0.8 broadcast_in_dim.101
  44.8 4.1 %all-to-all-start.1 = ((f32[16,2,32,128]{3,2,1,0:T(8,128)}), f32[16,2,32,128]{3,2,1,0:T(8,128)S(1)}, u32[]{:S(2)}, u32[]{:S(2)}) async-start(f32[16,2,32,128]{3,2,1,0:T(8,128)} %broadcast_in_dim.101), calls=%async_computation.1 | async-start | bytes 1048576 | tf_op jit(solution)/shard_map/all_to_all | solution.py:220
  49.9 13.4 %all-to-all-done.1 = f32[16,2,32,128]{3,2,1,0:T(8,128)S(1)} async-done(((f32[16,2,32,128]{3,2,1,0:T(8,128)}), f32[16,2,32,128]{3,2,1,0:T(8,128)S(1)}, u32[]{:S(2)}, u32[]{:S(2)}) %all-to-all-start.1) | async-done | bytes 524320 | tf_op jit(solution)/shard_map/all_to_all | solution.py:220
  63.4 0.8 copy-done
  64.2 18.5 %shard_map.105 = (f32[1,2048]{1,0:T(1,128)}, f32[64,32,128]{2,1,0:T(8,128)}) custom-call(s32[64]{0:T(128)} %reshape.84.source_ref, s32[64]{0:T(128)} %broadcast_select_fusion.1.pick_ref, f32[8,512,256]{2,1,0:T(8,128)} %table_hbm.1, f32[32,32,128]{2,1,0:T(8,128)} %bitcast.22, f32[1,2048]{1,0:T(1,128)} %bitcast.25, f32[1,2048]{1,0:T(1,128)} %bitcast.24), custom_call_target="tpu_custom_call" | custom-call | tf_op jit(solution)/shard_map/pallas_call | solution.py:184
  82.6 1.8 %gather_fusion.2 = f32[32,32,128]{2,1,0:T(8,128)S(1)} fusion(f32[64,32,128]{2,1,0:T(8,128)} %get-tuple-element.8, s32[1024]{0:T(1024)S(1)} %pad_clamp_fusion), kind=kCustom, calls=%fused_computation.2 | custom fusion | bytes 1048704 | tf_op jit(solution)/shard_map/gather | solution.py:244
  84.5 0.9 broadcast_select_fusion
  85.4 4.2 %all-to-all-start.2 = ((f32[16,2,32,128]{3,2,1,0:T(8,128)}), f32[16,2,32,128]{3,2,1,0:T(8,128)S(1)}, u32[]{:S(2)}, u32[]{:S(2)}) async-start(f32[16,2,32,128]{3,2,1,0:T(8,128)} %broadcast_select_fusion), calls=%async_computation.2 | async-start | bytes 1048576 | tf_op jit(solution)/shard_map/all_to_all | solution.py:247
  90.0 1.4 %reduce.7 = f32[2048]{0:T(1024)S(1)} reduce(f32[1,2048]{1,0:T(1,128)} %get-tuple-element.7, f32[]{:T(128)} %broadcast.85), dimensions={0}, to_apply=%get-tuple-element.7.reduce_sub_computation.3 | reduce | bytes 16388 | tf_op jit(solution)/shard_map/pallas_call | solution.py:184
  92.0 12.0 %all-to-all-done.2 = f32[16,2,32,128]{3,2,1,0:T(8,128)S(1)} async-done(((f32[16,2,32,128]{3,2,1,0:T(8,128)}), f32[16,2,32,128]{3,2,1,0:T(8,128)S(1)}, u32[]{:S(2)}, u32[]{:S(2)}) %all-to-all-start.2) | async-done | bytes 524320 | tf_op jit(solution)/shard_map/all_to_all | solution.py:247
  104.0 0.6 copy.23
  (36 shorter events, 3.8 us)
Async XLA Ops:
  5.4 24.0 %copy-start.3 = (s32[128,8]{0,1:T(8,128)S(1)}, s32[128,8]{0,1:T(8,128)}, u32[]{:S(2)}) copy-start(s32[128,8]{0,1:T(8,128)} %param.13) | copy-start | bytes 12292
  5.4 24.1 %copy-start.4 = (s32[128]{0:T(128)S(1)}, s32[128]{0:T(128)}, u32[]{:S(2)}) copy-start(s32[128]{0:T(128)} %param.14) | copy-start | bytes 1540
  5.4 27.5 %copy-start.1 = (f32[8,256]{1,0:T(8,128)S(1)}, f32[8,256]{1,0:T(8,128)}, u32[]{:S(2)}) copy-start(f32[8,256]{1,0:T(8,128)} %param.17) | copy-start | bytes 24580
  5.4 28.1 %copy-start.2 = (f32[8,256]{1,0:T(8,128)S(1)}, f32[8,256]{1,0:T(8,128)}, u32[]{:S(2)}) copy-start(f32[8,256]{1,0:T(8,128)} %param.16) | copy-start | bytes 24580
  22.0 21.9 %all-to-all-start = ((f32[16,2,32,128]{3,2,1,0:T(8,128)}), f32[16,2,32,128]{3,2,1,0:T(8,128)S(1)}, u32[]{:S(2)}, u32[]{:S(2)}) async-start(f32[16,2,32,128]{3,2,1,0:T(8,128)} %bitcast.20), calls=%async_computation | async-start | bytes 1048576 | tf_op jit(solution)/shard_map/all_to_all | solution.py:218
  44.8 18.6 %all-to-all-start.1 = ((f32[16,2,32,128]{3,2,1,0:T(8,128)}), f32[16,2,32,128]{3,2,1,0:T(8,128)S(1)}, u32[]{:S(2)}, u32[]{:S(2)}) async-start(f32[16,2,32,128]{3,2,1,0:T(8,128)} %broadcast_in_dim.101), calls=%async_computation.1 | async-start | bytes 1048576 | tf_op jit(solution)/shard_map/all_to_all | solution.py:220
  63.4 0.8 copy-start
  85.4 18.6 %all-to-all-start.2 = ((f32[16,2,32,128]{3,2,1,0:T(8,128)}), f32[16,2,32,128]{3,2,1,0:T(8,128)S(1)}, u32[]{:S(2)}, u32[]{:S(2)}) async-start(f32[16,2,32,128]{3,2,1,0:T(8,128)} %broadcast_select_fusion), calls=%async_computation.2 | async-start | bytes 1048576 | tf_op jit(solution)/shard_map/all_to_all | solution.py:247

commit v9 on v8

--- a/solution.py
+++ b/solution.py
@@ -10,10 +10,9 @@
 
 
 def tile_kernel(pairs_ref, *refs):
-    group = (len(refs) - 3) // 2
+    group = (len(refs) - 2) // 2
     occ_ref = refs[2 * group]
     out_ref = refs[2 * group + 1]
-    tile_ref = refs[2 * group + 2]
     k = pl.program_id(0)
     occ = occ_ref[...]
     for i in range(group):
@@ -23,15 +22,13 @@
         right = refs[group + i][...] * occ
         left = jnp.where(row_block % 2 == 0, left[:, :BS], left[:, BS:])
         right = jnp.where(col_block % 2 == 0, right[:, :BS], right[:, BS:])
-        tile_ref[:, :BS] = lax.dot_general(
+        out_ref[i] = lax.dot_general(
             left,
             right,
             (((0,), (0,)), ((), ())),
             precision=lax.Precision.HIGHEST,
             preferred_element_type=jnp.float32,
         )
-        out_ref[i, :, :BS] = tile_ref[pl.ds(0, BS // 2, stride=2), :BS]
-        out_ref[i, :, BS:] = tile_ref[pl.ds(1, BS // 2, stride=2), :BS]
 
 
 def tile_products(coeffs, occupation, pairs):
@@ -50,13 +47,12 @@
         in_specs=[block_of(i, 0) for i in range(group)]
         + [block_of(i, 1) for i in range(group)]
         + [pl.BlockSpec((state_count, 1), lambda k, p: (0, 0))],
-        out_specs=pl.BlockSpec((group, BS // 2, 2 * BS), lambda k, p: (k, 0, 0)),
-        scratch_shapes=[pltpu.VMEM((BS, 2 * BS), jnp.float32)],
+        out_specs=pl.BlockSpec((group, BS, BS), lambda k, p: (k, 0, 0)),
     )
     return pl.pallas_call(
         tile_kernel,
         grid_spec=grid_spec,
-        out_shape=jax.ShapeDtypeStruct((kept_count, BS // 2, 2 * BS), jnp.float32),
+        out_shape=jax.ShapeDtypeStruct((kept_count, BS, BS), jnp.float32),
     )(pairs.reshape(-1), *([coeffs] * (2 * group)), occupation.reshape(state_count, 1))
 
 

time: 105 us -> 101 us (0.962)
  Pallas kernels: 35.1 us -> 28.8 us
  local copies, waits for them, and re-layouts: 13.1 us -> 15.4 us
    pallas_call x1, Pallas kernels: 16.6 us -> 10.1 us  [tile_products(): pl.pallas_call(tile_kernel, grid_spec=grid_spec, out_shape=jax.ShapeDtype...]
    reshape x0 -> x1, local copies, waits for them, and re-layouts: none -> 2.25 us  [body(): tile_products(coeffs, occupation, pairs)]
where the time goes in v9:
time: 101 us; the launch traced here: 100 us
  waiting for transfers between devices  34.9 us (35%)
  Pallas kernels  28.8 us (29%)
  local copies, waits for them, and re-layouts  15.4 us (15%)
  starting transfers between devices  15.1 us (15%)
  other arithmetic  5.08 us (5%)
    pallas_call x1, Pallas kernels, batch_terms(): pl.pallas_call(batch_kernel, grid_spec=grid_spec, out_shape=[jax.ShapeDty...  18.8 us
    all_to_all x1, waiting for transfers between devices, body(): lax.all_to_all(spread, 'tiles', 0, 0, tiled=False)  13.4 us
    all_to_all x1, waiting for transfers between devices, body(): matrix = jnp.sum(lax.all_to_all(terms, 'tiles', 0, 0, tiled=False), axis=0)  11.9 us
    pallas_call x1, Pallas kernels, tile_products(): pl.pallas_call(tile_kernel, grid_spec=grid_spec, out_shape=jax.ShapeDtype...  10.1 us
    all_to_all x1, waiting for transfers between devices, body(): owned = jnp.sum(lax.all_to_all(partial, 'tiles', 0, 0, tiled=False), axis=0)  9.56 us
    all_to_all x1, starting transfers between devices, body(): owned = jnp.sum(lax.all_to_all(partial, 'tiles', 0, 0, tiled=False), axis=0)  7.39 us
    all_to_all x1, starting transfers between devices, body(): lax.all_to_all(spread, 'tiles', 0, 0, tiled=False)  4.1 us
    all_to_all x1, starting transfers between devices, body(): matrix = jnp.sum(lax.all_to_all(terms, 'tiles', 0, 0, tiled=False), axis=0)  3.57 us
  transfers between devices with their start and end apart: 3, of which 3 were waited for; matrix products, arithmetic and copies ran while one was open for 8% of the time, Pallas kernels for 0%

profile of v9, /device:TPU:0, one launch (start us, length us, event | category | flops | bytes accessed | tf_op | source)
XLA Modules:
  0.0 100.0 jit_solution(15688903476987226805)
XLA Ops:
  0.6 0.8 copy.17
  1.4 0.7 compare_select_fusion.4
  2.1 0.7 scatter_custom_fusion.1
  3.3 0.6 reshape.85.pairs_ref
  3.9 1.5 %copy.18.refs_16_ = f32[256,1]{1,0:T(8,128)} copy(f32[256,1]{0,1:T(1,128)} %bitcast.27) | data formatting | bytes 2048 | tf_op jit(solution)/shard_map/reshape | solution.py:56
  5.4 10.1 %shard_map.104 = f32[32,64,64]{2,1,0:T(8,128)} custom-call(s32[64]{0:T(128)} %reshape.85.pairs_ref, f32[256,16384]{1,0:T(8,128)} %refs_15_.1, f32[256,16384]{1,0:T(8,128)} %refs_15_.1, f32[256,16384]{1,0:T(8,128)} %refs_15_.1, f32[256,16384]{1,0:T(8,128)} %refs_15_.1, f32[256,16384]{1,0:T(8,128)} %refs_15_.1, f32[256,16384]{1,0:T(8,128)} %refs_15_.1, ...), custom_call_target="tpu_custom_call" | custom-call | tf_op jit(solution)/shard_map/pallas_call | solution.py:52
  15.5 2.2 %reshape.87 = f32[16,2,32,128]{3,2,1,0:T(8,128)} reshape(f32[32,64,64]{2,1,0:T(8,128)} %shard_map.104) | data formatting | bytes 1048576 | tf_op jit(solution)/shard_map/reshape | solution.py:213
  17.7 7.4 %all-to-all-start = ((f32[16,2,32,128]{3,2,1,0:T(8,128)}), f32[16,2,32,128]{3,2,1,0:T(8,128)S(1)}, u32[]{:S(2)}, u32[]{:S(2)}) async-start(f32[16,2,32,128]{3,2,1,0:T(8,128)} %reshape.87), calls=%async_computation | async-start | bytes 1048576 | tf_op jit(solution)/shard_map/all_to_all | solution.py:214
  25.3 1.0 scatter_custom_fusion
  26.9 1.0 sort.15
  28.0 0.7 reshape.84.source_ref
  28.6 0.6 copy.20
  30.0 9.6 %all-to-all-done = f32[16,2,32,128]{3,2,1,0:T(8,128)S(1)} async-done(((f32[16,2,32,128]{3,2,1,0:T(8,128)}), f32[16,2,32,128]{3,2,1,0:T(8,128)S(1)}, u32[]{:S(2)}, u32[]{:S(2)}) %all-to-all-start) | async-done | bytes 524320 | tf_op jit(solution)/shard_map/all_to_all | solution.py:214
  39.6 0.8 broadcast_in_dim.101
  40.5 4.1 %all-to-all-start.1 = ((f32[16,2,32,128]{3,2,1,0:T(8,128)}), f32[16,2,32,128]{3,2,1,0:T(8,128)S(1)}, u32[]{:S(2)}, u32[]{:S(2)}) async-start(f32[16,2,32,128]{3,2,1,0:T(8,128)} %broadcast_in_dim.101), calls=%async_computation.1 | async-start | bytes 1048576 | tf_op jit(solution)/shard_map/all_to_all | solution.py:216
  45.6 13.4 %all-to-all-done.1 = f32[16,2,32,128]{3,2,1,0:T(8,128)S(1)} async-done(((f32[16,2,32,128]{3,2,1,0:T(8,128)}), f32[16,2,32,128]{3,2,1,0:T(8,128)S(1)}, u32[]{:S(2)}, u32[]{:S(2)}) %all-to-all-start.1) | async-done | bytes 524320 | tf_op jit(solution)/shard_map/all_to_all | solution.py:216
  59.1 0.8 copy-done
  59.9 18.8 %shard_map.105 = (f32[1,2048]{1,0:T(1,128)}, f32[64,32,128]{2,1,0:T(8,128)}) custom-call(s32[64]{0:T(128)} %reshape.84.source_ref, s32[64]{0:T(128)} %broadcast_select_fusion.1.pick_ref, f32[8,512,256]{2,1,0:T(8,128)} %table_hbm.1, f32[32,32,128]{2,1,0:T(8,128)} %bitcast.20, f32[1,2048]{1,0:T(1,128)} %bitcast.23, f32[1,2048]{1,0:T(1,128)} %bitcast.22), custom_call_target="tpu_custom_call" | custom-call | tf_op jit(solution)/shard_map/pallas_call | solution.py:180
  78.6 1.8 %gather_fusion.2 = f32[32,32,128]{2,1,0:T(8,128)S(1)} fusion(f32[64,32,128]{2,1,0:T(8,128)} %get-tuple-element.8, s32[1024]{0:T(1024)S(1)} %pad_clamp_fusion), kind=kCustom, calls=%fused_computation.2 | custom fusion | bytes 1048704 | tf_op jit(solution)/shard_map/gather | solution.py:240
  80.4 0.9 broadcast_select_fusion
  81.3 3.6 %all-to-all-start.2 = ((f32[16,2,32,128]{3,2,1,0:T(8,128)}), f32[16,2,32,128]{3,2,1,0:T(8,128)S(1)}, u32[]{:S(2)}, u32[]{:S(2)}) async-start(f32[16,2,32,128]{3,2,1,0:T(8,128)} %broadcast_select_fusion), calls=%async_computation.2 | async-start | bytes 1048576 | tf_op jit(solution)/shard_map/all_to_all | solution.py:243
  85.4 1.4 %reduce.7 = f32[2048]{0:T(1024)S(1)} reduce(f32[1,2048]{1,0:T(1,128)} %get-tuple-element.7, f32[]{:T(128)} %broadcast.85), dimensions={0}, to_apply=%get-tuple-element.7.reduce_sub_computation.3 | reduce | bytes 16388 | tf_op jit(solution)/shard_map/pallas_call | solution.py:180
  87.4 11.9 %all-to-all-done.2 = f32[16,2,32,128]{3,2,1,0:T(8,128)S(1)} async-done(((f32[16,2,32,128]{3,2,1,0:T(8,128)}), f32[16,2,32,128]{3,2,1,0:T(8,128)S(1)}, u32[]{:S(2)}, u32[]{:S(2)}) %all-to-all-start.2) | async-done | bytes 524320 | tf_op jit(solution)/shard_map/all_to_all | solution.py:243
  99.4 0.6 copy.23
  (37 shorter events, 4.4 us)
Async XLA Ops:
  5.4 19.7 %copy-start.3 = (s32[128,8]{0,1:T(8,128)S(1)}, s32[128,8]{0,1:T(8,128)}, u32[]{:S(2)}) copy-start(s32[128,8]{0,1:T(8,128)} %param.13) | copy-start | bytes 12292
  5.4 19.8 %copy-start.4 = (s32[128]{0:T(128)S(1)}, s32[128]{0:T(128)}, u32[]{:S(2)}) copy-start(s32[128]{0:T(128)} %param.14) | copy-start | bytes 1540
  5.4 23.2 %copy-start.1 = (f32[8,256]{1,0:T(8,128)S(1)}, f32[8,256]{1,0:T(8,128)}, u32[]{:S(2)}) copy-start(f32[8,256]{1,0:T(8,128)} %param.17) | copy-start | bytes 24580
  5.4 23.8 %copy-start.2 = (f32[8,256]{1,0:T(8,128)S(1)}, f32[8,256]{1,0:T(8,128)}, u32[]{:S(2)}) copy-start(f32[8,256]{1,0:T(8,128)} %param.16) | copy-start | bytes 24580
  17.7 21.9 %all-to-all-start = ((f32[16,2,32,128]{3,2,1,0:T(8,128)}), f32[16,2,32,128]{3,2,1,0:T(8,128)S(1)}, u32[]{:S(2)}, u32[]{:S(2)}) async-start(f32[16,2,32,128]{3,2,1,0:T(8,128)} %reshape.87), calls=%async_computation | async-start | bytes 1048576 | tf_op jit(solution)/shard_map/all_to_all | solution.py:214
  40.5 18.6 %all-to-all-start.1 = ((f32[16,2,32,128]{3,2,1,0:T(8,128)}), f32[16,2,32,128]{3,2,1,0:T(8,128)S(1)}, u32[]{:S(2)}, u32[]{:S(2)}) async-start(f32[16,2,32,128]{3,2,1,0:T(8,128)} %broadcast_in_dim.101), calls=%async_computation.1 | async-start | bytes 1048576 | tf_op jit(solution)/shard_map/all_to_all | solution.py:216
  59.1 0.8 copy-start
  81.3 18.0 %all-to-all-start.2 = ((f32[16,2,32,128]{3,2,1,0:T(8,128)}), f32[16,2,32,128]{3,2,1,0:T(8,128)S(1)}, u32[]{:S(2)}, u32[]{:S(2)}) async-start(f32[16,2,32,128]{3,2,1,0:T(8,128)} %broadcast_select_fusion), calls=%async_computation.2 | async-start | bytes 1048576 | tf_op jit(solution)/shard_map/all_to_all | solution.py:243

commit v10 on v9

--- a/solution.py
+++ b/solution.py
@@ -68,15 +68,12 @@
     return one(left_hi, right_hi) + (one(left_hi, right_lo) + one(left_lo, right_hi))
 
 
-def batch_kernel(
-    source_ref, pick_ref, table_hbm, tile_hbm, weight_ref, base_ref,
-    density_ref, pair_ref, canon_ref, chunk_ref, perm_ref, stage_ref, dense_hi_ref, dense_lo_ref,
-    table_sems, chunk_sems, tile_sems,
-):
+def prep_kernel(source_ref, table_hbm, hi_ref, lo_ref, perm_ref, canon_ref, chunk_ref, table_sems, chunk_sems):
     half = BS // 2
     lane = 2 * BS
     batch_count, _, points = table_hbm.shape
     copies = []
+    chunk_copies = []
     for b in range(batch_count):
         for q in range(OV):
             start = pl.multiple_of(source_ref[b * OV + q] * BS, BS)
@@ -87,10 +84,6 @@
             )
             copy.start()
             copies.append(copy)
-    chunk_copies = []
-    for b in range(batch_count):
-        for q in range(OV):
-            start = pl.multiple_of(source_ref[b * OV + q] * BS, BS)
             for h in range(points // lane):
                 c = b * (points // lane) + h
                 copy = pltpu.make_async_copy(
@@ -100,13 +93,66 @@
                 )
                 copy.start()
                 chunk_copies.append(copy)
+    for copy in copies:
+        copy.wait()
+    grid = canon_ref[...]
+    grid_hi = grid.astype(jnp.bfloat16)
+    hi_ref[...] = grid_hi
+    lo_ref[...] = (grid - grid_hi.astype(jnp.float32)).astype(jnp.bfloat16)
+    for copy in chunk_copies:
+        copy.wait()
+    for c in range(chunk_ref.shape[0]):
+        for q in range(OV):
+            perm_ref[q * BS:q * BS + half, c * lane:(c + 1) * lane] = chunk_ref[c, pl.ds(q * BS, half, stride=2), :]
+            perm_ref[q * BS + half:(q + 1) * BS, c * lane:(c + 1) * lane] = chunk_ref[
+                c, pl.ds(q * BS + 1, half, stride=2), :
+            ]
+
+
+def prep_tables(source, tables):
+    batch_count, rows, points = tables.shape
+    span = batch_count * points
+    whole = lambda i, s: (0, 0)
+    grid_spec = pltpu.PrefetchScalarGridSpec(
+        num_scalar_prefetch=1,
+        grid=(1,),
+        in_specs=[pl.BlockSpec(memory_space=pl.ANY)],
+        out_specs=[
+            pl.BlockSpec((rows, span), whole),
+            pl.BlockSpec((rows, span), whole),
+            pl.BlockSpec((rows, span), whole),
+        ],
+        scratch_shapes=[
+            pltpu.VMEM((rows, span), jnp.float32),
+            pltpu.VMEM((span // (2 * BS), rows, 2 * BS), jnp.float32),
+            pltpu.SemaphoreType.DMA((batch_count * OV,)),
+            pltpu.SemaphoreType.DMA((span // (2 * BS) * OV,)),
+        ],
+    )
+    return pl.pallas_call(
+        prep_kernel,
+        grid_spec=grid_spec,
+        out_shape=[
+            jax.ShapeDtypeStruct((rows, span), jnp.bfloat16),
+            jax.ShapeDtypeStruct((rows, span), jnp.bfloat16),
+            jax.ShapeDtypeStruct((rows, span), jnp.float32),
+        ],
+    )(source.reshape(-1), tables)
+
+
+def batch_kernel(
+    pick_ref, hi_ref, lo_ref, perm_ref, tile_hbm, weight_ref, base_ref,
+    density_ref, pair_ref, stage_ref, dense_hi_ref, dense_lo_ref, tile_sems,
+):
+    half = BS // 2
+    copies = []
     for p in range(OV * OV):
         copy = pltpu.make_async_copy(
             tile_hbm.at[jnp.maximum(pick_ref[p], 0)], stage_ref.at[p], tile_sems.at[p]
         )
         copy.start()
         copies.append(copy)
-    for copy in copies[batch_count * OV:]:
+    for copy in copies:
         copy.wait()
     for q1 in range(OV):
         for q2 in range(OV):
@@ -118,30 +164,24 @@
             dense_hi_ref[q1 * BS + half:(q1 + 1) * BS, q2 * BS:(q2 + 1) * BS] = tile_hi[:, BS:]
             dense_lo_ref[q1 * BS:q1 * BS + half, q2 * BS:(q2 + 1) * BS] = tile_lo[:, :BS]
             dense_lo_ref[q1 * BS + half:(q1 + 1) * BS, q2 * BS:(q2 + 1) * BS] = tile_lo[:, BS:]
-    for copy in copies[:batch_count * OV] + chunk_copies:
-        copy.wait()
-    for c in range(chunk_ref.shape[0]):
-        for q in range(OV):
-            perm_ref[q * BS:q * BS + half, c * lane:(c + 1) * lane] = chunk_ref[c, pl.ds(q * BS, half, stride=2), :]
-            perm_ref[q * BS + half:(q + 1) * BS, c * lane:(c + 1) * lane] = chunk_ref[
-                c, pl.ds(q * BS + 1, half, stride=2), :
-            ]
-
-    grid = canon_ref[...]
-    grid_hi = grid.astype(jnp.bfloat16)
-    grid_lo = (grid - grid_hi.astype(jnp.float32)).astype(jnp.bfloat16)
-
-    def nn(a, c):
-        return lax.dot_general(a, c, (((1,), (0,)), ((), ())), preferred_element_type=jnp.float32)
-
+
+    def dot(a, c, dims):
+        return lax.dot_general(a, c, (dims, ((), ())), preferred_element_type=jnp.float32)
+
+    grid_hi = hi_ref[...]
+    grid_lo = lo_ref[...]
     dense_hi = dense_hi_ref[...]
-    mixed = nn(dense_hi, grid_hi) + (nn(dense_hi, grid_lo) + nn(dense_lo_ref[...], grid_hi))
+    nn = ((1,), (0,))
+    mixed = dot(dense_hi, grid_hi, nn) + (dot(dense_hi, grid_lo, nn) + dot(dense_lo_ref[...], grid_hi, nn))
     permuted = perm_ref[...]
     density = jnp.sum(permuted * mixed, axis=0, keepdims=True)
     potential = base_ref[...] + density - density * density * density / 6.0
     density_ref[...] = density
     weighted = permuted * (weight_ref[...] * potential)
-    terms = split_dot(weighted, grid, ((1,), (1,)))
+    weighted_hi = weighted.astype(jnp.bfloat16)
+    weighted_lo = (weighted - weighted_hi.astype(jnp.float32)).astype(jnp.bfloat16)
+    nt = ((1,), (1,))
+    terms = dot(weighted_hi, grid_hi, nt) + (dot(weighted_hi, grid_lo, nt) + dot(weighted_lo, grid_hi, nt))
     for q1 in range(OV):
         for q2 in range(OV):
             pair_ref[q1 * OV + q2, :, :BS] = terms[q1 * BS:q1 * BS + half, q2 * BS:(q2 + 1) * BS]
@@ -151,29 +191,27 @@
 def batch_terms(source, pick, tables, tile_values, weights, local_pot):
     batch_count, rows, points = tables.shape
     span = batch_count * points
-    whole = lambda i, s, k: (0, 0)
+    grid_hi, grid_lo, permuted = prep_tables(source, tables)
+    whole = lambda i, k: (0, 0)
     grid_spec = pltpu.PrefetchScalarGridSpec(
-        num_scalar_prefetch=2,
+        num_scalar_prefetch=1,
         grid=(1,),
         in_specs=[
-            pl.BlockSpec(memory_space=pl.ANY),
+            pl.BlockSpec((rows, span), whole),
+            pl.BlockSpec((rows, span), whole),
+            pl.BlockSpec((rows, span), whole),
             pl.BlockSpec(memory_space=pl.ANY),
             pl.BlockSpec((1, span), whole),
             pl.BlockSpec((1, span), whole),
         ],
         out_specs=[
             pl.BlockSpec((1, span), whole),
-            pl.BlockSpec((OV * OV, BS // 2, 2 * BS), lambda i, s, k: (0, 0, 0)),
+            pl.BlockSpec((OV * OV, BS // 2, 2 * BS), lambda i, k: (0, 0, 0)),
         ],
         scratch_shapes=[
-            pltpu.VMEM((rows, span), jnp.float32),
-            pltpu.VMEM((span // (2 * BS), rows, 2 * BS), jnp.float32),
-            pltpu.VMEM((rows, span), jnp.float32),
             pltpu.VMEM((OV * OV, BS // 2, 2 * BS), jnp.float32),
             pltpu.VMEM((rows, rows), jnp.bfloat16),
             pltpu.VMEM((rows, rows), jnp.bfloat16),
-            pltpu.SemaphoreType.DMA((batch_count * OV,)),
-            pltpu.SemaphoreType.DMA((span // (2 * BS) * OV,)),
             pltpu.SemaphoreType.DMA((OV * OV,)),
         ],
     )
@@ -185,9 +223,10 @@
             jax.ShapeDtypeStruct((OV * OV, BS // 2, 2 * BS), jnp.float32),
         ],
     )(
-        source.reshape(-1),
         pick,
-        tables,
+        grid_hi,
+        grid_lo,
+        permuted,
         tile_values,
         weights.reshape(1, span),
         local_pot.reshape(1, span),

time: 101 us -> 98.4 us (0.974)
  waiting for transfers between devices: 34.9 us -> 24.5 us
  Pallas kernels: 28.8 us -> 36.2 us
    pallas_call x0 -> x1, Pallas kernels: none -> 10.5 us  [prep_tables(): pl.pallas_call(prep_kernel, grid_spec=grid_spec, out_shape=[jax.ShapeDtyp...]
    all_to_all x1, waiting for transfers between devices: 13.4 us -> 2.96 us  [body(): lax.all_to_all(spread, 'tiles', 0, 0, tiled=False)]
    pallas_call x1, Pallas kernels: 18.8 us -> 15.7 us  [batch_terms(): pl.pallas_call(batch_kernel, grid_spec=grid_spec, out_shape=[jax.ShapeDty...]
  transfers between devices with their start and end apart: 3 -> 3, of which waited for: 3 -> 3; matrix products, arithmetic and copies ran while one was open for 8% -> 8% of each run, Pallas kernels for 0% -> 11%
where the time goes in v10:
time: 98.4 us; the launch traced here: 97.6 us
  Pallas kernels  36.2 us (37%)
  waiting for transfers between devices  24.5 us (25%)
  starting transfers between devices  15.6 us (16%)
  local copies, waits for them, and re-layouts  15.4 us (16%)
  other arithmetic  5.05 us (5%)
    pallas_call x1, Pallas kernels, batch_terms(): pl.pallas_call(batch_kernel, grid_spec=grid_spec, out_shape=[jax.ShapeDty...  15.7 us
    all_to_all x1, waiting for transfers between devices, body(): matrix = jnp.sum(lax.all_to_all(terms, 'tiles', 0, 0, tiled=False), axis=0)  12 us
    pallas_call x1, Pallas kernels, prep_tables(): pl.pallas_call(prep_kernel, grid_spec=grid_spec, out_shape=[jax.ShapeDtyp...  10.5 us
    pallas_call x1, Pallas kernels, tile_products(): pl.pallas_call(tile_kernel, grid_spec=grid_spec, out_shape=jax.ShapeDtype...  10.1 us
    all_to_all x1, waiting for transfers between devices, body(): owned = jnp.sum(lax.all_to_all(partial, 'tiles', 0, 0, tiled=False), axis=0)  9.6 us
    all_to_all x1, starting transfers between devices, body(): owned = jnp.sum(lax.all_to_all(partial, 'tiles', 0, 0, tiled=False), axis=0)  7.38 us
    all_to_all x1, starting transfers between devices, body(): lax.all_to_all(spread, 'tiles', 0, 0, tiled=False)  4.11 us
    all_to_all x1, starting transfers between devices, body(): matrix = jnp.sum(lax.all_to_all(terms, 'tiles', 0, 0, tiled=False), axis=0)  4.1 us
  transfers between devices with their start and end apart: 3, of which 3 were waited for; matrix products, arithmetic and copies ran while one was open for 8% of the time, Pallas kernels for 11%

profile of v10, /device:TPU:0, one launch (start us, length us, event | category | flops | bytes accessed | tf_op | source)
XLA Modules:
  0.0 97.6 jit_solution(12447273184768249842)
XLA Ops:
  0.6 0.8 copy.16
  1.4 0.7 compare_select_fusion.6
  2.1 0.7 scatter_custom_fusion
  3.3 0.6 reshape.85.pairs_ref
  3.9 1.5 %copy.18.refs_16_ = f32[256,1]{1,0:T(8,128)} copy(f32[256,1]{0,1:T(1,128)} %bitcast.27) | data formatting | bytes 2048 | tf_op jit(solution)/shard_map/reshape | solution.py:56
  5.4 10.1 %shard_map.105 = f32[32,64,64]{2,1,0:T(8,128)} custom-call(s32[64]{0:T(128)} %reshape.85.pairs_ref, f32[256,16384]{1,0:T(8,128)} %refs_15_.1, f32[256,16384]{1,0:T(8,128)} %refs_15_.1, f32[256,16384]{1,0:T(8,128)} %refs_15_.1, f32[256,16384]{1,0:T(8,128)} %refs_15_.1, f32[256,16384]{1,0:T(8,128)} %refs_15_.1, f32[256,16384]{1,0:T(8,128)} %refs_15_.1, ...), custom_call_target="tpu_custom_call" | custom-call | tf_op jit(solution)/shard_map/pallas_call | solution.py:52
  15.5 2.2 %reshape.87 = f32[16,2,32,128]{3,2,1,0:T(8,128)} reshape(f32[32,64,64]{2,1,0:T(8,128)} %shard_map.105) | data formatting | bytes 1048576 | tf_op jit(solution)/shard_map/reshape | solution.py:252
  17.7 7.4 %all-to-all-start = ((f32[16,2,32,128]{3,2,1,0:T(8,128)}), f32[16,2,32,128]{3,2,1,0:T(8,128)S(1)}, u32[]{:S(2)}, u32[]{:S(2)}) async-start(f32[16,2,32,128]{3,2,1,0:T(8,128)} %reshape.87), calls=%async_computation | async-start | bytes 1048576 | tf_op jit(solution)/shard_map/all_to_all | solution.py:253
  25.3 1.0 %scatter_custom_fusion.1 = s32[128]{0:T(128)S(1)} fusion(s32[128]{0:T(128)S(1)} %compare_select_fusion.4, s32[128]{0:T(128)S(1)} %iota.24, s32[]{:T(128)} %constant.9.clone.1), kind=kCustom, calls=%fused_computation.32 | custom fusion | bytes 516 | tf_op jit(solution)/shard_map/scatter | solution.py:260
  26.9 1.0 sort.15
  28.0 0.6 reshape.84.source_ref
  30.0 9.6 %all-to-all-done = f32[16,2,32,128]{3,2,1,0:T(8,128)S(1)} async-done(((f32[16,2,32,128]{3,2,1,0:T(8,128)}), f32[16,2,32,128]{3,2,1,0:T(8,128)S(1)}, u32[]{:S(2)}, u32[]{:S(2)}) %all-to-all-start) | async-done | bytes 524320 | tf_op jit(solution)/shard_map/all_to_all | solution.py:253
  39.6 0.9 broadcast_in_dim.101
  40.5 4.1 %all-to-all-start.1 = ((f32[16,2,32,128]{3,2,1,0:T(8,128)}), f32[16,2,32,128]{3,2,1,0:T(8,128)S(1)}, u32[]{:S(2)}, u32[]{:S(2)}) async-start(f32[16,2,32,128]{3,2,1,0:T(8,128)} %broadcast_in_dim.101), calls=%async_computation.1 | async-start | bytes 1048576 | tf_op jit(solution)/shard_map/all_to_all | solution.py:255
  44.8 10.5 %shard_map.104 = (bf16[512,2048]{1,0:T(8,128)(2,1)}, bf16[512,2048]{1,0:T(8,128)(2,1)}, f32[512,2048]{1,0:T(8,128)}) custom-call(s32[64]{0:T(128)} %reshape.84.source_ref, f32[8,512,256]{2,1,0:T(8,128)} %table_hbm.1), custom_call_target="tpu_custom_call" | custom-call | tf_op jit(solution)/shard_map/pallas_call | solution.py:132
  56.1 3.0 %all-to-all-done.1 = f32[16,2,32,128]{3,2,1,0:T(8,128)S(1)} async-done(((f32[16,2,32,128]{3,2,1,0:T(8,128)}), f32[16,2,32,128]{3,2,1,0:T(8,128)S(1)}, u32[]{:S(2)}, u32[]{:S(2)}) %all-to-all-start.1) | async-done | bytes 524320 | tf_op jit(solution)/shard_map/all_to_all | solution.py:255
  59.1 0.8 copy-done
  59.9 15.7 %shard_map.106 = (f32[1,2048]{1,0:T(1,128)}, f32[64,32,128]{2,1,0:T(8,128)}) custom-call(s32[64]{0:T(128)} %broadcast_select_fusion.1.pick_ref, bf16[512,2048]{1,0:T(8,128)(2,1)} %get-tuple-element.10.hi_ref, bf16[512,2048]{1,0:T(8,128)(2,1)} %get-tuple-element.11.lo_ref, f32[512,2048]{1,0:T(8,128)} %get-tuple-element.12.perm_ref, f32[32,32,128]{2,1,0:T(8,128)} %bitcast.19, ...), custom_call_target="tpu_custom_call" | custom-call | tf_op jit(solution)/shard_map/pallas_call | solution.py:218
  75.6 1.8 %gather_fusion.2 = f32[32,32,128]{2,1,0:T(8,128)S(1)} fusion(f32[64,32,128]{2,1,0:T(8,128)} %get-tuple-element.14, s32[1024]{0:T(1024)S(1)} %pad_clamp_fusion), kind=kCustom, calls=%fused_computation.2 | custom fusion | bytes 1048704 | tf_op jit(solution)/shard_map/gather | solution.py:279
  77.4 0.9 broadcast_select_fusion
  78.3 4.1 %all-to-all-start.2 = ((f32[16,2,32,128]{3,2,1,0:T(8,128)}), f32[16,2,32,128]{3,2,1,0:T(8,128)S(1)}, u32[]{:S(2)}, u32[]{:S(2)}) async-start(f32[16,2,32,128]{3,2,1,0:T(8,128)} %broadcast_select_fusion), calls=%async_computation.2 | async-start | bytes 1048576 | tf_op jit(solution)/shard_map/all_to_all | solution.py:282
  82.9 1.4 %reduce.7 = f32[2048]{0:T(1024)S(1)} reduce(f32[1,2048]{1,0:T(1,128)} %get-tuple-element.13, f32[]{:T(128)} %broadcast.85), dimensions={0}, to_apply=%get-tuple-element.13.reduce_sub_computation.3 | reduce | bytes 16388 | tf_op jit(solution)/shard_map/pallas_call | solution.py:218
  84.9 12.0 %all-to-all-done.2 = f32[16,2,32,128]{3,2,1,0:T(8,128)S(1)} async-done(((f32[16,2,32,128]{3,2,1,0:T(8,128)}), f32[16,2,32,128]{3,2,1,0:T(8,128)S(1)}, u32[]{:S(2)}, u32[]{:S(2)}) %all-to-all-start.2) | async-done | bytes 524320 | tf_op jit(solution)/shard_map/all_to_all | solution.py:282
  96.9 0.6 copy.23
  (38 shorter events, 5.0 us)
Async XLA Ops:
  5.4 19.7 %copy-start.3 = (s32[128,8]{0,1:T(8,128)S(1)}, s32[128,8]{0,1:T(8,128)}, u32[]{:S(2)}) copy-start(s32[128,8]{0,1:T(8,128)} %param.13) | copy-start | bytes 12292
  5.4 19.8 %copy-start.4 = (s32[128]{0:T(128)S(1)}, s32[128]{0:T(128)}, u32[]{:S(2)}) copy-start(s32[128]{0:T(128)} %param.14) | copy-start | bytes 1540
  5.4 23.2 %copy-start.1 = (f32[8,256]{1,0:T(8,128)S(1)}, f32[8,256]{1,0:T(8,128)}, u32[]{:S(2)}) copy-start(f32[8,256]{1,0:T(8,128)} %param.17) | copy-start | bytes 24580
  5.4 23.8 %copy-start.2 = (f32[8,256]{1,0:T(8,128)S(1)}, f32[8,256]{1,0:T(8,128)}, u32[]{:S(2)}) copy-start(f32[8,256]{1,0:T(8,128)} %param.16) | copy-start | bytes 24580
  17.7 21.9 %all-to-all-start = ((f32[16,2,32,128]{3,2,1,0:T(8,128)}), f32[16,2,32,128]{3,2,1,0:T(8,128)S(1)}, u32[]{:S(2)}, u32[]{:S(2)}) async-start(f32[16,2,32,128]{3,2,1,0:T(8,128)} %reshape.87), calls=%async_computation | async-start | bytes 1048576 | tf_op jit(solution)/shard_map/all_to_all | solution.py:253
  40.5 18.6 %all-to-all-start.1 = ((f32[16,2,32,128]{3,2,1,0:T(8,128)}), f32[16,2,32,128]{3,2,1,0:T(8,128)S(1)}, u32[]{:S(2)}, u32[]{:S(2)}) async-start(f32[16,2,32,128]{3,2,1,0:T(8,128)} %broadcast_in_dim.101), calls=%async_computation.1 | async-start | bytes 1048576 | tf_op jit(solution)/shard_map/all_to_all | solution.py:255
  59.1 0.8 copy-start
  78.3 18.6 %all-to-all-start.2 = ((f32[16,2,32,128]{3,2,1,0:T(8,128)}), f32[16,2,32,128]{3,2,1,0:T(8,128)S(1)}, u32[]{:S(2)}, u32[]{:S(2)}) async-start(f32[16,2,32,128]{3,2,1,0:T(8,128)} %broadcast_select_fusion), calls=%async_computation.2 | async-start | bytes 1048576 | tf_op jit(solution)/shard_map/all_to_all | solution.py:282

commit v11 on v10

--- a/solution.py
+++ b/solution.py
@@ -141,8 +141,8 @@
 
 
 def batch_kernel(
-    pick_ref, hi_ref, lo_ref, perm_ref, tile_hbm, weight_ref, base_ref,
-    density_ref, pair_ref, stage_ref, dense_hi_ref, dense_lo_ref, tile_sems,
+    pick_ref, code_ref, hi_ref, lo_ref, perm_ref, tile_hbm, weight_ref, base_ref,
+    density_ref, slot_hbm, stage_ref, dense_hi_ref, dense_lo_ref, pair_ref, tile_sems, slot_sems,
 ):
     half = BS // 2
     copies = []
@@ -186,15 +186,31 @@
         for q2 in range(OV):
             pair_ref[q1 * OV + q2, :, :BS] = terms[q1 * BS:q1 * BS + half, q2 * BS:(q2 + 1) * BS]
             pair_ref[q1 * OV + q2, :, BS:] = terms[q1 * BS + half:(q1 + 1) * BS, q2 * BS:(q2 + 1) * BS]
-
-
-def batch_terms(source, pick, tables, tile_values, weights, local_pot):
+    pair_ref[OV * OV] = jnp.zeros(pair_ref.shape[1:], jnp.float32)
+
+    def slot_copy(k):
+        return pltpu.make_async_copy(pair_ref.at[code_ref[k]], slot_hbm.at[k], slot_sems.at[k])
+
+    def start(k, carry):
+        slot_copy(k).start()
+        return carry
+
+    def wait(k, carry):
+        slot_copy(k).wait()
+        return carry
+
+    lax.fori_loop(0, slot_hbm.shape[0], start, 0)
+    lax.fori_loop(0, slot_hbm.shape[0], wait, 0)
+
+
+def batch_terms(source, pick, code, tables, tile_values, weights, local_pot):
     batch_count, rows, points = tables.shape
+    kept_count = code.shape[0]
     span = batch_count * points
     grid_hi, grid_lo, permuted = prep_tables(source, tables)
-    whole = lambda i, k: (0, 0)
+    whole = lambda i, k, c: (0, 0)
     grid_spec = pltpu.PrefetchScalarGridSpec(
-        num_scalar_prefetch=1,
+        num_scalar_prefetch=2,
         grid=(1,),
         in_specs=[
             pl.BlockSpec((rows, span), whole),
@@ -206,13 +222,15 @@
         ],
         out_specs=[
             pl.BlockSpec((1, span), whole),
-            pl.BlockSpec((OV * OV, BS // 2, 2 * BS), lambda i, k: (0, 0, 0)),
+            pl.BlockSpec(memory_space=pl.ANY),
         ],
         scratch_shapes=[
             pltpu.VMEM((OV * OV, BS // 2, 2 * BS), jnp.float32),
             pltpu.VMEM((rows, rows), jnp.bfloat16),
             pltpu.VMEM((rows, rows), jnp.bfloat16),
+            pltpu.VMEM((OV * OV + 1, BS // 2, 2 * BS), jnp.float32),
             pltpu.SemaphoreType.DMA((OV * OV,)),
+            pltpu.SemaphoreType.DMA((kept_count,)),
         ],
     )
     density, pair_tiles = pl.pallas_call(
@@ -220,10 +238,11 @@
         grid_spec=grid_spec,
         out_shape=[
             jax.ShapeDtypeStruct((1, span), jnp.float32),
-            jax.ShapeDtypeStruct((OV * OV, BS // 2, 2 * BS), jnp.float32),
+            jax.ShapeDtypeStruct((kept_count, BS // 2, 2 * BS), jnp.float32),
         ],
     )(
         pick,
+        code,
         grid_hi,
         grid_lo,
         permuted,
@@ -275,8 +294,8 @@
     pick = jnp.where(
         jnp.any(at_pair, axis=1), jnp.sum(jnp.where(at_pair, ladder_kept[None, :], 0), axis=1), -1
     )
-    density, pair_tiles = batch_terms(source, pick, tables, tile_values, weights, local_pot)
-    contrib = jnp.where(present[:, None, None], pair_tiles[pair_code], 0.0)
+    code = jnp.where(present, pair_code, OV * OV)
+    density, contrib = batch_terms(source, pick, code, tables, tile_values, weights, local_pot)
 
     terms = contrib.reshape(devices, owned_count, BS // 2, 2 * BS)
     matrix = jnp.sum(lax.all_to_all(terms, "tiles", 0, 0, tiled=False), axis=0)

time: 98.4 us -> 99.2 us (level)
  local copies, waits for them, and re-layouts: 15.4 us -> 13.5 us
  starting transfers between devices: 15.6 us -> 17.4 us
    all_to_all x1, waiting for transfers between devices: 2.96 us -> 12.7 us  [body(): lax.all_to_all(spread, 'tiles', 0, 0, tiled=False)]
    all_to_all x1, waiting for transfers between devices: 9.6 us -> 0.01 us  [body(): owned = jnp.sum(lax.all_to_all(partial, 'tiles', 0, 0, tiled=False), axis=0)]
    all_to_all x1, starting transfers between devices: 4.11 us -> 5.99 us  [body(): lax.all_to_all(spread, 'tiles', 0, 0, tiled=False)]
    gather x1 -> x0, local copies, waits for them, and re-layouts: 1.8 us -> none  [body(): contrib = jnp.where(present[:, None, None], pair_tiles[pair_code], 0.0)]
  transfers between devices with their start and end apart: 3 -> 3, of which waited for: 3 -> 2; matrix products, arithmetic and copies ran while one was open for 8% -> 9% of each run, Pallas kernels for 11% -> 11%
where the time goes in v11:
time: 99.2 us; the launch traced here: 98.4 us
  Pallas kernels  37 us (37%)
  waiting for transfers between devices  24.7 us (25%)
  starting transfers between devices  17.4 us (18%)
  local copies, waits for them, and re-layouts  13.5 us (14%)
  other arithmetic  4.87 us (5%)
    pallas_call x1, Pallas kernels, batch_terms(): pl.pallas_call(batch_kernel, grid_spec=grid_spec, out_shape=[jax.ShapeDty...  16.5 us
    all_to_all x1, waiting for transfers between devices, body(): lax.all_to_all(spread, 'tiles', 0, 0, tiled=False)  12.7 us
    all_to_all x1, waiting for transfers between devices, body(): matrix = jnp.sum(lax.all_to_all(terms, 'tiles', 0, 0, tiled=False), axis=0)  12 us
    pallas_call x1, Pallas kernels, prep_tables(): pl.pallas_call(prep_kernel, grid_spec=grid_spec, out_shape=[jax.ShapeDtyp...  10.5 us
    pallas_call x1, Pallas kernels, tile_products(): pl.pallas_call(tile_kernel, grid_spec=grid_spec, out_shape=jax.ShapeDtype...  10.1 us
    all_to_all x1, starting transfers between devices, body(): owned = jnp.sum(lax.all_to_all(partial, 'tiles', 0, 0, tiled=False), axis=0)  7.38 us
    all_to_all x1, starting transfers between devices, body(): lax.all_to_all(spread, 'tiles', 0, 0, tiled=False)  5.99 us
    all_to_all x1, starting transfers between devices, body(): matrix = jnp.sum(lax.all_to_all(terms, 'tiles', 0, 0, tiled=False), axis=0)  4.05 us
  transfers between devices with their start and end apart: 3, of which 2 were waited for; matrix products, arithmetic and copies ran while one was open for 9% of the time, Pallas kernels for 11%

profile of v11, /device:TPU:0, one launch (start us, length us, event | category | flops | bytes accessed | tf_op | source)
XLA Modules:
  0.0 98.4 jit_solution(1539703267484273822)
XLA Ops:
  0.6 0.7 compare_select_fusion.5
  1.3 0.7 scatter_custom_fusion
  2.0 0.8 copy.16
  3.3 0.6 reshape.50.pairs_ref
  4.0 1.5 %copy.18.refs_16_ = f32[256,1]{1,0:T(8,128)} copy(f32[256,1]{0,1:T(1,128)} %bitcast.25) | data formatting | bytes 2048 | tf_op jit(solution)/shard_map/reshape | solution.py:56
  5.4 10.1 %shard_map.105 = f32[32,64,64]{2,1,0:T(8,128)} custom-call(s32[64]{0:T(128)} %reshape.50.pairs_ref, f32[256,16384]{1,0:T(8,128)} %refs_15_.1, f32[256,16384]{1,0:T(8,128)} %refs_15_.1, f32[256,16384]{1,0:T(8,128)} %refs_15_.1, f32[256,16384]{1,0:T(8,128)} %refs_15_.1, f32[256,16384]{1,0:T(8,128)} %refs_15_.1, f32[256,16384]{1,0:T(8,128)} %refs_15_.1, ...), custom_call_target="tpu_custom_call" | custom-call | tf_op jit(solution)/shard_map/pallas_call | solution.py:52
  15.5 2.3 %reshape.52 = f32[16,2,32,128]{3,2,1,0:T(8,128)} reshape(f32[32,64,64]{2,1,0:T(8,128)} %shard_map.105) | data formatting | bytes 1048576 | tf_op jit(solution)/shard_map/reshape | solution.py:271
  17.8 7.4 %all-to-all-start = ((f32[16,2,32,128]{3,2,1,0:T(8,128)}), f32[16,2,32,128]{3,2,1,0:T(8,128)S(1)}, u32[]{:S(2)}, u32[]{:S(2)}) async-start(f32[16,2,32,128]{3,2,1,0:T(8,128)} %reshape.52), calls=%async_computation | async-start | bytes 1048576 | tf_op jit(solution)/shard_map/all_to_all | solution.py:272
  25.2 0.6 copy.19
  25.8 0.6 copy.20
  26.5 1.0 scatter_custom_fusion.1
  28.2 1.0 %sort.15 = (s32[8]{0:T(128)S(1)}, s32[8]{0:T(128)}) sort(s32[8]{0:T(128)S(1)} %slice_bitcast_fusion, s32[8]{0:T(128)S(1)} %iota.25), dimensions={0}, to_apply=%region_2.0 | sort | flops 24 | bytes 128 | tf_op jit(solution)/shard_map/jit(sort)/sort | solution.py:282
  29.3 0.6 reshape.49.source_ref
  29.9 10.5 %shard_map.104 = (bf16[512,2048]{1,0:T(8,128)(2,1)}, bf16[512,2048]{1,0:T(8,128)(2,1)}, f32[512,2048]{1,0:T(8,128)}) custom-call(s32[64]{0:T(128)} %reshape.49.source_ref, f32[8,512,256]{2,1,0:T(8,128)} %table_hbm.1), custom_call_target="tpu_custom_call" | custom-call | tf_op jit(solution)/shard_map/pallas_call | solution.py:132
  40.4 0.9 broadcast_in_dim.92
  41.4 6.0 %all-to-all-start.1 = ((f32[16,2,32,128]{3,2,1,0:T(8,128)}), f32[16,2,32,128]{3,2,1,0:T(8,128)S(1)}, u32[]{:S(2)}, u32[]{:S(2)}) async-start(f32[16,2,32,128]{3,2,1,0:T(8,128)} %broadcast_in_dim.92), calls=%async_computation.1 | async-start | bytes 1048576 | tf_op jit(solution)/shard_map/all_to_all | solution.py:274
  49.1 12.7 %all-to-all-done.1 = f32[16,2,32,128]{3,2,1,0:T(8,128)S(1)} async-done(((f32[16,2,32,128]{3,2,1,0:T(8,128)}), f32[16,2,32,128]{3,2,1,0:T(8,128)S(1)}, u32[]{:S(2)}, u32[]{:S(2)}) %all-to-all-start.1) | async-done | bytes 524320 | tf_op jit(solution)/shard_map/all_to_all | solution.py:274
  61.8 0.8 copy-done
  62.7 16.5 %shard_map.106 = (f32[1,2048]{1,0:T(1,128)}, f32[32,32,128]{2,1,0:T(8,128)}) custom-call(s32[64]{0:T(128)} %broadcast_select_fusion.1.pick_ref, s32[32]{0:T(128)} %get-tuple-element.21.code_ref, bf16[512,2048]{1,0:T(8,128)(2,1)} %get-tuple-element.10.hi_ref, bf16[512,2048]{1,0:T(8,128)(2,1)} %get-tuple-element.11.lo_ref, ...), custom_call_target="tpu_custom_call" | custom-call | tf_op jit(solution)/shard_map/pallas_call | solution.py:236
  79.2 4.0 %all-to-all-start.2 = ((f32[16,2,32,128]{3,2,1,0:T(8,128)}), f32[16,2,32,128]{3,2,1,0:T(8,128)S(1)}, u32[]{:S(2)}, u32[]{:S(2)}) async-start(f32[16,2,32,128]{3,2,1,0:T(8,128)} %bitcast.18), calls=%async_computation.2 | async-start | bytes 1048576 | tf_op jit(solution)/shard_map/all_to_all | solution.py:301
  83.7 1.4 %reduce.7 = f32[2048]{0:T(1024)S(1)} reduce(f32[1,2048]{1,0:T(1,128)} %get-tuple-element.13, f32[]{:T(128)} %broadcast.52), dimensions={0}, to_apply=%get-tuple-element.13.reduce_sub_computation.3 | reduce | bytes 16388 | tf_op jit(solution)/shard_map/pallas_call | solution.py:236
  85.1 0.6 reshape.56
  85.7 12.0 %all-to-all-done.2 = f32[16,2,32,128]{3,2,1,0:T(8,128)S(1)} async-done(((f32[16,2,32,128]{3,2,1,0:T(8,128)}), f32[16,2,32,128]{3,2,1,0:T(8,128)S(1)}, u32[]{:S(2)}, u32[]{:S(2)}) %all-to-all-start.2) | async-done | bytes 524320 | tf_op jit(solution)/shard_map/all_to_all | solution.py:301
  97.7 0.6 copy.23
  (33 shorter events, 3.7 us)
Async XLA Ops:
  5.4 19.7 %copy-start.1 = (f32[8,256]{1,0:T(8,128)S(1)}, f32[8,256]{1,0:T(8,128)}, u32[]{:S(2)}) copy-start(f32[8,256]{1,0:T(8,128)} %param.16) | copy-start | bytes 24580
  5.4 20.4 %copy-start.2 = (f32[8,256]{1,0:T(8,128)S(1)}, f32[8,256]{1,0:T(8,128)}, u32[]{:S(2)}) copy-start(f32[8,256]{1,0:T(8,128)} %param.17) | copy-start | bytes 24580
  5.4 21.0 %copy-start.3 = (s32[128,8]{0,1:T(8,128)S(1)}, s32[128,8]{0,1:T(8,128)}, u32[]{:S(2)}) copy-start(s32[128,8]{0,1:T(8,128)} %param.13) | copy-start | bytes 12292
  5.4 21.1 %copy-start.4 = (s32[128]{0:T(128)S(1)}, s32[128]{0:T(128)}, u32[]{:S(2)}) copy-start(s32[128]{0:T(128)} %param.14) | copy-start | bytes 1540
  17.8 22.6 %all-to-all-start = ((f32[16,2,32,128]{3,2,1,0:T(8,128)}), f32[16,2,32,128]{3,2,1,0:T(8,128)S(1)}, u32[]{:S(2)}, u32[]{:S(2)}) async-start(f32[16,2,32,128]{3,2,1,0:T(8,128)} %reshape.52), calls=%async_computation | async-start | bytes 1048576 | tf_op jit(solution)/shard_map/all_to_all | solution.py:272
  41.4 20.5 %all-to-all-start.1 = ((f32[16,2,32,128]{3,2,1,0:T(8,128)}), f32[16,2,32,128]{3,2,1,0:T(8,128)S(1)}, u32[]{:S(2)}, u32[]{:S(2)}) async-start(f32[16,2,32,128]{3,2,1,0:T(8,128)} %broadcast_in_dim.92), calls=%async_computation.1 | async-start | bytes 1048576 | tf_op jit(solution)/shard_map/all_to_all | solution.py:274
  61.8 0.8 copy-start
  79.2 18.5 %all-to-all-start.2 = ((f32[16,2,32,128]{3,2,1,0:T(8,128)}), f32[16,2,32,128]{3,2,1,0:T(8,128)S(1)}, u32[]{:S(2)}, u32[]{:S(2)}) async-start(f32[16,2,32,128]{3,2,1,0:T(8,128)} %bitcast.18), calls=%async_computation.2 | async-start | bytes 1048576 | tf_op jit(solution)/shard_map/all_to_all | solution.py:301

commit v12 on v10

--- a/solution.py
+++ b/solution.py
@@ -14,7 +14,10 @@
     occ_ref = refs[2 * group]
     out_ref = refs[2 * group + 1]
     k = pl.program_id(0)
-    occ = occ_ref[...]
+    occ_row = occ_ref[...]
+    size = occ_row.shape[1]
+    diagonal = lax.broadcasted_iota(jnp.int32, (size, size), 0) == lax.broadcasted_iota(jnp.int32, (size, size), 1)
+    occ = jnp.sum(jnp.where(diagonal, occ_row, 0.0), axis=1, keepdims=True)
     for i in range(group):
         row_block = pairs_ref[2 * (group * k + i)]
         col_block = pairs_ref[2 * (group * k + i) + 1]
@@ -34,7 +37,7 @@
 def tile_products(coeffs, occupation, pairs):
     state_count = coeffs.shape[0]
     kept_count = pairs.shape[0]
-    group = next(g for g in (8, 4, 2, 1) if kept_count % g == 0)
+    group = next(g for g in (16, 8, 4, 2, 1) if kept_count % g == 0)
 
     def block_of(i, side):
         return pl.BlockSpec(
@@ -46,14 +49,14 @@
         grid=(kept_count // group,),
         in_specs=[block_of(i, 0) for i in range(group)]
         + [block_of(i, 1) for i in range(group)]
-        + [pl.BlockSpec((state_count, 1), lambda k, p: (0, 0))],
+        + [pl.BlockSpec((1, state_count), lambda k, p: (0, 0))],
         out_specs=pl.BlockSpec((group, BS, BS), lambda k, p: (k, 0, 0)),
     )
     return pl.pallas_call(
         tile_kernel,
         grid_spec=grid_spec,
         out_shape=jax.ShapeDtypeStruct((kept_count, BS, BS), jnp.float32),
-    )(pairs.reshape(-1), *([coeffs] * (2 * group)), occupation.reshape(state_count, 1))
+    )(pairs.reshape(-1), *([coeffs] * (2 * group)), occupation.reshape(1, state_count))
 
 
 def split_dot(left, right, dims):

time: 98.4 us -> 97 us (0.986)
    reshape x1 -> x0, local copies, waits for them, and re-layouts: 1.46 us -> none  [tile_products(): occupation.reshape(state_count, 1)]
    unnamed x15 -> x17, local copies, waits for them, and re-layouts: 3.53 us -> 3.53 us
  transfers between devices with their start and end apart: 3 -> 3, of which waited for: 3 -> 3; matrix products, arithmetic and copies ran while one was open for 8% -> 9% of each run, Pallas kernels for 11% -> 11%
where the time goes in v12:
time: 97 us; the launch traced here: 96.1 us
  Pallas kernels  36.5 us (38%)
  waiting for transfers between devices  23.7 us (24%)
  starting transfers between devices  15.2 us (16%)
  local copies, waits for them, and re-layouts  14.7 us (15%)
  other arithmetic  5.05 us (5%)
    pallas_call x1, Pallas kernels, batch_terms(): pl.pallas_call(batch_kernel, grid_spec=grid_spec, out_shape=[jax.ShapeDty...  15.7 us
    all_to_all x1, waiting for transfers between devices, body(): matrix = jnp.sum(lax.all_to_all(terms, 'tiles', 0, 0, tiled=False), axis=0)  12 us
    pallas_call x1, Pallas kernels, prep_tables(): pl.pallas_call(prep_kernel, grid_spec=grid_spec, out_shape=[jax.ShapeDtyp...  10.5 us
    pallas_call x1, Pallas kernels, tile_products(): pl.pallas_call(tile_kernel, grid_spec=grid_spec, out_shape=jax.ShapeDtype...  10.3 us
    all_to_all x1, waiting for transfers between devices, body(): owned = jnp.sum(lax.all_to_all(partial, 'tiles', 0, 0, tiled=False), axis=0)  8.81 us
    all_to_all x1, starting transfers between devices, body(): owned = jnp.sum(lax.all_to_all(partial, 'tiles', 0, 0, tiled=False), axis=0)  7.38 us
    all_to_all x1, starting transfers between devices, body(): lax.all_to_all(spread, 'tiles', 0, 0, tiled=False)  4.11 us
    all_to_all x1, starting transfers between devices, body(): matrix = jnp.sum(lax.all_to_all(terms, 'tiles', 0, 0, tiled=False), axis=0)  3.76 us
  transfers between devices with their start and end apart: 3, of which 3 were waited for; matrix products, arithmetic and copies ran while one was open for 9% of the time, Pallas kernels for 11%

profile of v12, /device:TPU:0, one launch (start us, length us, event | category | flops | bytes accessed | tf_op | source)
XLA Modules:
  0.0 96.1 jit_solution(13130401481067264214)
XLA Ops:
  0.6 0.8 copy.15
  1.4 0.7 compare_select_fusion.6
  2.1 0.7 scatter_custom_fusion
  3.3 0.6 reshape.85.pairs_ref
  4.0 10.3 %shard_map.105 = f32[32,64,64]{2,1,0:T(8,128)} custom-call(s32[64]{0:T(128)} %reshape.85.pairs_ref, f32[256,16384]{1,0:T(8,128)} %refs_31_.1, f32[256,16384]{1,0:T(8,128)} %refs_31_.1, f32[256,16384]{1,0:T(8,128)} %refs_31_.1, f32[256,16384]{1,0:T(8,128)} %refs_31_.1, f32[256,16384]{1,0:T(8,128)} %refs_31_.1, f32[256,16384]{1,0:T(8,128)} %refs_31_.1, ...), custom_call_target="tpu_custom_call" | custom-call | tf_op jit(solution)/shard_map/pallas_call | solution.py:55
  14.3 2.2 %reshape.87 = f32[16,2,32,128]{3,2,1,0:T(8,128)} reshape(f32[32,64,64]{2,1,0:T(8,128)} %shard_map.105) | data formatting | bytes 1048576 | tf_op jit(solution)/shard_map/reshape | solution.py:255
  16.5 7.4 %all-to-all-start = ((f32[16,2,32,128]{3,2,1,0:T(8,128)}), f32[16,2,32,128]{3,2,1,0:T(8,128)S(1)}, u32[]{:S(2)}, u32[]{:S(2)}) async-start(f32[16,2,32,128]{3,2,1,0:T(8,128)} %reshape.87), calls=%async_computation | async-start | bytes 1048576 | tf_op jit(solution)/shard_map/all_to_all | solution.py:256
  24.1 1.0 %scatter_custom_fusion.1 = s32[128]{0:T(128)S(1)} fusion(s32[128]{0:T(128)S(1)} %compare_select_fusion.4, s32[128]{0:T(128)S(1)} %iota.24, s32[]{:T(128)} %constant.9.clone.1), kind=kCustom, calls=%fused_computation.32 | custom fusion | bytes 516 | tf_op jit(solution)/shard_map/scatter | solution.py:263
  25.7 1.0 %sort.15 = (s32[8]{0:T(128)S(1)}, s32[8]{0:T(128)}) sort(s32[8]{0:T(128)S(1)} %slice_bitcast_fusion, s32[8]{0:T(128)S(1)} %iota.25), dimensions={0}, to_apply=%region_2.0 | sort | flops 24 | bytes 128 | tf_op jit(solution)/shard_map/jit(sort)/sort | solution.py:266
  26.8 0.6 reshape.84.source_ref
  28.6 1.0 %slice_reduce_fusion.1 = (s32[32]{0:T(128)S(1)}, s32[32]{0:T(128)S(1)}) fusion(s32[32,2]{1,0:T(8,128)} %copy-done.1), kind=kLoop, calls=%fused_computation.9 | loop fusion | bytes 512 | tf_op jit(solution)/shard_map/slice | solution.py:270
  29.6 8.8 %all-to-all-done = f32[16,2,32,128]{3,2,1,0:T(8,128)S(1)} async-done(((f32[16,2,32,128]{3,2,1,0:T(8,128)}), f32[16,2,32,128]{3,2,1,0:T(8,128)S(1)}, u32[]{:S(2)}, u32[]{:S(2)}) %all-to-all-start) | async-done | bytes 524320 | tf_op jit(solution)/shard_map/all_to_all | solution.py:256
  38.4 0.9 broadcast_in_dim.101
  39.3 4.1 %all-to-all-start.1 = ((f32[16,2,32,128]{3,2,1,0:T(8,128)}), f32[16,2,32,128]{3,2,1,0:T(8,128)S(1)}, u32[]{:S(2)}, u32[]{:S(2)}) async-start(f32[16,2,32,128]{3,2,1,0:T(8,128)} %broadcast_in_dim.101), calls=%async_computation.1 | async-start | bytes 1048576 | tf_op jit(solution)/shard_map/all_to_all | solution.py:258
  43.6 10.5 %shard_map.104 = (bf16[512,2048]{1,0:T(8,128)(2,1)}, bf16[512,2048]{1,0:T(8,128)(2,1)}, f32[512,2048]{1,0:T(8,128)}) custom-call(s32[64]{0:T(128)} %reshape.84.source_ref, f32[8,512,256]{2,1,0:T(8,128)} %table_hbm.1), custom_call_target="tpu_custom_call" | custom-call | tf_op jit(solution)/shard_map/pallas_call | solution.py:135
  55.0 2.9 %all-to-all-done.1 = f32[16,2,32,128]{3,2,1,0:T(8,128)S(1)} async-done(((f32[16,2,32,128]{3,2,1,0:T(8,128)}), f32[16,2,32,128]{3,2,1,0:T(8,128)S(1)}, u32[]{:S(2)}, u32[]{:S(2)}) %all-to-all-start.1) | async-done | bytes 524320 | tf_op jit(solution)/shard_map/all_to_all | solution.py:258
  57.9 0.8 copy-done
  58.7 15.7 %shard_map.106 = (f32[1,2048]{1,0:T(1,128)}, f32[64,32,128]{2,1,0:T(8,128)}) custom-call(s32[64]{0:T(128)} %broadcast_select_fusion.1.pick_ref, bf16[512,2048]{1,0:T(8,128)(2,1)} %get-tuple-element.10.hi_ref, bf16[512,2048]{1,0:T(8,128)(2,1)} %get-tuple-element.11.lo_ref, f32[512,2048]{1,0:T(8,128)} %get-tuple-element.12.perm_ref, f32[32,32,128]{2,1,0:T(8,128)} %bitcast.19, ...), custom_call_target="tpu_custom_call" | custom-call | tf_op jit(solution)/shard_map/pallas_call | solution.py:221
  74.4 1.8 %gather_fusion.2 = f32[32,32,128]{2,1,0:T(8,128)S(1)} fusion(f32[64,32,128]{2,1,0:T(8,128)} %get-tuple-element.14, s32[1024]{0:T(1024)S(1)} %pad_clamp_fusion), kind=kCustom, calls=%fused_computation.2 | custom fusion | bytes 1048704 | tf_op jit(solution)/shard_map/gather | solution.py:282
  76.3 0.9 broadcast_select_fusion
  77.2 3.8 %all-to-all-start.2 = ((f32[16,2,32,128]{3,2,1,0:T(8,128)}), f32[16,2,32,128]{3,2,1,0:T(8,128)S(1)}, u32[]{:S(2)}, u32[]{:S(2)}) async-start(f32[16,2,32,128]{3,2,1,0:T(8,128)} %broadcast_select_fusion), calls=%async_computation.2 | async-start | bytes 1048576 | tf_op jit(solution)/shard_map/all_to_all | solution.py:285
  81.4 1.4 %reduce.7 = f32[2048]{0:T(1024)S(1)} reduce(f32[1,2048]{1,0:T(1,128)} %get-tuple-element.13, f32[]{:T(128)} %broadcast.85), dimensions={0}, to_apply=%get-tuple-element.13.reduce_sub_computation.3 | reduce | bytes 16388 | tf_op jit(solution)/shard_map/pallas_call | solution.py:221
  83.4 12.0 %all-to-all-done.2 = f32[16,2,32,128]{3,2,1,0:T(8,128)S(1)} async-done(((f32[16,2,32,128]{3,2,1,0:T(8,128)}), f32[16,2,32,128]{3,2,1,0:T(8,128)S(1)}, u32[]{:S(2)}, u32[]{:S(2)}) %all-to-all-start.2) | async-done | bytes 524320 | tf_op jit(solution)/shard_map/all_to_all | solution.py:285
  95.4 0.6 copy.21
  (39 shorter events, 4.9 us)
Async XLA Ops:
  3.3 11.0 %copy-start.1 = (s32[32,2]{1,0:T(8,128)}, s32[32,2]{1,0:T(8,128)S(1)}, u32[]{:S(2)}) copy-start(s32[32,2]{1,0:T(8,128)S(1)} %gather_fusion) | copy-start | bytes 772
  4.0 20.0 %copy-start.4 = (s32[128,8]{0,1:T(8,128)S(1)}, s32[128,8]{0,1:T(8,128)}, u32[]{:S(2)}) copy-start(s32[128,8]{0,1:T(8,128)} %param.13) | copy-start | bytes 12292
  4.0 20.1 %copy-start.5 = (s32[128]{0:T(128)S(1)}, s32[128]{0:T(128)}, u32[]{:S(2)}) copy-start(s32[128]{0:T(128)} %param.14) | copy-start | bytes 1540
  4.0 23.4 %copy-start.2 = (f32[8,256]{1,0:T(8,128)S(1)}, f32[8,256]{1,0:T(8,128)}, u32[]{:S(2)}) copy-start(f32[8,256]{1,0:T(8,128)} %param.17) | copy-start | bytes 24580
  4.0 24.0 %copy-start.3 = (f32[8,256]{1,0:T(8,128)S(1)}, f32[8,256]{1,0:T(8,128)}, u32[]{:S(2)}) copy-start(f32[8,256]{1,0:T(8,128)} %param.16) | copy-start | bytes 24580
  16.5 21.9 %all-to-all-start = ((f32[16,2,32,128]{3,2,1,0:T(8,128)}), f32[16,2,32,128]{3,2,1,0:T(8,128)S(1)}, u32[]{:S(2)}, u32[]{:S(2)}) async-start(f32[16,2,32,128]{3,2,1,0:T(8,128)} %reshape.87), calls=%async_computation | async-start | bytes 1048576 | tf_op jit(solution)/shard_map/all_to_all | solution.py:256
  39.3 18.6 %all-to-all-start.1 = ((f32[16,2,32,128]{3,2,1,0:T(8,128)}), f32[16,2,32,128]{3,2,1,0:T(8,128)S(1)}, u32[]{:S(2)}, u32[]{:S(2)}) async-start(f32[16,2,32,128]{3,2,1,0:T(8,128)} %broadcast_in_dim.101), calls=%async_computation.1 | async-start | bytes 1048576 | tf_op jit(solution)/shard_map/all_to_all | solution.py:258
  57.9 0.8 copy-start
  77.2 18.2 %all-to-all-start.2 = ((f32[16,2,32,128]{3,2,1,0:T(8,128)}), f32[16,2,32,128]{3,2,1,0:T(8,128)S(1)}, u32[]{:S(2)}, u32[]{:S(2)}) async-start(f32[16,2,32,128]{3,2,1,0:T(8,128)} %broadcast_select_fusion), calls=%async_computation.2 | async-start | bytes 1048576 | tf_op jit(solution)/shard_map/all_to_all | solution.py:285

commit v13 on v12

--- a/solution.py
+++ b/solution.py
@@ -144,10 +144,12 @@
 
 
 def batch_kernel(
-    pick_ref, hi_ref, lo_ref, perm_ref, tile_hbm, weight_ref, base_ref,
-    density_ref, pair_ref, stage_ref, dense_hi_ref, dense_lo_ref, tile_sems,
+    pick_ref, hi_ref, lo_ref, perm_hbm, tile_hbm, weight_ref, base_ref,
+    density_ref, pair_ref, stage_ref, dense_hi_ref, dense_lo_ref, perm_ref, tile_sems, perm_sem,
 ):
     half = BS // 2
+    perm_copy = pltpu.make_async_copy(perm_hbm, perm_ref, perm_sem.at[0])
+    perm_copy.start()
     copies = []
     for p in range(OV * OV):
         copy = pltpu.make_async_copy(
@@ -176,6 +178,7 @@
     dense_hi = dense_hi_ref[...]
     nn = ((1,), (0,))
     mixed = dot(dense_hi, grid_hi, nn) + (dot(dense_hi, grid_lo, nn) + dot(dense_lo_ref[...], grid_hi, nn))
+    perm_copy.wait()
     permuted = perm_ref[...]
     density = jnp.sum(permuted * mixed, axis=0, keepdims=True)
     potential = base_ref[...] + density - density * density * density / 6.0
@@ -202,7 +205,7 @@
         in_specs=[
             pl.BlockSpec((rows, span), whole),
             pl.BlockSpec((rows, span), whole),
-            pl.BlockSpec((rows, span), whole),
+            pl.BlockSpec(memory_space=pl.ANY),
             pl.BlockSpec(memory_space=pl.ANY),
             pl.BlockSpec((1, span), whole),
             pl.BlockSpec((1, span), whole),
@@ -215,7 +218,9 @@
             pltpu.VMEM((OV * OV, BS // 2, 2 * BS), jnp.float32),
             pltpu.VMEM((rows, rows), jnp.bfloat16),
             pltpu.VMEM((rows, rows), jnp.bfloat16),
+            pltpu.VMEM((rows, span), jnp.float32),
             pltpu.SemaphoreType.DMA((OV * OV,)),
+            pltpu.SemaphoreType.DMA((1,)),
         ],
     )
     density, pair_tiles = pl.pallas_call(

time: 97 us -> 97.3 us (level)
  no operation moved by 1% of the time
where the time goes in v13:
time: 97.3 us; the launch traced here: 96.6 us
  Pallas kernels  36.8 us (38%)
  waiting for transfers between devices  23.8 us (24%)
  starting transfers between devices  15.4 us (16%)
  local copies, waits for them, and re-layouts  14.7 us (15%)
  other arithmetic  5.05 us (5%)
    pallas_call x1, Pallas kernels, batch_terms(): pl.pallas_call(batch_kernel, grid_spec=grid_spec, out_shape=[jax.ShapeDty...  16.4 us
    all_to_all x1, waiting for transfers between devices, body(): matrix = jnp.sum(lax.all_to_all(terms, 'tiles', 0, 0, tiled=False), axis=0)  12 us
    pallas_call x1, Pallas kernels, prep_tables(): pl.pallas_call(prep_kernel, grid_spec=grid_spec, out_shape=[jax.ShapeDtyp...  10.5 us
    pallas_call x1, Pallas kernels, tile_products(): pl.pallas_call(tile_kernel, grid_spec=grid_spec, out_shape=jax.ShapeDtype...  9.99 us
    all_to_all x1, waiting for transfers between devices, body(): owned = jnp.sum(lax.all_to_all(partial, 'tiles', 0, 0, tiled=False), axis=0)  8.81 us
    all_to_all x1, starting transfers between devices, body(): owned = jnp.sum(lax.all_to_all(partial, 'tiles', 0, 0, tiled=False), axis=0)  7.39 us
    all_to_all x1, starting transfers between devices, body(): lax.all_to_all(spread, 'tiles', 0, 0, tiled=False)  4.11 us
    all_to_all x1, starting transfers between devices, body(): matrix = jnp.sum(lax.all_to_all(terms, 'tiles', 0, 0, tiled=False), axis=0)  3.95 us
  transfers between devices with their start and end apart: 3, of which 3 were waited for; matrix products, arithmetic and copies ran while one was open for 9% of the time, Pallas kernels for 11%

profile of v13, /device:TPU:0, one launch (start us, length us, event | category | flops | bytes accessed | tf_op | source)
XLA Modules:
  0.0 96.6 jit_solution(8181222333712574656)
XLA Ops:
  0.6 0.8 copy.15
  1.4 0.7 compare_select_fusion.6
  2.1 0.7 scatter_custom_fusion
  3.3 0.6 reshape.85.pairs_ref
  4.0 10.0 %shard_map.105 = f32[32,64,64]{2,1,0:T(8,128)} custom-call(s32[64]{0:T(128)} %reshape.85.pairs_ref, f32[256,16384]{1,0:T(8,128)} %refs_31_.1, f32[256,16384]{1,0:T(8,128)} %refs_31_.1, f32[256,16384]{1,0:T(8,128)} %refs_31_.1, f32[256,16384]{1,0:T(8,128)} %refs_31_.1, f32[256,16384]{1,0:T(8,128)} %refs_31_.1, f32[256,16384]{1,0:T(8,128)} %refs_31_.1, ...), custom_call_target="tpu_custom_call" | custom-call | tf_op jit(solution)/shard_map/pallas_call | solution.py:55
  14.0 2.2 %reshape.87 = f32[16,2,32,128]{3,2,1,0:T(8,128)} reshape(f32[32,64,64]{2,1,0:T(8,128)} %shard_map.105) | data formatting | bytes 1048576 | tf_op jit(solution)/shard_map/reshape | solution.py:260
  16.2 7.4 %all-to-all-start = ((f32[16,2,32,128]{3,2,1,0:T(8,128)}), f32[16,2,32,128]{3,2,1,0:T(8,128)S(1)}, u32[]{:S(2)}, u32[]{:S(2)}) async-start(f32[16,2,32,128]{3,2,1,0:T(8,128)} %reshape.87), calls=%async_computation | async-start | bytes 1048576 | tf_op jit(solution)/shard_map/all_to_all | solution.py:261
  23.8 1.0 %scatter_custom_fusion.1 = s32[128]{0:T(128)S(1)} fusion(s32[128]{0:T(128)S(1)} %compare_select_fusion.4, s32[128]{0:T(128)S(1)} %iota.24, s32[]{:T(128)} %constant.9.clone.1), kind=kCustom, calls=%fused_computation.32 | custom fusion | bytes 516 | tf_op jit(solution)/shard_map/scatter | solution.py:268
  25.4 1.0 sort.15
  26.5 0.6 reshape.84.source_ref
  28.3 1.0 %slice_reduce_fusion.1 = (s32[32]{0:T(128)S(1)}, s32[32]{0:T(128)S(1)}) fusion(s32[32,2]{1,0:T(8,128)} %copy-done.1), kind=kLoop, calls=%fused_computation.9 | loop fusion | bytes 512 | tf_op jit(solution)/shard_map/slice | solution.py:275
  29.3 8.8 %all-to-all-done = f32[16,2,32,128]{3,2,1,0:T(8,128)S(1)} async-done(((f32[16,2,32,128]{3,2,1,0:T(8,128)}), f32[16,2,32,128]{3,2,1,0:T(8,128)S(1)}, u32[]{:S(2)}, u32[]{:S(2)}) %all-to-all-start) | async-done | bytes 524320 | tf_op jit(solution)/shard_map/all_to_all | solution.py:261
  38.1 0.9 broadcast_in_dim.101
  39.0 4.1 %all-to-all-start.1 = ((f32[16,2,32,128]{3,2,1,0:T(8,128)}), f32[16,2,32,128]{3,2,1,0:T(8,128)S(1)}, u32[]{:S(2)}, u32[]{:S(2)}) async-start(f32[16,2,32,128]{3,2,1,0:T(8,128)} %broadcast_in_dim.101), calls=%async_computation.1 | async-start | bytes 1048576 | tf_op jit(solution)/shard_map/all_to_all | solution.py:263
  43.3 10.5 %shard_map.104 = (bf16[512,2048]{1,0:T(8,128)(2,1)}, bf16[512,2048]{1,0:T(8,128)(2,1)}, f32[512,2048]{1,0:T(8,128)}) custom-call(s32[64]{0:T(128)} %reshape.84.source_ref, f32[8,512,256]{2,1,0:T(8,128)} %table_hbm.1), custom_call_target="tpu_custom_call" | custom-call | tf_op jit(solution)/shard_map/pallas_call | solution.py:135
  54.6 3.0 %all-to-all-done.1 = f32[16,2,32,128]{3,2,1,0:T(8,128)S(1)} async-done(((f32[16,2,32,128]{3,2,1,0:T(8,128)}), f32[16,2,32,128]{3,2,1,0:T(8,128)S(1)}, u32[]{:S(2)}, u32[]{:S(2)}) %all-to-all-start.1) | async-done | bytes 524320 | tf_op jit(solution)/shard_map/all_to_all | solution.py:263
  57.6 0.8 copy-done
  58.4 16.4 %shard_map.106 = (f32[1,2048]{1,0:T(1,128)}, f32[64,32,128]{2,1,0:T(8,128)}) custom-call(s32[64]{0:T(128)} %broadcast_select_fusion.1.pick_ref, bf16[512,2048]{1,0:T(8,128)(2,1)} %get-tuple-element.10.hi_ref, bf16[512,2048]{1,0:T(8,128)(2,1)} %get-tuple-element.11.lo_ref, f32[512,2048]{1,0:T(8,128)} %get-tuple-element.12.perm_hbm, f32[32,32,128]{2,1,0:T(8,128)} %bitcast.19, ...), custom_call_target="tpu_custom_call" | custom-call | tf_op jit(solution)/shard_map/pallas_call | solution.py:226
  74.8 1.8 %gather_fusion.2 = f32[32,32,128]{2,1,0:T(8,128)S(1)} fusion(f32[64,32,128]{2,1,0:T(8,128)} %get-tuple-element.14, s32[1024]{0:T(1024)S(1)} %pad_clamp_fusion), kind=kCustom, calls=%fused_computation.2 | custom fusion | bytes 1048704 | tf_op jit(solution)/shard_map/gather | solution.py:287
  76.6 0.9 broadcast_select_fusion
  77.5 3.9 %all-to-all-start.2 = ((f32[16,2,32,128]{3,2,1,0:T(8,128)}), f32[16,2,32,128]{3,2,1,0:T(8,128)S(1)}, u32[]{:S(2)}, u32[]{:S(2)}) async-start(f32[16,2,32,128]{3,2,1,0:T(8,128)} %broadcast_select_fusion), calls=%async_computation.2 | async-start | bytes 1048576 | tf_op jit(solution)/shard_map/all_to_all | solution.py:290
  81.9 1.4 %reduce.7 = f32[2048]{0:T(1024)S(1)} reduce(f32[1,2048]{1,0:T(1,128)} %get-tuple-element.13, f32[]{:T(128)} %broadcast.85), dimensions={0}, to_apply=%get-tuple-element.13.reduce_sub_computation.3 | reduce | bytes 16388 | tf_op jit(solution)/shard_map/pallas_call | solution.py:226
  83.9 12.0 %all-to-all-done.2 = f32[16,2,32,128]{3,2,1,0:T(8,128)S(1)} async-done(((f32[16,2,32,128]{3,2,1,0:T(8,128)}), f32[16,2,32,128]{3,2,1,0:T(8,128)S(1)}, u32[]{:S(2)}, u32[]{:S(2)}) %all-to-all-start.2) | async-done | bytes 524320 | tf_op jit(solution)/shard_map/all_to_all | solution.py:290
  95.9 0.6 copy.21
  (39 shorter events, 4.9 us)
Async XLA Ops:
  3.3 10.6 %copy-start.1 = (s32[32,2]{1,0:T(8,128)}, s32[32,2]{1,0:T(8,128)S(1)}, u32[]{:S(2)}) copy-start(s32[32,2]{1,0:T(8,128)S(1)} %gather_fusion) | copy-start | bytes 772
  4.0 19.7 %copy-start.4 = (s32[128,8]{0,1:T(8,128)S(1)}, s32[128,8]{0,1:T(8,128)}, u32[]{:S(2)}) copy-start(s32[128,8]{0,1:T(8,128)} %param.13) | copy-start | bytes 12292
  4.0 19.8 %copy-start.5 = (s32[128]{0:T(128)S(1)}, s32[128]{0:T(128)}, u32[]{:S(2)}) copy-start(s32[128]{0:T(128)} %param.14) | copy-start | bytes 1540
  4.0 23.1 %copy-start.2 = (f32[8,256]{1,0:T(8,128)S(1)}, f32[8,256]{1,0:T(8,128)}, u32[]{:S(2)}) copy-start(f32[8,256]{1,0:T(8,128)} %param.17) | copy-start | bytes 24580
  4.0 23.7 %copy-start.3 = (f32[8,256]{1,0:T(8,128)S(1)}, f32[8,256]{1,0:T(8,128)}, u32[]{:S(2)}) copy-start(f32[8,256]{1,0:T(8,128)} %param.16) | copy-start | bytes 24580
  16.2 21.9 %all-to-all-start = ((f32[16,2,32,128]{3,2,1,0:T(8,128)}), f32[16,2,32,128]{3,2,1,0:T(8,128)S(1)}, u32[]{:S(2)}, u32[]{:S(2)}) async-start(f32[16,2,32,128]{3,2,1,0:T(8,128)} %reshape.87), calls=%async_computation | async-start | bytes 1048576 | tf_op jit(solution)/shard_map/all_to_all | solution.py:261
  39.0 18.6 %all-to-all-start.1 = ((f32[16,2,32,128]{3,2,1,0:T(8,128)}), f32[16,2,32,128]{3,2,1,0:T(8,128)S(1)}, u32[]{:S(2)}, u32[]{:S(2)}) async-start(f32[16,2,32,128]{3,2,1,0:T(8,128)} %broadcast_in_dim.101), calls=%async_computation.1 | async-start | bytes 1048576 | tf_op jit(solution)/shard_map/all_to_all | solution.py:263
  57.6 0.8 copy-start
  77.5 18.4 %all-to-all-start.2 = ((f32[16,2,32,128]{3,2,1,0:T(8,128)}), f32[16,2,32,128]{3,2,1,0:T(8,128)S(1)}, u32[]{:S(2)}, u32[]{:S(2)}) async-start(f32[16,2,32,128]{3,2,1,0:T(8,128)} %broadcast_select_fusion), calls=%async_computation.2 | async-start | bytes 1048576 | tf_op jit(solution)/shard_map/all_to_all | solution.py:290

commit v14 on v12

--- a/solution.py
+++ b/solution.py
@@ -144,8 +144,8 @@
 
 
 def batch_kernel(
-    pick_ref, hi_ref, lo_ref, perm_ref, tile_hbm, weight_ref, base_ref,
-    density_ref, pair_ref, stage_ref, dense_hi_ref, dense_lo_ref, tile_sems,
+    pick_ref, code_ref, hi_ref, lo_ref, perm_ref, tile_hbm, weight_ref, base_ref,
+    density_ref, slot_ref, stage_ref, dense_hi_ref, dense_lo_ref, pair_ref, tile_sems,
 ):
     half = BS // 2
     copies = []
@@ -189,15 +189,23 @@
         for q2 in range(OV):
             pair_ref[q1 * OV + q2, :, :BS] = terms[q1 * BS:q1 * BS + half, q2 * BS:(q2 + 1) * BS]
             pair_ref[q1 * OV + q2, :, BS:] = terms[q1 * BS + half:(q1 + 1) * BS, q2 * BS:(q2 + 1) * BS]
-
-
-def batch_terms(source, pick, tables, tile_values, weights, local_pot):
+    pair_ref[OV * OV] = jnp.zeros(pair_ref.shape[1:], jnp.float32)
+
+    def place(k, carry):
+        slot_ref[k] = pair_ref[code_ref[k]]
+        return carry
+
+    lax.fori_loop(0, slot_ref.shape[0], place, 0)
+
+
+def batch_terms(source, pick, code, tables, tile_values, weights, local_pot):
     batch_count, rows, points = tables.shape
+    kept_count = code.shape[0]
     span = batch_count * points
     grid_hi, grid_lo, permuted = prep_tables(source, tables)
-    whole = lambda i, k: (0, 0)
+    whole = lambda i, k, c: (0, 0)
     grid_spec = pltpu.PrefetchScalarGridSpec(
-        num_scalar_prefetch=1,
+        num_scalar_prefetch=2,
         grid=(1,),
         in_specs=[
             pl.BlockSpec((rows, span), whole),
@@ -209,12 +217,13 @@
         ],
         out_specs=[
             pl.BlockSpec((1, span), whole),
-            pl.BlockSpec((OV * OV, BS // 2, 2 * BS), lambda i, k: (0, 0, 0)),
+            pl.BlockSpec((kept_count, BS // 2, 2 * BS), lambda i, k, c: (0, 0, 0)),
         ],
         scratch_shapes=[
             pltpu.VMEM((OV * OV, BS // 2, 2 * BS), jnp.float32),
             pltpu.VMEM((rows, rows), jnp.bfloat16),
             pltpu.VMEM((rows, rows), jnp.bfloat16),
+            pltpu.VMEM((OV * OV + 1, BS // 2, 2 * BS), jnp.float32),
             pltpu.SemaphoreType.DMA((OV * OV,)),
         ],
     )
@@ -223,10 +232,11 @@
         grid_spec=grid_spec,
         out_shape=[
             jax.ShapeDtypeStruct((1, span), jnp.float32),
-            jax.ShapeDtypeStruct((OV * OV, BS // 2, 2 * BS), jnp.float32),
+            jax.ShapeDtypeStruct((kept_count, BS // 2, 2 * BS), jnp.float32),
         ],
     )(
         pick,
+        code,
         grid_hi,
         grid_lo,
         permuted,
@@ -278,8 +288,10 @@
     pick = jnp.where(
         jnp.any(at_pair, axis=1), jnp.sum(jnp.where(at_pair, ladder_kept[None, :], 0), axis=1), -1
     )
-    density, pair_tiles = batch_terms(source, pick, tables, tile_values, weights, local_pot)
-    contrib = jnp.where(present[:, None, None], pair_tiles[pair_code], 0.0)
+    code = jnp.where(present, pair_code, OV * OV)
+    after = (owned[0, 0, 0] != owned[0, 0, 0]).astype(jnp.int32)
+    source = jnp.minimum(source + after, OV - 1)
+    density, contrib = batch_terms(source, pick, code, tables, tile_values, weights, local_pot)
 
     terms = contrib.reshape(devices, owned_count, BS // 2, 2 * BS)
     matrix = jnp.sum(lax.all_to_all(terms, "tiles", 0, 0, tiled=False), axis=0)

time: 97 us -> 96.2 us (level)
  waiting for transfers between devices: 23.7 us -> 21.4 us
  starting transfers between devices: 15.2 us -> 17.3 us
  local copies, waits for them, and re-layouts: 14.7 us -> 13.3 us
  between operations: 0.81 us -> 2.09 us
    all_to_all x1, waiting for transfers between devices: 2.95 us -> 0.12 us  [body(): lax.all_to_all(spread, 'tiles', 0, 0, tiled=False)]
    all_to_all x1, starting transfers between devices: 3.76 us -> 5.77 us  [body(): matrix = jnp.sum(lax.all_to_all(terms, 'tiles', 0, 0, tiled=False), axis=0)]
    gather x1 -> x0, local copies, waits for them, and re-layouts: 1.8 us -> none  [body(): contrib = jnp.where(present[:, None, None], pair_tiles[pair_code], 0.0)]
  transfers between devices with their start and end apart: 3 -> 3, of which waited for: 3 -> 3; matrix products, arithmetic and copies ran while one was open for 9% -> 11% of each run, Pallas kernels for 11% -> 11%
where the time goes in v14:
time: 96.2 us; the launch traced here: 95.5 us
  Pallas kernels  36.5 us (38%)
  waiting for transfers between devices  21.4 us (22%)
  starting transfers between devices  17.3 us (18%)
  local copies, waits for them, and re-layouts  13.3 us (14%)
  other arithmetic  4.87 us (5%)
  between operations  2.09 us (2%)
    pallas_call x1, Pallas kernels, batch_terms(): pl.pallas_call(batch_kernel, grid_spec=grid_spec, out_shape=[jax.ShapeDty...  15.9 us
    all_to_all x1, waiting for transfers between devices, body(): matrix = jnp.sum(lax.all_to_all(terms, 'tiles', 0, 0, tiled=False), axis=0)  12 us
    pallas_call x1, Pallas kernels, prep_tables(): pl.pallas_call(prep_kernel, grid_spec=grid_spec, out_shape=[jax.ShapeDtyp...  10.5 us
    pallas_call x1, Pallas kernels, tile_products(): pl.pallas_call(tile_kernel, grid_spec=grid_spec, out_shape=jax.ShapeDtype...  10.2 us
    all_to_all x1, waiting for transfers between devices, body(): owned = jnp.sum(lax.all_to_all(partial, 'tiles', 0, 0, tiled=False), axis=0)  9.27 us
    all_to_all x1, starting transfers between devices, body(): owned = jnp.sum(lax.all_to_all(partial, 'tiles', 0, 0, tiled=False), axis=0)  7.39 us
    all_to_all x1, starting transfers between devices, body(): matrix = jnp.sum(lax.all_to_all(terms, 'tiles', 0, 0, tiled=False), axis=0)  5.77 us
    all_to_all x1, starting transfers between devices, body(): lax.all_to_all(spread, 'tiles', 0, 0, tiled=False)  4.11 us
  transfers between devices with their start and end apart: 3, of which 3 were waited for; matrix products, arithmetic and copies ran while one was open for 11% of the time, Pallas kernels for 11%

profile of v14, /device:TPU:0, one launch (start us, length us, event | category | flops | bytes accessed | tf_op | source)
XLA Modules:
  0.0 95.5 jit_solution(13402857094435397875)
XLA Ops:
  0.6 0.8 copy.15
  1.4 0.7 compare_select_fusion.5
  2.1 0.7 scatter_custom_fusion
  3.3 0.6 reshape.55.pairs_ref
  4.0 10.2 %shard_map.104 = f32[32,64,64]{2,1,0:T(8,128)} custom-call(s32[64]{0:T(128)} %reshape.55.pairs_ref, f32[256,16384]{1,0:T(8,128)} %refs_31_.1, f32[256,16384]{1,0:T(8,128)} %refs_31_.1, f32[256,16384]{1,0:T(8,128)} %refs_31_.1, f32[256,16384]{1,0:T(8,128)} %refs_31_.1, f32[256,16384]{1,0:T(8,128)} %refs_31_.1, f32[256,16384]{1,0:T(8,128)} %refs_31_.1, ...), custom_call_target="tpu_custom_call" | custom-call | tf_op jit(solution)/shard_map/pallas_call | solution.py:55
  14.2 2.2 %reshape.57 = f32[16,2,32,128]{3,2,1,0:T(8,128)} reshape(f32[32,64,64]{2,1,0:T(8,128)} %shard_map.104) | data formatting | bytes 1048576 | tf_op jit(solution)/shard_map/reshape | solution.py:265
  16.5 7.4 %all-to-all-start = ((f32[16,2,32,128]{3,2,1,0:T(8,128)}), f32[16,2,32,128]{3,2,1,0:T(8,128)S(1)}, u32[]{:S(2)}, u32[]{:S(2)}) async-start(f32[16,2,32,128]{3,2,1,0:T(8,128)} %reshape.57), calls=%async_computation | async-start | bytes 1048576 | tf_op jit(solution)/shard_map/all_to_all | solution.py:266
  24.0 0.6 copy.18
  24.6 0.6 copy.17
  25.2 1.0 %scatter_custom_fusion.1 = s32[128]{0:T(128)S(1)} fusion(s32[128]{0:T(128)S(1)} %compare_select_fusion.3, s32[128]{0:T(128)S(1)} %iota.24, s32[]{:T(128)} %constant.10.clone.1), kind=kCustom, calls=%fused_computation.29 | custom fusion | bytes 516 | tf_op jit(solution)/shard_map/scatter | solution.py:273
  26.9 1.0 %sort.15 = (s32[8]{0:T(128)S(1)}, s32[8]{0:T(128)}) sort(s32[8]{0:T(128)S(1)} %slice_bitcast_fusion, s32[8]{0:T(128)S(1)} %iota.25), dimensions={0}, to_apply=%region_2.0 | sort | flops 24 | bytes 128 | tf_op jit(solution)/shard_map/jit(sort)/sort | solution.py:276
  27.9 1.0 %slice_reduce_fusion.1 = (s32[32]{0:T(128)S(1)}, s32[32]{0:T(128)S(1)}) fusion(s32[32,2]{1,0:T(8,128)} %copy-done.1), kind=kLoop, calls=%fused_computation.7 | loop fusion | bytes 512 | tf_op jit(solution)/shard_map/slice | solution.py:280
  29.1 9.3 %all-to-all-done = f32[16,2,32,128]{3,2,1,0:T(8,128)S(1)} async-done(((f32[16,2,32,128]{3,2,1,0:T(8,128)}), f32[16,2,32,128]{3,2,1,0:T(8,128)S(1)}, u32[]{:S(2)}, u32[]{:S(2)}) %all-to-all-start) | async-done | bytes 524320 | tf_op jit(solution)/shard_map/all_to_all | solution.py:266
  38.4 0.9 broadcast_in_dim.92
  39.3 4.1 %all-to-all-start.1 = ((f32[16,2,32,128]{3,2,1,0:T(8,128)}), f32[16,2,32,128]{3,2,1,0:T(8,128)S(1)}, u32[]{:S(2)}, u32[]{:S(2)}) async-start(f32[16,2,32,128]{3,2,1,0:T(8,128)} %broadcast_in_dim.92), calls=%async_computation.1 | async-start | bytes 1048576 | tf_op jit(solution)/shard_map/all_to_all | solution.py:268
  46.7 0.6 min.12.source_ref
  47.3 10.5 %shard_map.105 = (bf16[512,2048]{1,0:T(8,128)(2,1)}, bf16[512,2048]{1,0:T(8,128)(2,1)}, f32[512,2048]{1,0:T(8,128)}) custom-call(s32[64]{0:T(128)} %min.12.source_ref, f32[8,512,256]{2,1,0:T(8,128)} %table_hbm.1), custom_call_target="tpu_custom_call" | custom-call | tf_op jit(solution)/shard_map/pallas_call | solution.py:135
  57.8 0.8 copy-done
  58.7 15.9 %shard_map.106 = (f32[1,2048]{1,0:T(1,128)}, f32[32,32,128]{2,1,0:T(8,128)}) custom-call(s32[64]{0:T(128)} %broadcast_select_fusion.1.pick_ref, s32[32]{0:T(128)} %get-tuple-element.21.code_ref, bf16[512,2048]{1,0:T(8,128)(2,1)} %get-tuple-element.10.hi_ref, bf16[512,2048]{1,0:T(8,128)(2,1)} %get-tuple-element.11.lo_ref, ...), custom_call_target="tpu_custom_call" | custom-call | tf_op jit(solution)/shard_map/pallas_call | solution.py:230
  74.5 5.8 %all-to-all-start.2 = ((f32[16,2,32,128]{3,2,1,0:T(8,128)}), f32[16,2,32,128]{3,2,1,0:T(8,128)S(1)}, u32[]{:S(2)}, u32[]{:S(2)}) async-start(f32[16,2,32,128]{3,2,1,0:T(8,128)} %bitcast.17), calls=%async_computation.2 | async-start | bytes 1048576 | tf_op jit(solution)/shard_map/all_to_all | solution.py:297
  80.8 1.4 %reduce.7 = f32[2048]{0:T(1024)S(1)} reduce(f32[1,2048]{1,0:T(1,128)} %get-tuple-element.13, f32[]{:T(128)} %broadcast.58), dimensions={0}, to_apply=%get-tuple-element.13.reduce_sub_computation.3 | reduce | bytes 16388 | tf_op jit(solution)/shard_map/pallas_call | solution.py:230
  82.2 0.6 reshape.61
  82.8 12.0 %all-to-all-done.2 = f32[16,2,32,128]{3,2,1,0:T(8,128)S(1)} async-done(((f32[16,2,32,128]{3,2,1,0:T(8,128)}), f32[16,2,32,128]{3,2,1,0:T(8,128)S(1)}, u32[]{:S(2)}, u32[]{:S(2)}) %all-to-all-start.2) | async-done | bytes 524320 | tf_op jit(solution)/shard_map/all_to_all | solution.py:297
  94.8 0.6 copy.21
  (36 shorter events, 4.2 us)
Async XLA Ops:
  3.3 10.9 %copy-start.1 = (s32[32,2]{1,0:T(8,128)}, s32[32,2]{1,0:T(8,128)S(1)}, u32[]{:S(2)}) copy-start(s32[32,2]{1,0:T(8,128)S(1)} %gather_fusion) | copy-start | bytes 772
  4.0 19.9 %copy-start.4 = (s32[128,8]{0,1:T(8,128)S(1)}, s32[128,8]{0,1:T(8,128)}, u32[]{:S(2)}) copy-start(s32[128,8]{0,1:T(8,128)} %param.13) | copy-start | bytes 12292
  4.0 20.0 %copy-start.2 = (f32[8,256]{1,0:T(8,128)S(1)}, f32[8,256]{1,0:T(8,128)}, u32[]{:S(2)}) copy-start(f32[8,256]{1,0:T(8,128)} %param.17) | copy-start | bytes 24580
  4.0 20.6 %copy-start.3 = (f32[8,256]{1,0:T(8,128)S(1)}, f32[8,256]{1,0:T(8,128)}, u32[]{:S(2)}) copy-start(f32[8,256]{1,0:T(8,128)} %param.16) | copy-start | bytes 24580
  4.0 21.2 %copy-start.5 = (s32[128]{0:T(128)S(1)}, s32[128]{0:T(128)}, u32[]{:S(2)}) copy-start(s32[128]{0:T(128)} %param.14) | copy-start | bytes 1540
  16.5 21.9 %all-to-all-start = ((f32[16,2,32,128]{3,2,1,0:T(8,128)}), f32[16,2,32,128]{3,2,1,0:T(8,128)S(1)}, u32[]{:S(2)}, u32[]{:S(2)}) async-start(f32[16,2,32,128]{3,2,1,0:T(8,128)} %reshape.57), calls=%async_computation | async-start | bytes 1048576 | tf_op jit(solution)/shard_map/all_to_all | solution.py:266
  39.3 18.6 %all-to-all-start.1 = ((f32[16,2,32,128]{3,2,1,0:T(8,128)}), f32[16,2,32,128]{3,2,1,0:T(8,128)S(1)}, u32[]{:S(2)}, u32[]{:S(2)}) async-start(f32[16,2,32,128]{3,2,1,0:T(8,128)} %broadcast_in_dim.92), calls=%async_computation.1 | async-start | bytes 1048576 | tf_op jit(solution)/shard_map/all_to_all | solution.py:268
  57.8 0.8 copy-start
  74.5 20.2 %all-to-all-start.2 = ((f32[16,2,32,128]{3,2,1,0:T(8,128)}), f32[16,2,32,128]{3,2,1,0:T(8,128)S(1)}, u32[]{:S(2)}, u32[]{:S(2)}) async-start(f32[16,2,32,128]{3,2,1,0:T(8,128)} %bitcast.17), calls=%async_computation.2 | async-start | bytes 1048576 | tf_op jit(solution)/shard_map/all_to_all | solution.py:297

commit v15 on v14

--- a/solution.py
+++ b/solution.py
@@ -262,7 +262,12 @@
     ladder_kept = jnp.arange(kept_count, dtype=jnp.int32)
     slot_kept = jnp.zeros((kept_count,), jnp.int32).at[tile_slot].set(ladder_kept)
     pairs = kept_tiles[slot_kept]
-    partial = tile_products(coeffs, occupation, pairs).reshape(devices, owned_count, BS // 2, 2 * BS)
+    group = next(g for g in (16, 8, 4, 2, 1) if kept_count % g == 0)
+    order = jnp.argsort(pairs[:, 0] * block_total + pairs[:, 1])
+    layout = order.reshape(group, kept_count // group).T.reshape(-1)
+    computed = tile_products(coeffs, occupation, pairs[layout])
+    inverse = jnp.zeros((kept_count,), jnp.int32).at[layout].set(ladder_kept)
+    partial = computed[inverse].reshape(devices, owned_count, BS // 2, 2 * BS)
     owned = jnp.sum(lax.all_to_all(partial, "tiles", 0, 0, tiled=False), axis=0)
     spread = jnp.broadcast_to(owned[None], (devices, owned_count, BS // 2, 2 * BS))
     tile_values = lax.all_to_all(spread, "tiles", 0, 0, tiled=False).reshape(

time: 96.2 us -> 101 us (1.050)
  other arithmetic: 4.87 us -> 7.09 us
  local copies, waits for them, and re-layouts: 13.3 us -> 15.4 us
    gather x0 -> x2, local copies, waits for them, and re-layouts: none -> 2.54 us  [the longest x1 1.96 us: body(): partial = computed[inverse].reshape(devices, owned_count, BS // 2, 2 * BS)]
    sort x0 -> x1, other arithmetic: none -> 1.61 us  [body(): order = jnp.argsort(pairs[:, 0] * block_total + pairs[:, 1])]
    reshape x1 -> x3, local copies, waits for them, and re-layouts: 2.25 us -> 1.16 us  [the longest x1 0.99 us: body(): partial = computed[inverse].reshape(devices, owned_count, BS // 2, 2 * BS)]
    unnamed x17 -> x23, local copies, waits for them, and re-layouts: 3.58 us -> 4.18 us
  transfers between devices with their start and end apart: 3 -> 3, of which waited for: 3 -> 3; matrix products, arithmetic and copies ran while one was open for 11% -> 9% of each run, Pallas kernels for 11% -> 10%
where the time goes in v15:
time: 101 us; the launch traced here: 100 us
  Pallas kernels  36.2 us (36%)
  waiting for transfers between devices  22.3 us (22%)
  starting transfers between devices  17 us (17%)
  local copies, waits for them, and re-layouts  15.4 us (15%)
  other arithmetic  7.09 us (7%)
  between operations  2.16 us (2%)
    pallas_call x1, Pallas kernels, batch_terms(): pl.pallas_call(batch_kernel, grid_spec=grid_spec, out_shape=[jax.ShapeDty...  15.8 us
    all_to_all x1, waiting for transfers between devices, body(): matrix = jnp.sum(lax.all_to_all(terms, 'tiles', 0, 0, tiled=False), axis=0)  12 us
    pallas_call x1, Pallas kernels, prep_tables(): pl.pallas_call(prep_kernel, grid_spec=grid_spec, out_shape=[jax.ShapeDtyp...  10.5 us
    all_to_all x1, waiting for transfers between devices, body(): owned = jnp.sum(lax.all_to_all(partial, 'tiles', 0, 0, tiled=False), axis=0)  10.2 us
    pallas_call x1, Pallas kernels, tile_products(): pl.pallas_call(tile_kernel, grid_spec=grid_spec, out_shape=jax.ShapeDtype...  9.93 us
    all_to_all x1, starting transfers between devices, body(): owned = jnp.sum(lax.all_to_all(partial, 'tiles', 0, 0, tiled=False), axis=0)  7.39 us
    all_to_all x1, starting transfers between devices, body(): matrix = jnp.sum(lax.all_to_all(terms, 'tiles', 0, 0, tiled=False), axis=0)  5.54 us
    unnamed x23, local copies, waits for them, and re-layouts  4.18 us
  transfers between devices with their start and end apart: 3, of which 3 were waited for; matrix products, arithmetic and copies ran while one was open for 9% of the time, Pallas kernels for 10%

profile of v15, /device:TPU:0, one launch (start us, length us, event | category | flops | bytes accessed | tf_op | source)
XLA Modules:
  0.0 100.2 jit_solution(7581754222760580491)
XLA Ops:
  0.6 0.8 copy.17
  1.4 0.7 compare_select_fusion.7
  2.1 0.7 scatter_custom_fusion
  4.1 1.6 %sort.33 = (s32[32]{0:T(128)}, s32[32]{0:T(128)S(1)}) sort(s32[32]{0:T(128)S(1)} %multiply_add_fusion, s32[32]{0:T(128)S(1)} %iota.32), dimensions={0}, to_apply=%region_10.11 | sort | flops 160 | bytes 512 | tf_op jit(solution)/shard_map/jit(argsort)/sort | solution.py:266
  6.6 0.6 reshape.91.pairs_ref
  7.2 0.7 scatter_custom_fusion.2
  8.5 9.9 %shard_map.104 = f32[32,64,64]{2,1,0:T(8,128)} custom-call(s32[64]{0:T(128)} %reshape.91.pairs_ref, f32[256,16384]{1,0:T(8,128)} %refs_31_.1, f32[256,16384]{1,0:T(8,128)} %refs_31_.1, f32[256,16384]{1,0:T(8,128)} %refs_31_.1, f32[256,16384]{1,0:T(8,128)} %refs_31_.1, f32[256,16384]{1,0:T(8,128)} %refs_31_.1, f32[256,16384]{1,0:T(8,128)} %refs_31_.1, ...), custom_call_target="tpu_custom_call" | custom-call | tf_op jit(solution)/shard_map/pallas_call | solution.py:55
  18.5 2.0 %gather_fusion.3 = f32[32,64,64]{2,1,0:T(8,128)S(1)} fusion(f32[32,64,64]{2,1,0:T(8,128)} %shard_map.104, s32[1024]{0:T(1024)} %pad_clamp_fusion), kind=kCustom, calls=%fused_computation.3 | custom fusion | bytes 1048704 | tf_op jit(solution)/shard_map/gather | solution.py:270
  20.5 1.0 reshape.93
  21.4 7.4 %all-to-all-start = ((f32[16,2,32,128]{3,2,1,0:T(8,128)}), f32[16,2,32,128]{3,2,1,0:T(8,128)S(1)}, u32[]{:S(2)}, u32[]{:S(2)}) async-start(f32[16,2,32,128]{3,2,1,0:T(8,128)} %reshape.93), calls=%async_computation | async-start | bytes 1048576 | tf_op jit(solution)/shard_map/all_to_all | solution.py:271
  29.0 0.6 copy.21
  30.2 1.0 scatter_custom_fusion.1
  31.8 1.0 %sort.32 = (s32[8]{0:T(128)S(1)}, s32[8]{0:T(128)}) sort(s32[8]{0:T(128)S(1)} %slice_bitcast_fusion, s32[8]{0:T(128)S(1)} %iota.31), dimensions={0}, to_apply=%region_2.3 | sort | flops 24 | bytes 128 | tf_op jit(solution)/shard_map/jit(sort)/sort | solution.py:281
  33.1 10.2 %all-to-all-done = f32[16,2,32,128]{3,2,1,0:T(8,128)S(1)} async-done(((f32[16,2,32,128]{3,2,1,0:T(8,128)}), f32[16,2,32,128]{3,2,1,0:T(8,128)S(1)}, u32[]{:S(2)}, u32[]{:S(2)}) %all-to-all-start) | async-done | bytes 524320 | tf_op jit(solution)/shard_map/all_to_all | solution.py:271
  43.3 0.9 broadcast_in_dim.98
  44.3 4.1 %all-to-all-start.1 = ((f32[16,2,32,128]{3,2,1,0:T(8,128)}), f32[16,2,32,128]{3,2,1,0:T(8,128)S(1)}, u32[]{:S(2)}, u32[]{:S(2)}) async-start(f32[16,2,32,128]{3,2,1,0:T(8,128)} %broadcast_in_dim.98), calls=%async_computation.1 | async-start | bytes 1048576 | tf_op jit(solution)/shard_map/all_to_all | solution.py:273
  51.7 0.6 min.12.source_ref
  52.3 10.5 %shard_map.105 = (bf16[512,2048]{1,0:T(8,128)(2,1)}, bf16[512,2048]{1,0:T(8,128)(2,1)}, f32[512,2048]{1,0:T(8,128)}) custom-call(s32[64]{0:T(128)} %min.12.source_ref, f32[8,512,256]{2,1,0:T(8,128)} %table_hbm.1), custom_call_target="tpu_custom_call" | custom-call | tf_op jit(solution)/shard_map/pallas_call | solution.py:135
  62.8 0.8 copy-done
  63.7 15.8 %shard_map.106 = (f32[1,2048]{1,0:T(1,128)}, f32[32,32,128]{2,1,0:T(8,128)}) custom-call(s32[64]{0:T(128)} %broadcast_select_fusion.1.pick_ref, s32[32]{0:T(128)} %get-tuple-element.23.code_ref, bf16[512,2048]{1,0:T(8,128)(2,1)} %get-tuple-element.12.hi_ref, bf16[512,2048]{1,0:T(8,128)(2,1)} %get-tuple-element.13.lo_ref, ...), custom_call_target="tpu_custom_call" | custom-call | tf_op jit(solution)/shard_map/pallas_call | solution.py:230
  79.5 5.5 %all-to-all-start.2 = ((f32[16,2,32,128]{3,2,1,0:T(8,128)}), f32[16,2,32,128]{3,2,1,0:T(8,128)S(1)}, u32[]{:S(2)}, u32[]{:S(2)}) async-start(f32[16,2,32,128]{3,2,1,0:T(8,128)} %bitcast.20), calls=%async_computation.2 | async-start | bytes 1048576 | tf_op jit(solution)/shard_map/all_to_all | solution.py:302
  85.6 1.4 %reduce.7 = f32[2048]{0:T(1024)S(1)} reduce(f32[1,2048]{1,0:T(1,128)} %get-tuple-element.15, f32[]{:T(128)} %broadcast.92), dimensions={0}, to_apply=%get-tuple-element.15.reduce_sub_computation.3 | reduce | bytes 16388 | tf_op jit(solution)/shard_map/pallas_call | solution.py:230
  87.5 12.0 %all-to-all-done.2 = f32[16,2,32,128]{3,2,1,0:T(8,128)S(1)} async-done(((f32[16,2,32,128]{3,2,1,0:T(8,128)}), f32[16,2,32,128]{3,2,1,0:T(8,128)S(1)}, u32[]{:S(2)}, u32[]{:S(2)}) %all-to-all-start.2) | async-done | bytes 524320 | tf_op jit(solution)/shard_map/all_to_all | solution.py:302
  99.5 0.6 copy.24
  (56 shorter events, 7.6 us)
Async XLA Ops:
  3.5 0.5 copy-start.3
  3.5 0.6 copy-start.5
  18.4 10.4 %copy-start.7 = (s32[128,8]{0,1:T(8,128)S(1)}, s32[128,8]{0,1:T(8,128)}, u32[]{:S(2)}) copy-start(s32[128,8]{0,1:T(8,128)} %param.13) | copy-start | bytes 12292
  18.4 10.5 %copy-start.1 = (f32[8,256]{1,0:T(8,128)S(1)}, f32[8,256]{1,0:T(8,128)}, u32[]{:S(2)}) copy-start(f32[8,256]{1,0:T(8,128)} %param.17) | copy-start | bytes 24580
  18.4 11.1 %copy-start.2 = (f32[8,256]{1,0:T(8,128)S(1)}, f32[8,256]{1,0:T(8,128)}, u32[]{:S(2)}) copy-start(f32[8,256]{1,0:T(8,128)} %param.16) | copy-start | bytes 24580
  18.4 11.7 %copy-start.8 = (s32[128]{0:T(128)S(1)}, s32[128]{0:T(128)}, u32[]{:S(2)}) copy-start(s32[128]{0:T(128)} %param.14) | copy-start | bytes 1540
  18.5 14.4 %copy-start.4 = (s32[32]{0:T(128)S(1)}, s32[32]{0:T(128)}, u32[]{:S(2)}) copy-start(s32[32]{0:T(128)} %copy-done.3) | copy-start | bytes 388
  18.5 14.4 %copy-start.6 = (s32[32]{0:T(128)S(1)}, s32[32]{0:T(128)}, u32[]{:S(2)}) copy-start(s32[32]{0:T(128)} %copy-done.5) | copy-start | bytes 388
  21.4 21.9 %all-to-all-start = ((f32[16,2,32,128]{3,2,1,0:T(8,128)}), f32[16,2,32,128]{3,2,1,0:T(8,128)S(1)}, u32[]{:S(2)}, u32[]{:S(2)}) async-start(f32[16,2,32,128]{3,2,1,0:T(8,128)} %reshape.93), calls=%async_computation | async-start | bytes 1048576 | tf_op jit(solution)/shard_map/all_to_all | solution.py:271
  44.3 18.6 %all-to-all-start.1 = ((f32[16,2,32,128]{3,2,1,0:T(8,128)}), f32[16,2,32,128]{3,2,1,0:T(8,128)S(1)}, u32[]{:S(2)}, u32[]{:S(2)}) async-start(f32[16,2,32,128]{3,2,1,0:T(8,128)} %broadcast_in_dim.98), calls=%async_computation.1 | async-start | bytes 1048576 | tf_op jit(solution)/shard_map/all_to_all | solution.py:273
  62.8 0.8 copy-start
  79.5 20.0 %all-to-all-start.2 = ((f32[16,2,32,128]{3,2,1,0:T(8,128)}), f32[16,2,32,128]{3,2,1,0:T(8,128)S(1)}, u32[]{:S(2)}, u32[]{:S(2)}) async-start(f32[16,2,32,128]{3,2,1,0:T(8,128)} %bitcast.20), calls=%async_computation.2 | async-start | bytes 1048576 | tf_op jit(solution)/shard_map/all_to_all | solution.py:302

commit v16 on v14

--- a/solution.py
+++ b/solution.py
@@ -25,13 +25,7 @@
         right = refs[group + i][...] * occ
         left = jnp.where(row_block % 2 == 0, left[:, :BS], left[:, BS:])
         right = jnp.where(col_block % 2 == 0, right[:, :BS], right[:, BS:])
-        out_ref[i] = lax.dot_general(
-            left,
-            right,
-            (((0,), (0,)), ((), ())),
-            precision=lax.Precision.HIGHEST,
-            preferred_element_type=jnp.float32,
-        )
+        out_ref[i] = split_dot(left, right, ((0,), (0,)))
 
 
 def tile_products(coeffs, occupation, pairs):

time: 96.2 us -> 97 us (level)
  no operation moved by 1% of the time
where the time goes in v16:
time: 97 us; the launch traced here: 96.2 us
  Pallas kernels  36.7 us (38%)
  waiting for transfers between devices  21.4 us (22%)
  starting transfers between devices  17.8 us (18%)
  local copies, waits for them, and re-layouts  13.3 us (14%)
  other arithmetic  4.87 us (5%)
  between operations  2.09 us (2%)
    pallas_call x1, Pallas kernels, batch_terms(): pl.pallas_call(batch_kernel, grid_spec=grid_spec, out_shape=[jax.ShapeDty...  15.4 us
    all_to_all x1, waiting for transfers between devices, body(): matrix = jnp.sum(lax.all_to_all(terms, 'tiles', 0, 0, tiled=False), axis=0)  12 us
    pallas_call x1, Pallas kernels, tile_products(): pl.pallas_call(tile_kernel, grid_spec=grid_spec, out_shape=jax.ShapeDtype...  10.9 us
    pallas_call x1, Pallas kernels, prep_tables(): pl.pallas_call(prep_kernel, grid_spec=grid_spec, out_shape=[jax.ShapeDtyp...  10.5 us
    all_to_all x1, waiting for transfers between devices, body(): owned = jnp.sum(lax.all_to_all(partial, 'tiles', 0, 0, tiled=False), axis=0)  9.27 us
    all_to_all x1, starting transfers between devices, body(): owned = jnp.sum(lax.all_to_all(partial, 'tiles', 0, 0, tiled=False), axis=0)  7.37 us
    all_to_all x1, starting transfers between devices, body(): matrix = jnp.sum(lax.all_to_all(terms, 'tiles', 0, 0, tiled=False), axis=0)  6.32 us
    all_to_all x1, starting transfers between devices, body(): lax.all_to_all(spread, 'tiles', 0, 0, tiled=False)  4.11 us
  transfers between devices with their start and end apart: 3, of which 3 were waited for; matrix products, arithmetic and copies ran while one was open for 11% of the time, Pallas kernels for 11%

profile of v16, /device:TPU:0, one launch (start us, length us, event | category | flops | bytes accessed | tf_op | source)
XLA Modules:
  0.0 96.2 jit_solution(7728575172264522148)
XLA Ops:
  0.6 0.8 copy.15
  1.4 0.7 compare_select_fusion.5
  2.1 0.7 scatter_custom_fusion
  3.3 0.6 reshape.55.pairs_ref
  4.0 10.9 %shard_map.104 = f32[32,64,64]{2,1,0:T(8,128)} custom-call(s32[64]{0:T(128)} %reshape.55.pairs_ref, f32[256,16384]{1,0:T(8,128)} %refs_31_.1, f32[256,16384]{1,0:T(8,128)} %refs_31_.1, f32[256,16384]{1,0:T(8,128)} %refs_31_.1, f32[256,16384]{1,0:T(8,128)} %refs_31_.1, f32[256,16384]{1,0:T(8,128)} %refs_31_.1, f32[256,16384]{1,0:T(8,128)} %refs_31_.1, ...), custom_call_target="tpu_custom_call" | custom-call | tf_op jit(solution)/shard_map/pallas_call | solution.py:49
  14.9 2.2 %reshape.57 = f32[16,2,32,128]{3,2,1,0:T(8,128)} reshape(f32[32,64,64]{2,1,0:T(8,128)} %shard_map.104) | data formatting | bytes 1048576 | tf_op jit(solution)/shard_map/reshape | solution.py:259
  17.2 7.4 %all-to-all-start = ((f32[16,2,32,128]{3,2,1,0:T(8,128)}), f32[16,2,32,128]{3,2,1,0:T(8,128)S(1)}, u32[]{:S(2)}, u32[]{:S(2)}) async-start(f32[16,2,32,128]{3,2,1,0:T(8,128)} %reshape.57), calls=%async_computation | async-start | bytes 1048576 | tf_op jit(solution)/shard_map/all_to_all | solution.py:260
  24.7 0.6 copy.18
  25.3 0.6 copy.17
  25.9 1.0 %scatter_custom_fusion.1 = s32[128]{0:T(128)S(1)} fusion(s32[128]{0:T(128)S(1)} %compare_select_fusion.3, s32[128]{0:T(128)S(1)} %iota.24, s32[]{:T(128)} %constant.10.clone.1), kind=kCustom, calls=%fused_computation.29 | custom fusion | bytes 516 | tf_op jit(solution)/shard_map/scatter | solution.py:267
  27.5 1.0 %sort.15 = (s32[8]{0:T(128)S(1)}, s32[8]{0:T(128)}) sort(s32[8]{0:T(128)S(1)} %slice_bitcast_fusion, s32[8]{0:T(128)S(1)} %iota.25), dimensions={0}, to_apply=%region_2.0 | sort | flops 24 | bytes 128 | tf_op jit(solution)/shard_map/jit(sort)/sort | solution.py:270
  28.6 1.0 %slice_reduce_fusion.1 = (s32[32]{0:T(128)S(1)}, s32[32]{0:T(128)S(1)}) fusion(s32[32,2]{1,0:T(8,128)} %copy-done.1), kind=kLoop, calls=%fused_computation.7 | loop fusion | bytes 512 | tf_op jit(solution)/shard_map/slice | solution.py:274
  29.7 9.3 %all-to-all-done = f32[16,2,32,128]{3,2,1,0:T(8,128)S(1)} async-done(((f32[16,2,32,128]{3,2,1,0:T(8,128)}), f32[16,2,32,128]{3,2,1,0:T(8,128)S(1)}, u32[]{:S(2)}, u32[]{:S(2)}) %all-to-all-start) | async-done | bytes 524320 | tf_op jit(solution)/shard_map/all_to_all | solution.py:260
  39.0 0.9 broadcast_in_dim.92
  39.9 4.1 %all-to-all-start.1 = ((f32[16,2,32,128]{3,2,1,0:T(8,128)}), f32[16,2,32,128]{3,2,1,0:T(8,128)S(1)}, u32[]{:S(2)}, u32[]{:S(2)}) async-start(f32[16,2,32,128]{3,2,1,0:T(8,128)} %broadcast_in_dim.92), calls=%async_computation.1 | async-start | bytes 1048576 | tf_op jit(solution)/shard_map/all_to_all | solution.py:262
  47.3 0.6 min.12.source_ref
  47.9 10.5 %shard_map.105 = (bf16[512,2048]{1,0:T(8,128)(2,1)}, bf16[512,2048]{1,0:T(8,128)(2,1)}, f32[512,2048]{1,0:T(8,128)}) custom-call(s32[64]{0:T(128)} %min.12.source_ref, f32[8,512,256]{2,1,0:T(8,128)} %table_hbm.1), custom_call_target="tpu_custom_call" | custom-call | tf_op jit(solution)/shard_map/pallas_call | solution.py:129
  58.5 0.8 copy-done
  59.4 15.4 %shard_map.106 = (f32[1,2048]{1,0:T(1,128)}, f32[32,32,128]{2,1,0:T(8,128)}) custom-call(s32[64]{0:T(128)} %broadcast_select_fusion.1.pick_ref, s32[32]{0:T(128)} %get-tuple-element.21.code_ref, bf16[512,2048]{1,0:T(8,128)(2,1)} %get-tuple-element.10.hi_ref, bf16[512,2048]{1,0:T(8,128)(2,1)} %get-tuple-element.11.lo_ref, ...), custom_call_target="tpu_custom_call" | custom-call | tf_op jit(solution)/shard_map/pallas_call | solution.py:224
  74.7 6.3 %all-to-all-start.2 = ((f32[16,2,32,128]{3,2,1,0:T(8,128)}), f32[16,2,32,128]{3,2,1,0:T(8,128)S(1)}, u32[]{:S(2)}, u32[]{:S(2)}) async-start(f32[16,2,32,128]{3,2,1,0:T(8,128)} %bitcast.17), calls=%async_computation.2 | async-start | bytes 1048576 | tf_op jit(solution)/shard_map/all_to_all | solution.py:291
  81.6 1.4 %reduce.7 = f32[2048]{0:T(1024)S(1)} reduce(f32[1,2048]{1,0:T(1,128)} %get-tuple-element.13, f32[]{:T(128)} %broadcast.58), dimensions={0}, to_apply=%get-tuple-element.13.reduce_sub_computation.3 | reduce | bytes 16388 | tf_op jit(solution)/shard_map/pallas_call | solution.py:224
  82.9 0.6 reshape.61
  83.5 12.0 %all-to-all-done.2 = f32[16,2,32,128]{3,2,1,0:T(8,128)S(1)} async-done(((f32[16,2,32,128]{3,2,1,0:T(8,128)}), f32[16,2,32,128]{3,2,1,0:T(8,128)S(1)}, u32[]{:S(2)}, u32[]{:S(2)}) %all-to-all-start.2) | async-done | bytes 524320 | tf_op jit(solution)/shard_map/all_to_all | solution.py:291
  95.6 0.6 copy.21
  (36 shorter events, 4.2 us)
Async XLA Ops:
  3.3 11.6 %copy-start.1 = (s32[32,2]{1,0:T(8,128)}, s32[32,2]{1,0:T(8,128)S(1)}, u32[]{:S(2)}) copy-start(s32[32,2]{1,0:T(8,128)S(1)} %gather_fusion) | copy-start | bytes 772
  4.0 20.6 %copy-start.4 = (s32[128,8]{0,1:T(8,128)S(1)}, s32[128,8]{0,1:T(8,128)}, u32[]{:S(2)}) copy-start(s32[128,8]{0,1:T(8,128)} %param.13) | copy-start | bytes 12292
  4.0 20.7 %copy-start.2 = (f32[8,256]{1,0:T(8,128)S(1)}, f32[8,256]{1,0:T(8,128)}, u32[]{:S(2)}) copy-start(f32[8,256]{1,0:T(8,128)} %param.17) | copy-start | bytes 24580
  4.0 21.3 %copy-start.3 = (f32[8,256]{1,0:T(8,128)S(1)}, f32[8,256]{1,0:T(8,128)}, u32[]{:S(2)}) copy-start(f32[8,256]{1,0:T(8,128)} %param.16) | copy-start | bytes 24580
  4.0 21.9 %copy-start.5 = (s32[128]{0:T(128)S(1)}, s32[128]{0:T(128)}, u32[]{:S(2)}) copy-start(s32[128]{0:T(128)} %param.14) | copy-start | bytes 1540
  17.2 21.8 %all-to-all-start = ((f32[16,2,32,128]{3,2,1,0:T(8,128)}), f32[16,2,32,128]{3,2,1,0:T(8,128)S(1)}, u32[]{:S(2)}, u32[]{:S(2)}) async-start(f32[16,2,32,128]{3,2,1,0:T(8,128)} %reshape.57), calls=%async_computation | async-start | bytes 1048576 | tf_op jit(solution)/shard_map/all_to_all | solution.py:260
  39.9 18.6 %all-to-all-start.1 = ((f32[16,2,32,128]{3,2,1,0:T(8,128)}), f32[16,2,32,128]{3,2,1,0:T(8,128)S(1)}, u32[]{:S(2)}, u32[]{:S(2)}) async-start(f32[16,2,32,128]{3,2,1,0:T(8,128)} %broadcast_in_dim.92), calls=%async_computation.1 | async-start | bytes 1048576 | tf_op jit(solution)/shard_map/all_to_all | solution.py:262
  58.5 0.8 copy-start
  74.7 20.8 %all-to-all-start.2 = ((f32[16,2,32,128]{3,2,1,0:T(8,128)}), f32[16,2,32,128]{3,2,1,0:T(8,128)S(1)}, u32[]{:S(2)}, u32[]{:S(2)}) async-start(f32[16,2,32,128]{3,2,1,0:T(8,128)} %bitcast.17), calls=%async_computation.2 | async-start | bytes 1048576 | tf_op jit(solution)/shard_map/all_to_all | solution.py:291
